TPU v7x, 256 devices: a whole 4x4x8 slice. The times are simulated.
256 devices in a mesh: dp: 16 (over z_lo, y, core), ctx: 16 (over x, z_hi).
Axes of the slice: x: 4, y: 4, z: 8 (z_hi: 4, z_lo: 2; z = z_hi * 2 + z_lo), core: 2. Of those that a mesh axis runs over, the one named last changes fastest.
Arguments:
- tokens: bfloat16 [16, 2048, 2560], P('dp', 'ctx'), may hold values from -6 to 6
- shard_counts: int32 [16, 16], P('dp'), may hold values from 64 to 128, as said below
- stretch_start: int32 [16], P('dp'), may hold values from 102 to 409, as said below
- segment_ids: int32 [16, 2048], P('dp', 'ctx'), may hold values from 0 to 1, as said below
- span_ids: int32 [16, 2048], P('dp', 'ctx'), may hold values from -1 to 31, as said below
- query_weight: bfloat16 [2560, 2560], P('dp'), may hold values from -0.125 to 0.125
- key_matrix: bfloat16 [2560, 512], P('dp'), may hold values from -0.125 to 0.125
- value_matrix: bfloat16 [2560, 512], P('dp'), may hold values from -0.125 to 0.125
- score_vector: bfloat16 [2560], replicated, may hold values from -4 to 4
Outputs:
- attention: bfloat16 [16, 2048, 2560], P('dp', 'ctx')
- candidate_loglik: float32 [16, 32], P('dp')
Inputs may be any that keep to these rules, and one draw needn't show every extreme that they name: `shard_counts`: in every sequence at least one shard has exactly 128 live tokens. `stretch_start`: A stretch of each sequence starts at a position held by one of its live tokens, after the first. `segment_ids`: along the live tokens of a sequence, segment ids never fall. `span_ids`: each candidate of every sequence covers one or more live tokens, in one run of consecutive positions; empty slots have -1.
All inputs are finite; a program needn't handle non-finite values.
Results may differ from a plain program's by a relative error of at most 0.0066.
Values may be sent and summed in bfloat16 or wider, within the bound.
No kernel may reach another device: no remote copies, remote signals or barrier semaphores. Data moves between devices by JAX's collectives and lax.ppermute only.
A program may use at most 128 MiB of HBM per device.

v0:
```python
import math

import jax
import jax.numpy as jnp
from jax import lax
from jax.sharding import PartitionSpec as P

QUERY_HEADS = 20
KEY_VALUE_HEADS = 4
HEAD_SIZE = 128
STRETCH = 8192
CAND = 32


THETA = 500000.0
EPS = 1e-05


def rotary_then_norm(value_rows, token_places, heads):
    token_count = value_rows.shape[0]
    half = HEAD_SIZE // 2
    shaped = value_rows.reshape(token_count, heads, HEAD_SIZE)
    freqs = jnp.exp(jnp.arange(half, dtype=jnp.float32) * (-2.0 * math.log(THETA) / HEAD_SIZE))
    angles = token_places.astype(jnp.float32)[:, None] * freqs[None, :]
    cosine = jnp.cos(angles)[:, None, :]
    sine = jnp.sin(angles)[:, None, :]
    leading_block = shaped[..., :half]
    second = shaped[..., half:]
    turned = jnp.concatenate(
        [leading_block * cosine - second * sine, second * cosine + leading_block * sine], axis=-1
    )
    scale = lax.rsqrt(jnp.mean(turned * turned, axis=-1, keepdims=True) + EPS)
    return (turned * scale).astype(jnp.bfloat16).reshape(token_count, heads * HEAD_SIZE)


def per_device(
    tokens,
    shard_counts,
    stretch_start,
    segment_ids,
    span_ids,
    query_weight,
    key_matrix,
    value_matrix,
    score_vector,
):
    inputs = tokens[0]
    token_slots = inputs.shape[0]
    shards = lax.axis_size("ctx")
    mine = lax.axis_index("ctx")
    counts = shard_counts[0]
    order = jnp.arange(shards, dtype=jnp.int32)
    count_mine = jnp.sum(jnp.where(order == mine, counts, 0))
    start_mine = jnp.sum(jnp.where(order < mine, counts, 0))
    offsets = jnp.arange(token_slots, dtype=jnp.int32)
    token_places = start_mine + offsets
    live = offsets < count_mine
    cstart = stretch_start[0]
    qseg = segment_ids[0]
    qchunk = (token_places + STRETCH - cstart) // STRETCH
    pieces = (
        lax.all_gather(query_weight, "dp", axis=0, tiled=True),
        lax.all_gather(key_matrix, "dp", axis=0, tiled=True),
        lax.all_gather(value_matrix, "dp", axis=0, tiled=True),
    )
    query, key_rows, raw_values = tuple(
        (jnp.dot(inputs, piece, preferred_element_type=jnp.float32) for piece in pieces)
    )
    value_rows = raw_values.astype(jnp.bfloat16)
    query_norm = rotary_then_norm(query, token_places, QUERY_HEADS)
    key_norm = rotary_then_norm(key_rows, token_places, KEY_VALUE_HEADS)
    kplace = jnp.where(live, token_places + 1, 0)
    head_group = QUERY_HEADS // KEY_VALUE_HEADS
    per_head_queries = query_norm.reshape(token_slots, KEY_VALUE_HEADS, head_group, HEAD_SIZE)

    def add_keys(piece):
        key_portion, value_portion, kpos, kseg = piece
        token_count = key_portion.shape[0]
        kchunk = (kpos - 1 + STRETCH - cstart) // STRETCH
        scores = jnp.einsum(
            "qhgd,khd->hgqk",
            per_head_queries,
            key_portion.reshape(token_count, KEY_VALUE_HEADS, HEAD_SIZE),
            preferred_element_type=jnp.float32,
        ) * (1.0 / math.sqrt(HEAD_SIZE))
        allowed = (kseg[None, :] == qseg[:, None]) & (kchunk[None, :] == qchunk[:, None])
        allowed = allowed & (kpos[None, :] >= 1) & (kpos[None, :] <= token_places[:, None] + 1)
        weights = jnp.where(allowed[None, None], jnp.exp(scores), 0.0)
        denom = jnp.sum(weights, axis=-1)
        numer = jnp.einsum(
            "hgqk,khd->qhgd",
            weights.astype(jnp.bfloat16),
            value_portion.reshape(token_count, KEY_VALUE_HEADS, HEAD_SIZE),
            preferred_element_type=jnp.float32,
        )
        return (numer, denom)

    empty = (
        jnp.zeros((token_slots, KEY_VALUE_HEADS, head_group, HEAD_SIZE), jnp.float32),
        jnp.zeros((KEY_VALUE_HEADS, head_group, token_slots), jnp.float32),
    )
    own_block = (key_norm, value_rows, kplace, qseg)
    piece = (
        lax.all_gather(own_block[0], "ctx", axis=0, tiled=True),
        lax.all_gather(own_block[1], "ctx", axis=0, tiled=True),
        lax.all_gather(own_block[2], "ctx", axis=0, tiled=True),
        lax.all_gather(own_block[3], "ctx", axis=0, tiled=True),
    )
    owner = jnp.int32(0) // token_slots
    numer, denom = lax.cond(
        owner <= mine, lambda state: add_keys(piece), lambda state: state, empty
    )
    denom_rows = jnp.transpose(denom, (2, 0, 1))
    safe = jnp.where(live[:, None, None], denom_rows, 1.0)
    result = numer / safe[..., None] * live[:, None, None, None].astype(jnp.float32)
    attention = result.reshape(token_slots, QUERY_HEADS * HEAD_SIZE).astype(jnp.bfloat16)
    verdict = jnp.dot(attention, score_vector, preferred_element_type=jnp.float32)
    loglik = jax.nn.log_sigmoid(verdict)
    onehot = span_ids[0][:, None] == jnp.arange(CAND, dtype=jnp.int32)[None, :]
    sums = jnp.sum(jnp.where(onehot, loglik[:, None], 0.0), axis=0)
    tally = jnp.sum(onehot.astype(jnp.float32), axis=0)
    sums, tally = lax.psum((sums, tally), "ctx")
    return (attention[None], (sums / tally)[None])


def solution(mesh):
    placed = (
        P("dp", "ctx", None),
        P("dp", None),
        P("dp"),
        P("dp", "ctx"),
        P("dp", "ctx"),
        P("dp", None),
        P("dp", None),
        P("dp", None),
        P(),
    )
    return jax.shard_map(
        per_device,
        mesh=mesh,
        in_specs=placed,
        out_specs=(P("dp", "ctx", None), P("dp", None)),
        check_vma=False,
    )
```

profile of v0, /device:TPU:2, one launch (start us, length us, event | category | flops | bytes accessed | tf_op | source)
XLA Modules:
  0.0 370.3 jit_solution(2490414776641406215)
XLA Ops:
  7.2 0.7 all-gather.8.cloned.1.call-update
  8.0 0.7 all-gather.14.cloned.1.call-update
  8.7 0.7 all-gather.12.cloned.1.call-update
  9.5 1.3 fusion.27
  11.5 38.4 %all-gather.8.cloned.1.call-done = bf16[2560,512]{1,0:T(8,128)(2,1)} async-done(((bf16[160,512]{1,0:T(8,128)(2,1)}), bf16[2560,512]{1,0:T(8,128)(2,1)}) %all-gather.8.cloned.1.call-update) | async-done | bytes 2621456 | tf_op jit(solution)/shard_map/all_gather | solution.py:63
  50.0 3.0 copy.43
  53.0 0.8 fusion.24
  54.0 0.8 copy.44
  54.8 34.2 %all-gather.14.cloned.1.call-done = bf16[2560,512]{1,0:T(8,128)(2,1)} async-done(((bf16[160,512]{1,0:T(8,128)(2,1)}), bf16[2560,512]{1,0:T(8,128)(2,1)}) %all-gather.14.cloned.1.call-update) | async-done | bytes 2621456 | tf_op jit(solution)/shard_map/all_gather | solution.py:64
  89.0 2.9 convolution_convert_fusion
  92.6 39.1 %all-gather = s32[1,2048]{1,0:T(1,128)S(1)} all-gather(s32[1,128]{1,0:T(1,128)S(1)} %copy-done.5), channel_id=2, replica_groups=mesh['dp'=16,'ctx'=16] {'ctx'}, dimensions={1}, use_global_device_ids=true | all-gather | bytes 8704 | tf_op jit(solution)/shard_map/all_gather | solution.py:107
  131.7 1.2 select_bitcast_fusion.1
  132.8 38.4 %all-gather.1 = s32[16,1,128]{2,1,0:T(1,128)S(1)} all-gather(s32[1,1,128]{2,1,0:T(1,128)S(1)} %select_bitcast_fusion.1), channel_id=1, replica_groups=mesh['dp'=16,'ctx'=16] {'ctx'}, dimensions={0}, use_global_device_ids=true | all-gather | bytes 8704 | tf_op jit(solution)/shard_map/all_gather | solution.py:106
  171.8 1.2 fusion.31
  173.0 1.2 iota_compare_fusion.1
  174.1 17.7 %copy.45 = bf16[2560,2560]{1,0:T(8,128)(2,1)} copy(bf16[2560,2560]{0,1:T(8,128)(2,1)} %bitcast.64) | data formatting | bytes 26214400 | tf_op jit(solution)/shard_map/dot_general | solution.py:67
  191.8 6.7 %fusion.22 = f32[128,20,128]{0,2,1:T(8,128)S(1)} fusion(bf16[20,128,2560]{2,1,0:T(8,128)(2,1)} %bitcast.63, bf16[1,128,2560]{2,1,0:T(8,128)(2,1)S(1)} %copy-done), kind=kOutput, calls=%fused_computation.37 | convolution fusion | flops 1677721600 | bytes 15073280 | tf_op jit(solution)/shard_map/dot_general | solution.py:67
  199.1 1.5 copy.46
  200.7 2.1 fusion.19
  202.8 27.4 %all-gather.10.cloned.1.call-done = bf16[2048,512]{1,0:T(8,128)(2,1)} async-done(((bf16[128,512]{1,0:T(8,128)(2,1)}), bf16[2048,512]{1,0:T(8,128)(2,1)}) %all-gather.10.cloned.1.call-update) | async-done | bytes 2097168 | tf_op jit(solution)/shard_map/all_gather | solution.py:104
  230.2 59.5 %all-gather.16.cloned.1.call-done = bf16[2048,512]{1,0:T(8,128)(2,1)} async-done(((bf16[128,512]{1,0:T(8,128)(2,1)}), bf16[2048,512]{1,0:T(8,128)(2,1)}) %all-gather.16.cloned.1.call-update) | async-done | bytes 2097168 | tf_op jit(solution)/shard_map/all_gather | solution.py:105
  289.7 32.8 %conditional.1 = (f32[4,5,128]{2,1,0:T(8,128)}, f32[128,4,5,128]{0,3,2,1:T(8,128)S(1)}) conditional(s32[]{:T(128)} %convert_element_type.59, () %tuple.28, (s32[2048]{0:T(1024)S(1)}, s32[1,128]{1,0:T(1,128)S(1)}, s32[2048]{0:T(1024)S(1)}, s32[]{:T(128)}, s32[128]{0:T(128)S(1)}, /*index=5*/s32[128]{0:T(128)S(1)}, s32[]{:T(128)}, s32[]{:T(128)}, ...), branch_computations={%region_4.5_spmd, %region_5.7_spmd.clone.clone} | conditional | flops 2717421312 | bytes 68356152 | solution.py:110
  290.4 0.7 add_select_fusion
  291.1 1.9 compare_and_fusion
  293.0 4.0 %reshape.253 = bf16[2048,4,128]{2,1,0:T(4,128)(2,1)} reshape(bf16[2048,512]{1,0:T(8,128)(2,1)} %get-tuple-element.241) | data formatting | bytes 4194304 | tf_op jit(solution)/shard_map/cond/branch_1_fun/reshape | solution.py:83
  297.0 11.2 %fusion = (f32[4,5,128]{2,1,0:T(8,128)}, f32[4,2048,128,5]{2,1,3,0:T(8,128)}) fusion(pred[128,2048]{0,1:T(8,128)(4,1)S(1)} %compare_and_fusion, bf16[128,4,5,128]{3,0,2,1:T(8,128)(2,1)S(1)} %get-tuple-element.242, bf16[2048,4,128,1]{2,1,0,3:T(4,128)(2,1)} %bitcast.72), kind=kOutput, calls=%fused_computation.1 | convolution fusion | flops 1357903360 | bytes 23996416 | tf_op jit(solution)/shard_map/cond/branch_1_fun/qhgd,khd->hgqk/dot_general | solution.py:80
  308.2 2.1 reshape.254
  310.3 11.9 %fusion.10 = f32[128,4,5,128]{3,0,2,1:T(8,128)S(1)} fusion(bf16[2048,4,128,1]{2,1,0,3:T(4,128)(2,1)} %bitcast.71, f32[4,2048,128,5]{2,1,3,0:T(8,128)} %get-tuple-element.266, pred[128,2048]{0,1:T(8,128)(4,1)S(1)} %compare_and_fusion), kind=kOutput, calls=%fused_computation.10 | convolution fusion | flops 1357905920 | bytes 24641536 | tf_op jit(solution)/shard_map/cond/branch_1_fun/hgqk,khd->qhgd/dot_general | solution.py:90
  322.6 0.8 select_bitcast_fusion
  323.4 0.9 multiply_convert_fusion
  324.2 1.1 copy.49
  325.7 37.6 %all-reduce = (f32[32]{0:T(128)S(1)}, f32[32]{0:T(128)S(1)}) all-reduce(f32[32]{0:T(128)S(1)} %get-tuple-element.260, f32[32]{0:T(128)S(1)} %get-tuple-element.259), channel_id=1, replica_groups=mesh['dp'=16,'ctx'=16] {'ctx'}, use_global_device_ids=true, to_apply=%region_8.9 | all-reduce | flops 64 | bytes 512 | tf_op jit(solution)/shard_map/psum | solution.py:122
  (43 shorter events, 4.9 us)
Async XLA Ops:
  7.2 45.8 %copy-start = (bf16[1,128,2560]{2,1,0:T(8,128)(2,1)S(1)}, bf16[1,128,2560]{2,1,0:T(8,128)(2,1)}, u32[]{:S(2)}) copy-start(bf16[1,128,2560]{2,1,0:T(8,128)(2,1)} %param.11) | copy-start | bytes 1966084
  7.2 42.8 %all-gather.8.cloned.1.call-start = ((), (), s32[]{:S(2)}) async-start(), calls=%async_computation | async-start | bytes 2785280 | tf_op jit(solution)/shard_map/all_gather | solution.py:63
  7.9 81.1 %all-gather.14.cloned.1.call-start = ((), (), s32[]{:S(2)}) async-start(), calls=%async_computation.3 | async-start | bytes 2785280 | tf_op jit(solution)/shard_map/all_gather | solution.py:64
  8.7 165.5 %all-gather.12.cloned.1.call-start = ((), (), s32[]{:S(2)}) async-start(), calls=%async_computation.2 | async-start | bytes 13926400 | tf_op jit(solution)/shard_map/all_gather | solution.py:62
  9.4 220.8 %all-gather.10.cloned.1.call-start = ((), (), s32[]{:S(2)}) async-start(), calls=%async_computation.1 | async-start | bytes 2228224 | tf_op jit(solution)/shard_map/all_gather | solution.py:104
  53.9 38.0 %copy-start.4 = (bf16[2560]{0:T(1024)(128)(2,1)S(1)}, bf16[2560]{0:T(1024)(128)(2,1)}, u32[]{:S(2)}) copy-start(bf16[2560]{0:T(1024)(128)(2,1)} %param.19) | copy-start | bytes 15364
  53.9 38.6 %copy-start.5 = (s32[1,128]{1,0:T(1,128)S(1)}, s32[1,128]{1,0:T(1,128)}, u32[]{:S(2)}) copy-start(s32[1,128]{1,0:T(1,128)} %param.14) | copy-start | bytes 1540
  54.8 235.0 %all-gather.16.cloned.1.call-start = ((), (), s32[]{:S(2)}) async-start(), calls=%async_computation.4 | async-start | bytes 2228224 | tf_op jit(solution)/shard_map/all_gather | solution.py:105
  297.0 11.2 %copy-start.2 = (bf16[2048,512]{1,0:T(8,128)(2,1)S(1)}, bf16[2048,512]{1,0:T(8,128)(2,1)}, u32[]{:S(2)}) copy-start(bf16[2048,512]{1,0:T(8,128)(2,1)} %get-tuple-element.243) | copy-start | bytes 6291460 | tf_op jit(solution)/shard_map/cond
  322.5 2.8 copy-start.3
  322.6 3.0 copy-start.6
  322.6 41.2 %copy-start.1 = (bf16[1,128,2560]{2,1,0:T(8,128)(2,1)S(1)}, bf16[1,128,2560]{2,1,0:T(8,128)(2,1)}, u32[]{:S(2)}) copy-start(bf16[1,128,2560]{2,1,0:T(8,128)(2,1)} %param.11) | copy-start | bytes 1966084
Sparse Core Ops, SparseCore 0:
  9.8 40.1 all-gather.7
  51.8 37.1 all-gather.13
  90.9 77.0 all-gather.11
  170.8 59.3 all-gather.9
  232.5 57.2 all-gather.15
where the time goes:
time: 376 us; the launch traced here: 370 us
  waiting for transfers between devices  162 us (43%)
  blocking collectives  115 us (31%)
  matrix products  33.7 us (9%)
  local copies, waits for them, and re-layouts  31.5 us (8%)
  other arithmetic  14.1 us (4%)
  between operations  14 us (4%)
    all_gather x1, waiting for transfers between devices, per_device(): lax.all_gather(own_block[1], 'ctx', axis=0, tiled=True)  59.5 us
    all_gather x1, blocking collectives, per_device(): lax.all_gather(own_block[3], 'ctx', axis=0, tiled=True)  39.1 us
    all_gather x1, waiting for transfers between devices, per_device(): lax.all_gather(key_matrix, 'dp', axis=0, tiled=True)  38.4 us
    all_gather x1, blocking collectives, per_device(): lax.all_gather(own_block[2], 'ctx', axis=0, tiled=True)  38.4 us
    psum x1, blocking collectives, per_device(): sums, tally = lax.psum((sums, tally), 'ctx')  37.6 us
    all_gather x1, waiting for transfers between devices, per_device(): lax.all_gather(value_matrix, 'dp', axis=0, tiled=True)  34.2 us
    all_gather x1, waiting for transfers between devices, per_device(): lax.all_gather(own_block[0], 'ctx', axis=0, tiled=True)  27.4 us
    dot_general x2, local copies, waits for them, and re-layouts, per_device(): jnp.dot(inputs, piece, preferred_element_type=jnp.float32)  20.7 us
  transfers between devices with their start and end apart: 5, of which 4 were waited for; matrix products, arithmetic and copies ran while one was open for 12% of the time, Pallas kernels for 0%

commit v1 on v0

v1 whole, which is shorter than its diff:
```python
import math

import jax
import jax.numpy as jnp
from jax import lax
from jax.sharding import PartitionSpec as P

QUERY_HEADS = 20
KEY_VALUE_HEADS = 4
HEAD_SIZE = 128
STRETCH = 8192
CAND = 32


THETA = 500000.0
EPS = 1e-05


def rotary_then_norm(value_rows, token_places, heads):
    token_count = value_rows.shape[0]
    half = HEAD_SIZE // 2
    shaped = value_rows.reshape(token_count, heads, HEAD_SIZE)
    freqs = jnp.exp(jnp.arange(half, dtype=jnp.float32) * (-2.0 * math.log(THETA) / HEAD_SIZE))
    angles = token_places.astype(jnp.float32)[:, None] * freqs[None, :]
    cosine = jnp.cos(angles)[:, None, :]
    sine = jnp.sin(angles)[:, None, :]
    leading_block = shaped[..., :half]
    second = shaped[..., half:]
    turned = jnp.concatenate(
        [leading_block * cosine - second * sine, second * cosine + leading_block * sine], axis=-1
    )
    scale = lax.rsqrt(jnp.mean(turned * turned, axis=-1, keepdims=True) + EPS)
    return (turned * scale).astype(jnp.bfloat16).reshape(token_count, heads * HEAD_SIZE)


def make_per_device(shards):
    def per_device(
        tokens,
        shard_counts,
        stretch_start,
        segment_ids,
        span_ids,
        query_weight,
        key_matrix,
        value_matrix,
        score_vector,
    ):
        inputs = tokens[0]
        token_slots = inputs.shape[0]
        kv_width = KEY_VALUE_HEADS * HEAD_SIZE
        mine = lax.axis_index("ctx")
        counts = shard_counts[0]
        starts = jnp.cumsum(counts) - counts
        offsets = jnp.arange(token_slots, dtype=jnp.int32)
        token_places = starts[mine] + offsets
        live = offsets < counts[mine]
        cstart = stretch_start[0]
        qseg = segment_ids[0]
        qchunk = (token_places + STRETCH - cstart) // STRETCH

        kv_weights = lax.all_gather(
            jnp.concatenate([key_matrix, value_matrix], axis=1), "dp", axis=0, tiled=True
        )
        kv_rows = jnp.dot(inputs, kv_weights, preferred_element_type=jnp.float32)
        key_norm = rotary_then_norm(kv_rows[:, :kv_width], token_places, KEY_VALUE_HEADS)
        value_rows = kv_rows[:, kv_width:].astype(jnp.bfloat16)
        seg_row = jnp.zeros((8, 2 * kv_width), jnp.bfloat16)
        seg_row = seg_row.at[0, :token_slots].set(qseg.astype(jnp.bfloat16))
        own_block = jnp.concatenate(
            [jnp.concatenate([key_norm, value_rows], axis=1), seg_row], axis=0
        )
        blocks = [own_block]
        for shift in range(1, shards):
            pairs = [(s, s + shift) for s in range(shards - shift)]
            blocks.append(lax.ppermute(own_block, "ctx", pairs))

        query_weights = lax.all_gather(query_weight, "dp", axis=0, tiled=True)
        query = jnp.dot(inputs, query_weights, preferred_element_type=jnp.float32)
        query_norm = rotary_then_norm(query, token_places, QUERY_HEADS)
        head_group = QUERY_HEADS // KEY_VALUE_HEADS
        per_head_queries = query_norm.reshape(token_slots, KEY_VALUE_HEADS, head_group, HEAD_SIZE)

        numer = jnp.zeros((token_slots, KEY_VALUE_HEADS, head_group, HEAD_SIZE), jnp.float32)
        denom = jnp.zeros((KEY_VALUE_HEADS, head_group, token_slots), jnp.float32)
        for shift, block in enumerate(blocks):
            source = mine - shift
            present = source >= 0
            source = jnp.maximum(source, 0)
            kpos = starts[source] + offsets
            klive = (offsets < counts[source]) & present
            kchunk = (kpos + STRETCH - cstart) // STRETCH
            kseg = block[token_slots, :token_slots].astype(jnp.int32)
            key_portion = block[:token_slots, :kv_width].reshape(
                token_slots, KEY_VALUE_HEADS, HEAD_SIZE
            )
            value_portion = block[:token_slots, kv_width:].reshape(
                token_slots, KEY_VALUE_HEADS, HEAD_SIZE
            )
            scores = jnp.einsum(
                "qhgd,khd->hgqk",
                per_head_queries,
                key_portion,
                preferred_element_type=jnp.float32,
            ) * (1.0 / math.sqrt(HEAD_SIZE))
            allowed = (kseg[None, :] == qseg[:, None]) & (kchunk[None, :] == qchunk[:, None])
            allowed = allowed & klive[None, :] & (kpos[None, :] <= token_places[:, None])
            weights = jnp.where(allowed[None, None], jnp.exp(scores), 0.0)
            denom = denom + jnp.sum(weights, axis=-1)
            numer = numer + jnp.einsum(
                "hgqk,khd->qhgd",
                weights.astype(jnp.bfloat16),
                value_portion,
                preferred_element_type=jnp.float32,
            )

        denom_rows = jnp.transpose(denom, (2, 0, 1))
        safe = jnp.where(live[:, None, None], denom_rows, 1.0)
        result = numer / safe[..., None] * live[:, None, None, None].astype(jnp.float32)
        attention = result.reshape(token_slots, QUERY_HEADS * HEAD_SIZE).astype(jnp.bfloat16)
        verdict = jnp.dot(attention, score_vector, preferred_element_type=jnp.float32)
        loglik = jax.nn.log_sigmoid(verdict)
        onehot = span_ids[0][:, None] == jnp.arange(CAND, dtype=jnp.int32)[None, :]
        sums = jnp.sum(jnp.where(onehot, loglik[:, None], 0.0), axis=0)
        tally = jnp.sum(onehot.astype(jnp.float32), axis=0)
        partial = jnp.concatenate([sums, tally])
        gathered = [partial]
        for shift in range(1, shards):
            pairs = [(s, (s + shift) % shards) for s in range(shards)]
            gathered.append(lax.ppermute(partial, "ctx", pairs))
        stacked = jnp.stack(gathered)
        order = (mine - jnp.arange(shards, dtype=jnp.int32)) % shards
        total = jnp.sum(jnp.take(stacked, order, axis=0), axis=0)
        return (attention[None], (total[:CAND] / total[CAND:])[None])

    return per_device


def solution(mesh):
    placed = (
        P("dp", "ctx", None),
        P("dp", None),
        P("dp"),
        P("dp", "ctx"),
        P("dp", "ctx"),
        P("dp", None),
        P("dp", None),
        P("dp", None),
        P(),
    )
    return jax.shard_map(
        make_per_device(mesh.shape["ctx"]),
        mesh=mesh,
        in_specs=placed,
        out_specs=(P("dp", "ctx", None), P("dp", None)),
        check_vma=False,
    )
```

time: 376 us -> 441 us (1.17)
  starting transfers between devices: 0.19 us -> 218 us
  blocking collectives: 115 us -> 0 us
  waiting for transfers between devices: 162 us -> 79 us
  other arithmetic: 14.1 us -> 46.2 us
  local copies, waits for them, and re-layouts: 31.5 us -> 40.8 us
    ppermute x0 -> x30, starting transfers between devices: none -> 218 us  [the longest x15 161 us: per_device(): blocks.append(lax.ppermute(own_block, 'ctx', pairs))]
    all_gather x5 -> x2, waiting for transfers between devices: 160 us -> 10.8 us  [the longest x1 10.8 us: per_device(): lax.all_gather(jnp.concatenate([key_matrix, value_matrix], axis=1), 'dp',...]
    all_gather x2 -> x0, blocking collectives: 77.5 us -> none  [the longest x1 39.1 us: per_device(): lax.all_gather(own_block[3], 'ctx', axis=0, tiled=True)]
    ppermute x0 -> x30, waiting for transfers between devices: none -> 67.4 us  [the longest x15 61.9 us: per_device(): blocks.append(lax.ppermute(own_block, 'ctx', pairs))]
    psum x1 -> x0, blocking collectives: 37.6 us -> none  [per_device(): sums, tally = lax.psum((sums, tally), 'ctx')]
    and x1 -> x13, other arithmetic: 1.91 us -> 14 us  [the longest x8 10.1 us: per_device(): klive = (offsets < counts[source]) & present]
    slice x0 -> x18, local copies, waits for them, and re-layouts: none -> 10.6 us  [the longest x15 10.5 us: per_device(): block[:token_slots, :kv_width]]
    add x1 -> x8, other arithmetic: 0.55 us -> 10.1 us  [per_device(): kpos = starts[source] + offsets]
  transfers between devices with their start and end apart: 5 -> 32, of which waited for: 4 -> 8; matrix products, arithmetic and copies ran while one was open for 12% -> 14% of each run, Pallas kernels for 0% -> 0%
where the time goes in v1:
time: 441 us; the launch traced here: 436 us
  starting transfers between devices  218 us (49%)
  waiting for transfers between devices  79 us (18%)
  other arithmetic  46.2 us (10%)
  local copies, waits for them, and re-layouts  40.8 us (9%)
  matrix products  36.1 us (8%)
  between operations  16.3 us (4%)
    ppermute x15, starting transfers between devices, per_device(): blocks.append(lax.ppermute(own_block, 'ctx', pairs))  161 us
    ppermute x15, waiting for transfers between devices, per_device(): blocks.append(lax.ppermute(own_block, 'ctx', pairs))  61.9 us
    ppermute x15, starting transfers between devices, per_device(): gathered.append(lax.ppermute(partial, 'ctx', pairs))  56.8 us
    dot_general x1, local copies, waits for them, and re-layouts, per_device(): query = jnp.dot(inputs, query_weights, preferred_element_type=jnp.float32)  17.5 us
    dot_general x16, matrix products, per_device(): jnp.einsum('hgqk,khd->qhgd', weights.astype(jnp.bfloat16), value_portion,...  16.4 us
    all_gather x1, waiting for transfers between devices, per_device(): lax.all_gather(jnp.concatenate([key_matrix, value_matrix], axis=1), 'dp',...  10.8 us
    slice x15, local copies, waits for them, and re-layouts, per_device(): block[:token_slots, :kv_width]  10.5 us
    select_n x8, other arithmetic, per_device(): kchunk = (kpos + STRETCH - cstart) // STRETCH  10.2 us
  transfers between devices with their start and end apart: 32, of which 8 were waited for; matrix products, arithmetic and copies ran while one was open for 14% of the time, Pallas kernels for 0%

profile of v1, /device:TPU:2, one launch (start us, length us, event | category | flops | bytes accessed | tf_op | source)
XLA Modules:
  0.0 436.2 jit_solution(17176758637463742985)
XLA Ops:
  7.2 1.8 pad_maximum_fusion
  14.4 1.3 iota_add_fusion.12
  15.7 1.3 and_select_fusion.14
  44.3 10.8 %all-gather.3.cloned.1.call-done = bf16[2560,1024]{1,0:T(8,128)(2,1)} async-done(((bf16[160,1024]{1,0:T(8,128)(2,1)}), bf16[2560,1024]{1,0:T(8,128)(2,1)}) %all-gather.3.cloned.1.call-update) | async-done | bytes 5242896 | tf_op jit(solution)/shard_map/all_gather | solution.py:61
  55.2 4.0 convolution_bitcast_fusion
  67.1 9.4 %collective-permute-start.10 = (bf16[136,1024]{0,1:T(8,128)(2,1)S(1)}, bf16[136,1024]{0,1:T(8,128)(2,1)S(1)}, u32[]{:S(2)}, u32[]{:S(2)}) collective-permute-start(bf16[136,1024]{0,1:T(8,128)(2,1)S(1)} %fusion.99), channel_id=1, source_target_pairs={{0,11},{1,12},{2,13},{3,14},{4,15},{16,27},{17,28},{18,29},{19,30}... | collective-permute-start | bytes 835592 | tf_op jit(solution)/shard_map/ppermute | solution.py:75
  76.6 2.5 collective-permute-start.9
  83.5 16.7 %collective-permute-done.10 = bf16[136,1024]{0,1:T(8,128)(2,1)S(1)} collective-permute-done((bf16[136,1024]{0,1:T(8,128)(2,1)S(1)}, bf16[136,1024]{0,1:T(8,128)(2,1)S(1)}, u32[]{:S(2)}, u32[]{:S(2)}) %collective-permute-start.10) | collective-permute-done | bytes 278560 | tf_op jit(solution)/shard_map/ppermute | solution.py:75
  102.6 71.4 %collective-permute-start.4 = (bf16[136,1024]{0,1:T(8,128)(2,1)S(1)}, bf16[136,1024]{0,1:T(8,128)(2,1)S(1)}, u32[]{:S(2)}, u32[]{:S(2)}) collective-permute-start(bf16[136,1024]{0,1:T(8,128)(2,1)S(1)} %fusion.99), channel_id=1, source_target_pairs={{0,5},{1,6},{2,7},{3,8},{4,9},{5,10},{6,11},{7,12},{8,13},{9,14},{... | collective-permute-start | bytes 835592 | tf_op jit(solution)/shard_map/ppermute | solution.py:75
  174.1 1.9 collective-permute-start.3
  176.2 25.1 %collective-permute-start.2 = (bf16[136,1024]{0,1:T(8,128)(2,1)S(1)}, bf16[136,1024]{0,1:T(8,128)(2,1)S(1)}, u32[]{:S(2)}, u32[]{:S(2)}) collective-permute-start(bf16[136,1024]{0,1:T(8,128)(2,1)S(1)} %fusion.99), channel_id=1, source_target_pairs={{0,3},{1,4},{2,5},{3,6},{4,7},{5,8},{6,9},{7,10},{8,11},{9,12},{10... | collective-permute-start | bytes 835592 | tf_op jit(solution)/shard_map/ppermute | solution.py:75
  201.4 38.5 %collective-permute-start.1 = (bf16[136,1024]{0,1:T(8,128)(2,1)S(1)}, bf16[136,1024]{0,1:T(8,128)(2,1)S(1)}, u32[]{:S(2)}, u32[]{:S(2)}) collective-permute-start(bf16[136,1024]{0,1:T(8,128)(2,1)S(1)} %fusion.99), channel_id=1, source_target_pairs={{0,2},{1,3},{2,4},{3,5},{4,6},{5,7},{6,8},{7,9},{8,10},{9,11},{10,... | collective-permute-start | bytes 835592 | tf_op jit(solution)/shard_map/ppermute | solution.py:75
  240.0 4.3 collective-permute-start
  244.6 7.7 %collective-permute-done.2 = bf16[136,1024]{0,1:T(8,128)(2,1)S(1)} collective-permute-done((bf16[136,1024]{0,1:T(8,128)(2,1)S(1)}, bf16[136,1024]{0,1:T(8,128)(2,1)S(1)}, u32[]{:S(2)}, u32[]{:S(2)}) %collective-permute-start.2) | collective-permute-done | bytes 278560 | tf_op jit(solution)/shard_map/ppermute | solution.py:75
  252.5 27.9 %collective-permute-done.1 = bf16[136,1024]{0,1:T(8,128)(2,1)S(1)} collective-permute-done((bf16[136,1024]{0,1:T(8,128)(2,1)S(1)}, bf16[136,1024]{0,1:T(8,128)(2,1)S(1)}, u32[]{:S(2)}, u32[]{:S(2)}) %collective-permute-start.1) | collective-permute-done | bytes 278560 | tf_op jit(solution)/shard_map/ppermute | solution.py:75
  280.5 8.6 %collective-permute-done = bf16[136,1024]{0,1:T(8,128)(2,1)S(1)} collective-permute-done((bf16[136,1024]{0,1:T(8,128)(2,1)S(1)}, bf16[136,1024]{0,1:T(8,128)(2,1)S(1)}, u32[]{:S(2)}, u32[]{:S(2)}) %collective-permute-start) | collective-permute-done | bytes 278560 | tf_op jit(solution)/shard_map/ppermute | solution.py:75
  303.6 17.5 %copy.101 = bf16[2560,2560]{1,0:T(8,128)(2,1)} copy(bf16[2560,2560]{0,1:T(8,128)(2,1)} %bitcast.393) | data formatting | bytes 26214400 | tf_op jit(solution)/shard_map/dot_general | solution.py:78
  321.1 6.9 %fusion.66 = f32[128,20,128]{0,2,1:T(8,128)S(1)} fusion(bf16[20,128,2560]{2,1,0:T(8,128)(2,1)} %bitcast.392, bf16[1,128,2560]{2,1,0:T(8,128)(2,1)S(1)} %copy-done), kind=kOutput, calls=%fused_computation.91 | convolution fusion | flops 1677721600 | bytes 15073280 | tf_op jit(solution)/shard_map/dot_general | solution.py:78
  328.8 1.5 copy.102
  330.3 2.1 fusion.62
  349.1 10.7 %fusion.79 = f32[4,128,5,128]{3,1,2,0:T(8,128)S(1)} fusion(bf16[128,4,128,1]{0,2,3,1:T(8,128)(2,1)S(1)} %bitcast.407, bf16[4,5,128,128]{2,3,1,0:T(8,128)(2,1)S(1)} %get-tuple-element.123), kind=kOutput, calls=%fused_computation.104 | convolution fusion | flops 83886080 | bytes 2097152 | tf_op jit(solution)/shard_map/hgqk,khd->qhgd/dot_general | solution.py:109
  364.3 16.5 %collective-permute-start.29 = (f32[64]{0:T(128)S(1)}, f32[64]{0:T(128)S(1)}, u32[]{:S(2)}, u32[]{:S(2)}) collective-permute-start(f32[64]{0:T(128)S(1)} %pad_maximum_fusion.2), channel_id=1, source_target_pairs={{0,15},{1,0},{2,1},{3,2},{4,3},{5,4},{6,5},{7,6},{8,7},{9,8},{10,9... | collective-permute-start | bytes 776 | tf_op jit(solution)/shard_map/ppermute | solution.py:129
  380.9 10.7 %collective-permute-start.28 = (f32[64]{0:T(128)S(1)}, f32[64]{0:T(128)S(1)}, u32[]{:S(2)}, u32[]{:S(2)}) collective-permute-start(f32[64]{0:T(128)S(1)} %pad_maximum_fusion.2), channel_id=1, source_target_pairs={{0,14},{1,15},{2,0},{3,1},{4,2},{5,3},{6,4},{7,5},{8,6},{9,7},{10,... | collective-permute-start | bytes 776 | tf_op jit(solution)/shard_map/ppermute | solution.py:129
  391.6 8.8 %collective-permute-start.24 = (f32[64]{0:T(128)S(1)}, f32[64]{0:T(128)S(1)}, u32[]{:S(2)}, u32[]{:S(2)}) collective-permute-start(f32[64]{0:T(128)S(1)} %pad_maximum_fusion.2), channel_id=1, source_target_pairs={{0,10},{1,11},{2,12},{3,13},{4,14},{5,15},{6,0},{7,1},{8,2},{9,3},... | collective-permute-start | bytes 776 | tf_op jit(solution)/shard_map/ppermute | solution.py:129
  400.5 2.3 collective-permute-start.22
  402.8 2.7 collective-permute-start.21
  405.5 7.1 %collective-permute-start.20 = (f32[64]{0:T(128)S(1)}, f32[64]{0:T(128)S(1)}, u32[]{:S(2)}, u32[]{:S(2)}) collective-permute-start(f32[64]{0:T(128)S(1)} %pad_maximum_fusion.2), channel_id=1, source_target_pairs={{0,6},{1,7},{2,8},{3,9},{4,10},{5,11},{6,12},{7,13},{8,14},{9,15},... | collective-permute-start | bytes 776 | tf_op jit(solution)/shard_map/ppermute | solution.py:129
  412.6 1.9 collective-permute-start.19
  414.7 3.0 collective-permute-start.17
  417.7 3.5 collective-permute-start.16
  422.3 3.8 collective-permute-done.16
  426.1 1.7 collective-permute-done.15
  (275 shorter events, 85.9 us)
Async XLA Ops:
  7.2 48.0 %all-gather.3.cloned.1.call-start = ((), (), s32[]{:S(2)}) async-start(), calls=%async_computation | async-start | bytes 5570560 | tf_op jit(solution)/shard_map/all_gather | solution.py:61
  9.1 294.5 %all-gather.5.cloned.1.call-start = ((), (), s32[]{:S(2)}) async-start(), calls=%async_computation.1 | async-start | bytes 13926400 | tf_op jit(solution)/shard_map/all_gather | solution.py:77
  60.3 16.2 %collective-permute-start.14 = (bf16[136,1024]{0,1:T(8,128)(2,1)S(1)}, bf16[136,1024]{0,1:T(8,128)(2,1)S(1)}, u32[]{:S(2)}, u32[]{:S(2)}) collective-permute-start(bf16[136,1024]{0,1:T(8,128)(2,1)S(1)} %fusion.99), channel_id=1, source_target_pairs={{0,15},{16,31},{32,47},{48,63},{64,79},{80,95},{96,111},{112,127},... | collective-permute-start | bytes 835592 | tf_op jit(solution)/shard_map/ppermute | solution.py:75
  62.3 16.8 %collective-permute-start.13 = (bf16[136,1024]{0,1:T(8,128)(2,1)S(1)}, bf16[136,1024]{0,1:T(8,128)(2,1)S(1)}, u32[]{:S(2)}, u32[]{:S(2)}) collective-permute-start(bf16[136,1024]{0,1:T(8,128)(2,1)S(1)} %fusion.99), channel_id=1, source_target_pairs={{0,14},{1,15},{16,30},{17,31},{32,46},{33,47},{48,62},{49,63},{64,... | collective-permute-start | bytes 835592 | tf_op jit(solution)/shard_map/ppermute | solution.py:75
  64.1 16.5 %collective-permute-start.12 = (bf16[136,1024]{0,1:T(8,128)(2,1)S(1)}, bf16[136,1024]{0,1:T(8,128)(2,1)S(1)}, u32[]{:S(2)}, u32[]{:S(2)}) collective-permute-start(bf16[136,1024]{0,1:T(8,128)(2,1)S(1)} %fusion.99), channel_id=1, source_target_pairs={{0,13},{1,14},{2,15},{16,29},{17,30},{18,31},{32,45},{33,46},{34,4... | collective-permute-start | bytes 835592 | tf_op jit(solution)/shard_map/ppermute | solution.py:75
  66.5 15.6 %collective-permute-start.11 = (bf16[136,1024]{0,1:T(8,128)(2,1)S(1)}, bf16[136,1024]{0,1:T(8,128)(2,1)S(1)}, u32[]{:S(2)}, u32[]{:S(2)}) collective-permute-start(bf16[136,1024]{0,1:T(8,128)(2,1)S(1)} %fusion.99), channel_id=1, source_target_pairs={{0,12},{1,13},{2,14},{3,15},{16,28},{17,29},{18,30},{19,31},{32,44... | collective-permute-start | bytes 835592 | tf_op jit(solution)/shard_map/ppermute | solution.py:75
  67.1 33.1 %collective-permute-start.10 = (bf16[136,1024]{0,1:T(8,128)(2,1)S(1)}, bf16[136,1024]{0,1:T(8,128)(2,1)S(1)}, u32[]{:S(2)}, u32[]{:S(2)}) collective-permute-start(bf16[136,1024]{0,1:T(8,128)(2,1)S(1)} %fusion.99), channel_id=1, source_target_pairs={{0,11},{1,12},{2,13},{3,14},{4,15},{16,27},{17,28},{18,29},{19,30}... | collective-permute-start | bytes 835592 | tf_op jit(solution)/shard_map/ppermute | solution.py:75
  76.6 26.0 %collective-permute-start.9 = (bf16[136,1024]{0,1:T(8,128)(2,1)S(1)}, bf16[136,1024]{0,1:T(8,128)(2,1)S(1)}, u32[]{:S(2)}, u32[]{:S(2)}) collective-permute-start(bf16[136,1024]{0,1:T(8,128)(2,1)S(1)} %fusion.99), channel_id=1, source_target_pairs={{0,10},{1,11},{2,12},{3,13},{4,14},{5,15},{16,26},{17,27},{18,28},... | collective-permute-start | bytes 835592 | tf_op jit(solution)/shard_map/ppermute | solution.py:75
  79.2 94.9 %collective-permute-start.8 = (bf16[136,1024]{0,1:T(8,128)(2,1)S(1)}, bf16[136,1024]{0,1:T(8,128)(2,1)S(1)}, u32[]{:S(2)}, u32[]{:S(2)}) collective-permute-start(bf16[136,1024]{0,1:T(8,128)(2,1)S(1)} %fusion.99), channel_id=1, source_target_pairs={{0,9},{1,10},{2,11},{3,12},{4,13},{5,14},{6,15},{16,25},{17,26},{1... | collective-permute-start | bytes 835592 | tf_op jit(solution)/shard_map/ppermute | solution.py:75
  80.6 95.5 %collective-permute-start.7 = (bf16[136,1024]{0,1:T(8,128)(2,1)S(1)}, bf16[136,1024]{0,1:T(8,128)(2,1)S(1)}, u32[]{:S(2)}, u32[]{:S(2)}) collective-permute-start(bf16[136,1024]{0,1:T(8,128)(2,1)S(1)} %fusion.99), channel_id=1, source_target_pairs={{0,8},{1,9},{2,10},{3,11},{4,12},{5,13},{6,14},{7,15},{16,24},{17,... | collective-permute-start | bytes 835592 | tf_op jit(solution)/shard_map/ppermute | solution.py:75
  82.1 119.3 %collective-permute-start.6 = (bf16[136,1024]{0,1:T(8,128)(2,1)S(1)}, bf16[136,1024]{0,1:T(8,128)(2,1)S(1)}, u32[]{:S(2)}, u32[]{:S(2)}) collective-permute-start(bf16[136,1024]{0,1:T(8,128)(2,1)S(1)} %fusion.99), channel_id=1, source_target_pairs={{0,7},{1,8},{2,9},{3,10},{4,11},{5,12},{6,13},{7,14},{8,15},{16,23... | collective-permute-start | bytes 835592 | tf_op jit(solution)/shard_map/ppermute | solution.py:75
  100.3 139.7 %collective-permute-start.5 = (bf16[136,1024]{0,1:T(8,128)(2,1)S(1)}, bf16[136,1024]{0,1:T(8,128)(2,1)S(1)}, u32[]{:S(2)}, u32[]{:S(2)}) collective-permute-start(bf16[136,1024]{0,1:T(8,128)(2,1)S(1)} %fusion.99), channel_id=1, source_target_pairs={{0,6},{1,7},{2,8},{3,9},{4,10},{5,11},{6,12},{7,13},{8,14},{9,15},... | collective-permute-start | bytes 835592 | tf_op jit(solution)/shard_map/ppermute | solution.py:75
  102.6 141.8 %collective-permute-start.4 = (bf16[136,1024]{0,1:T(8,128)(2,1)S(1)}, bf16[136,1024]{0,1:T(8,128)(2,1)S(1)}, u32[]{:S(2)}, u32[]{:S(2)}) collective-permute-start(bf16[136,1024]{0,1:T(8,128)(2,1)S(1)} %fusion.99), channel_id=1, source_target_pairs={{0,5},{1,6},{2,7},{3,8},{4,9},{5,10},{6,11},{7,12},{8,13},{9,14},{... | collective-permute-start | bytes 835592 | tf_op jit(solution)/shard_map/ppermute | solution.py:75
  174.1 70.3 %collective-permute-start.3 = (bf16[136,1024]{0,1:T(8,128)(2,1)S(1)}, bf16[136,1024]{0,1:T(8,128)(2,1)S(1)}, u32[]{:S(2)}, u32[]{:S(2)}) collective-permute-start(bf16[136,1024]{0,1:T(8,128)(2,1)S(1)} %fusion.99), channel_id=1, source_target_pairs={{0,4},{1,5},{2,6},{3,7},{4,8},{5,9},{6,10},{7,11},{8,12},{9,13},{1... | collective-permute-start | bytes 835592 | tf_op jit(solution)/shard_map/ppermute | solution.py:75
  176.2 76.2 %collective-permute-start.2 = (bf16[136,1024]{0,1:T(8,128)(2,1)S(1)}, bf16[136,1024]{0,1:T(8,128)(2,1)S(1)}, u32[]{:S(2)}, u32[]{:S(2)}) collective-permute-start(bf16[136,1024]{0,1:T(8,128)(2,1)S(1)} %fusion.99), channel_id=1, source_target_pairs={{0,3},{1,4},{2,5},{3,6},{4,7},{5,8},{6,9},{7,10},{8,11},{9,12},{10... | collective-permute-start | bytes 835592 | tf_op jit(solution)/shard_map/ppermute | solution.py:75
  201.4 79.0 %collective-permute-start.1 = (bf16[136,1024]{0,1:T(8,128)(2,1)S(1)}, bf16[136,1024]{0,1:T(8,128)(2,1)S(1)}, u32[]{:S(2)}, u32[]{:S(2)}) collective-permute-start(bf16[136,1024]{0,1:T(8,128)(2,1)S(1)} %fusion.99), channel_id=1, source_target_pairs={{0,2},{1,3},{2,4},{3,5},{4,6},{5,7},{6,8},{7,9},{8,10},{9,11},{10,... | collective-permute-start | bytes 835592 | tf_op jit(solution)/shard_map/ppermute | solution.py:75
  240.0 49.1 %collective-permute-start = (bf16[136,1024]{0,1:T(8,128)(2,1)S(1)}, bf16[136,1024]{0,1:T(8,128)(2,1)S(1)}, u32[]{:S(2)}, u32[]{:S(2)}) collective-permute-start(bf16[136,1024]{0,1:T(8,128)(2,1)S(1)} %fusion.99), channel_id=1, source_target_pairs={{0,1},{1,2},{2,3},{3,4},{4,5},{5,6},{6,7},{7,8},{8,9},{9,10},{10,1... | collective-permute-start | bytes 835592 | tf_op jit(solution)/shard_map/ppermute | solution.py:75
  364.3 27.2 %collective-permute-start.29 = (f32[64]{0:T(128)S(1)}, f32[64]{0:T(128)S(1)}, u32[]{:S(2)}, u32[]{:S(2)}) collective-permute-start(f32[64]{0:T(128)S(1)} %pad_maximum_fusion.2), channel_id=1, source_target_pairs={{0,15},{1,0},{2,1},{3,2},{4,3},{5,4},{6,5},{7,6},{8,7},{9,8},{10,9... | collective-permute-start | bytes 776 | tf_op jit(solution)/shard_map/ppermute | solution.py:129
  380.9 19.5 %collective-permute-start.28 = (f32[64]{0:T(128)S(1)}, f32[64]{0:T(128)S(1)}, u32[]{:S(2)}, u32[]{:S(2)}) collective-permute-start(f32[64]{0:T(128)S(1)} %pad_maximum_fusion.2), channel_id=1, source_target_pairs={{0,14},{1,15},{2,0},{3,1},{4,2},{5,3},{6,4},{7,5},{8,6},{9,7},{10,... | collective-permute-start | bytes 776 | tf_op jit(solution)/shard_map/ppermute | solution.py:129
  391.5 9.0 %collective-permute-start.27 = (f32[64]{0:T(128)S(1)}, f32[64]{0:T(128)S(1)}, u32[]{:S(2)}, u32[]{:S(2)}) collective-permute-start(f32[64]{0:T(128)S(1)} %pad_maximum_fusion.2), channel_id=1, source_target_pairs={{0,13},{1,14},{2,15},{3,0},{4,1},{5,2},{6,3},{7,4},{8,5},{9,6},{10... | collective-permute-start | bytes 776 | tf_op jit(solution)/shard_map/ppermute | solution.py:129
  391.5 11.3 %collective-permute-start.26 = (f32[64]{0:T(128)S(1)}, f32[64]{0:T(128)S(1)}, u32[]{:S(2)}, u32[]{:S(2)}) collective-permute-start(f32[64]{0:T(128)S(1)} %pad_maximum_fusion.2), channel_id=1, source_target_pairs={{0,12},{1,13},{2,14},{3,15},{4,0},{5,1},{6,2},{7,3},{8,4},{9,5},{1... | collective-permute-start | bytes 776 | tf_op jit(solution)/shard_map/ppermute | solution.py:129
  391.5 14.0 %collective-permute-start.25 = (f32[64]{0:T(128)S(1)}, f32[64]{0:T(128)S(1)}, u32[]{:S(2)}, u32[]{:S(2)}) collective-permute-start(f32[64]{0:T(128)S(1)} %pad_maximum_fusion.2), channel_id=1, source_target_pairs={{0,11},{1,12},{2,13},{3,14},{4,15},{5,0},{6,1},{7,2},{8,3},{9,4},{... | collective-permute-start | bytes 776 | tf_op jit(solution)/shard_map/ppermute | solution.py:129
  391.6 21.1 %collective-permute-start.24 = (f32[64]{0:T(128)S(1)}, f32[64]{0:T(128)S(1)}, u32[]{:S(2)}, u32[]{:S(2)}) collective-permute-start(f32[64]{0:T(128)S(1)} %pad_maximum_fusion.2), channel_id=1, source_target_pairs={{0,10},{1,11},{2,12},{3,13},{4,14},{5,15},{6,0},{7,1},{8,2},{9,3},... | collective-permute-start | bytes 776 | tf_op jit(solution)/shard_map/ppermute | solution.py:129
  400.4 14.2 %collective-permute-start.23 = (f32[64]{0:T(128)S(1)}, f32[64]{0:T(128)S(1)}, u32[]{:S(2)}, u32[]{:S(2)}) collective-permute-start(f32[64]{0:T(128)S(1)} %pad_maximum_fusion.2), channel_id=1, source_target_pairs={{0,9},{1,10},{2,11},{3,12},{4,13},{5,14},{6,15},{7,0},{8,1},{9,2},... | collective-permute-start | bytes 776 | tf_op jit(solution)/shard_map/ppermute | solution.py:129
  400.5 14.2 %collective-permute-start.22 = (f32[64]{0:T(128)S(1)}, f32[64]{0:T(128)S(1)}, u32[]{:S(2)}, u32[]{:S(2)}) collective-permute-start(f32[64]{0:T(128)S(1)} %pad_maximum_fusion.2), channel_id=1, source_target_pairs={{0,8},{1,9},{2,10},{3,11},{4,12},{5,13},{6,14},{7,15},{8,0},{9,1},... | collective-permute-start | bytes 776 | tf_op jit(solution)/shard_map/ppermute | solution.py:129
  402.8 14.9 %collective-permute-start.21 = (f32[64]{0:T(128)S(1)}, f32[64]{0:T(128)S(1)}, u32[]{:S(2)}, u32[]{:S(2)}) collective-permute-start(f32[64]{0:T(128)S(1)} %pad_maximum_fusion.2), channel_id=1, source_target_pairs={{0,7},{1,8},{2,9},{3,10},{4,11},{5,12},{6,13},{7,14},{8,15},{9,0},... | collective-permute-start | bytes 776 | tf_op jit(solution)/shard_map/ppermute | solution.py:129
  405.5 15.7 %collective-permute-start.20 = (f32[64]{0:T(128)S(1)}, f32[64]{0:T(128)S(1)}, u32[]{:S(2)}, u32[]{:S(2)}) collective-permute-start(f32[64]{0:T(128)S(1)} %pad_maximum_fusion.2), channel_id=1, source_target_pairs={{0,6},{1,7},{2,8},{3,9},{4,10},{5,11},{6,12},{7,13},{8,14},{9,15},... | collective-permute-start | bytes 776 | tf_op jit(solution)/shard_map/ppermute | solution.py:129
  412.6 9.7 %collective-permute-start.19 = (f32[64]{0:T(128)S(1)}, f32[64]{0:T(128)S(1)}, u32[]{:S(2)}, u32[]{:S(2)}) collective-permute-start(f32[64]{0:T(128)S(1)} %pad_maximum_fusion.2), channel_id=1, source_target_pairs={{0,5},{1,6},{2,7},{3,8},{4,9},{5,10},{6,11},{7,12},{8,13},{9,14},{... | collective-permute-start | bytes 776 | tf_op jit(solution)/shard_map/ppermute | solution.py:129
  414.6 7.7 %collective-permute-start.18 = (f32[64]{0:T(128)S(1)}, f32[64]{0:T(128)S(1)}, u32[]{:S(2)}, u32[]{:S(2)}) collective-permute-start(f32[64]{0:T(128)S(1)} %pad_maximum_fusion.2), channel_id=1, source_target_pairs={{0,4},{1,5},{2,6},{3,7},{4,8},{5,9},{6,10},{7,11},{8,12},{9,13},{1... | collective-permute-start | bytes 776 | tf_op jit(solution)/shard_map/ppermute | solution.py:129
  414.7 7.6 %collective-permute-start.17 = (f32[64]{0:T(128)S(1)}, f32[64]{0:T(128)S(1)}, u32[]{:S(2)}, u32[]{:S(2)}) collective-permute-start(f32[64]{0:T(128)S(1)} %pad_maximum_fusion.2), channel_id=1, source_target_pairs={{0,3},{1,4},{2,5},{3,6},{4,7},{5,8},{6,9},{7,10},{8,11},{9,12},{10... | collective-permute-start | bytes 776 | tf_op jit(solution)/shard_map/ppermute | solution.py:129
  417.7 8.4 %collective-permute-start.16 = (f32[64]{0:T(128)S(1)}, f32[64]{0:T(128)S(1)}, u32[]{:S(2)}, u32[]{:S(2)}) collective-permute-start(f32[64]{0:T(128)S(1)} %pad_maximum_fusion.2), channel_id=1, source_target_pairs={{0,2},{1,3},{2,4},{3,5},{4,6},{5,7},{6,8},{7,9},{8,10},{9,11},{10,... | collective-permute-start | bytes 776 | tf_op jit(solution)/shard_map/ppermute | solution.py:129
  421.2 6.6 %collective-permute-start.15 = (f32[64]{0:T(128)S(1)}, f32[64]{0:T(128)S(1)}, u32[]{:S(2)}, u32[]{:S(2)}) collective-permute-start(f32[64]{0:T(128)S(1)} %pad_maximum_fusion.2), channel_id=1, source_target_pairs={{0,1},{1,2},{2,3},{3,4},{4,5},{5,6},{6,7},{7,8},{8,9},{9,10},{10,1... | collective-permute-start | bytes 776 | tf_op jit(solution)/shard_map/ppermute | solution.py:129
  (50 other events, 182.4 us)
Sparse Core Ops, SparseCore 0:
  10.4 44.6 all-gather.2
  57.0 175.3 all-gather.4

commit v2 on v1

--- a/solution.py
+++ b/solution.py
@@ -69,10 +69,20 @@
         own_block = jnp.concatenate(
             [jnp.concatenate([key_norm, value_rows], axis=1), seg_row], axis=0
         )
-        blocks = [own_block]
-        for shift in range(1, shards):
-            pairs = [(s, s + shift) for s in range(shards - shift)]
-            blocks.append(lax.ppermute(own_block, "ctx", pairs))
+        gathered = lax.all_gather(own_block, "ctx", axis=0, tiled=True).reshape(
+            shards, token_slots + 8, 2 * kv_width
+        )
+        key_count = shards * token_slots
+        key_portion = gathered[:, :token_slots, :kv_width].reshape(
+            key_count, KEY_VALUE_HEADS, HEAD_SIZE
+        )
+        value_portion = gathered[:, :token_slots, kv_width:].reshape(
+            key_count, KEY_VALUE_HEADS, HEAD_SIZE
+        )
+        kseg = gathered[:, token_slots, :token_slots].reshape(key_count).astype(jnp.int32)
+        kpos = (starts[:, None] + offsets[None, :]).reshape(key_count)
+        klive = (offsets[None, :] < counts[:, None]).reshape(key_count)
+        kchunk = (kpos + STRETCH - cstart) // STRETCH
 
         query_weights = lax.all_gather(query_weight, "dp", axis=0, tiled=True)
         query = jnp.dot(inputs, query_weights, preferred_element_type=jnp.float32)
@@ -80,38 +90,22 @@
         head_group = QUERY_HEADS // KEY_VALUE_HEADS
         per_head_queries = query_norm.reshape(token_slots, KEY_VALUE_HEADS, head_group, HEAD_SIZE)
 
-        numer = jnp.zeros((token_slots, KEY_VALUE_HEADS, head_group, HEAD_SIZE), jnp.float32)
-        denom = jnp.zeros((KEY_VALUE_HEADS, head_group, token_slots), jnp.float32)
-        for shift, block in enumerate(blocks):
-            source = mine - shift
-            present = source >= 0
-            source = jnp.maximum(source, 0)
-            kpos = starts[source] + offsets
-            klive = (offsets < counts[source]) & present
-            kchunk = (kpos + STRETCH - cstart) // STRETCH
-            kseg = block[token_slots, :token_slots].astype(jnp.int32)
-            key_portion = block[:token_slots, :kv_width].reshape(
-                token_slots, KEY_VALUE_HEADS, HEAD_SIZE
-            )
-            value_portion = block[:token_slots, kv_width:].reshape(
-                token_slots, KEY_VALUE_HEADS, HEAD_SIZE
-            )
-            scores = jnp.einsum(
-                "qhgd,khd->hgqk",
-                per_head_queries,
-                key_portion,
-                preferred_element_type=jnp.float32,
-            ) * (1.0 / math.sqrt(HEAD_SIZE))
-            allowed = (kseg[None, :] == qseg[:, None]) & (kchunk[None, :] == qchunk[:, None])
-            allowed = allowed & klive[None, :] & (kpos[None, :] <= token_places[:, None])
-            weights = jnp.where(allowed[None, None], jnp.exp(scores), 0.0)
-            denom = denom + jnp.sum(weights, axis=-1)
-            numer = numer + jnp.einsum(
-                "hgqk,khd->qhgd",
-                weights.astype(jnp.bfloat16),
-                value_portion,
-                preferred_element_type=jnp.float32,
-            )
+        scores = jnp.einsum(
+            "qhgd,khd->hgqk",
+            per_head_queries,
+            key_portion,
+            preferred_element_type=jnp.float32,
+        ) * (1.0 / math.sqrt(HEAD_SIZE))
+        allowed = (kseg[None, :] == qseg[:, None]) & (kchunk[None, :] == qchunk[:, None])
+        allowed = allowed & klive[None, :] & (kpos[None, :] <= token_places[:, None])
+        weights = jnp.where(allowed[None, None], jnp.exp(scores), 0.0)
+        denom = jnp.sum(weights, axis=-1)
+        numer = jnp.einsum(
+            "hgqk,khd->qhgd",
+            weights.astype(jnp.bfloat16),
+            value_portion,
+            preferred_element_type=jnp.float32,
+        )
 
         denom_rows = jnp.transpose(denom, (2, 0, 1))
         safe = jnp.where(live[:, None, None], denom_rows, 1.0)
@@ -122,15 +116,8 @@
         onehot = span_ids[0][:, None] == jnp.arange(CAND, dtype=jnp.int32)[None, :]
         sums = jnp.sum(jnp.where(onehot, loglik[:, None], 0.0), axis=0)
         tally = jnp.sum(onehot.astype(jnp.float32), axis=0)
-        partial = jnp.concatenate([sums, tally])
-        gathered = [partial]
-        for shift in range(1, shards):
-            pairs = [(s, (s + shift) % shards) for s in range(shards)]
-            gathered.append(lax.ppermute(partial, "ctx", pairs))
-        stacked = jnp.stack(gathered)
-        order = (mine - jnp.arange(shards, dtype=jnp.int32)) % shards
-        total = jnp.sum(jnp.take(stacked, order, axis=0), axis=0)
-        return (attention[None], (total[:CAND] / total[CAND:])[None])
+        sums, tally = lax.psum((sums, tally), "ctx")
+        return (attention[None], (sums / tally)[None])
 
     return per_device
 

time: 441 us -> 319 us (0.72)
  starting transfers between devices: 218 us -> 0.12 us
  waiting for transfers between devices: 79 us -> 182 us
  blocking collectives: 0 us -> 39.7 us
  other arithmetic: 46.2 us -> 10.2 us
  local copies, waits for them, and re-layouts: 40.8 us -> 34.8 us
  matrix products: 36.1 us -> 31.1 us
    ppermute x30 -> x0, starting transfers between devices: 218 us -> none  [the longest x15 161 us: per_device(): blocks.append(lax.ppermute(own_block, 'ctx', pairs))]
    all_gather x0 -> x1, waiting for transfers between devices: none -> 72.4 us  [per_device(): lax.all_gather(own_block, 'ctx', axis=0, tiled=True)]
    ppermute x30 -> x0, waiting for transfers between devices: 67.4 us -> none  [the longest x15 61.9 us: per_device(): blocks.append(lax.ppermute(own_block, 'ctx', pairs))]
    all_gather x1, waiting for transfers between devices: 0.01 us -> 66.9 us  [per_device(): query_weights = lax.all_gather(query_weight, 'dp', axis=0, tiled=True)]
    psum x0 -> x1, blocking collectives: none -> 39.7 us  [per_device(): sums, tally = lax.psum((sums, tally), 'ctx')]
    all_gather x1, waiting for transfers between devices: 10.8 us -> 42.2 us  [per_device(): lax.all_gather(jnp.concatenate([key_matrix, value_matrix], axis=1), 'dp',...]
    select_n x8 -> x1, other arithmetic: 10.2 us -> 0.08 us  [per_device(): kchunk = (kpos + STRETCH - cstart) // STRETCH]
    and x9 -> x0, other arithmetic: 10.1 us -> none  [the longest x8 10.1 us: per_device(): klive = (offsets < counts[source]) & present]
  transfers between devices with their start and end apart: 32 -> 3, of which waited for: 8 -> 3; matrix products, arithmetic and copies ran while one was open for 14% -> 6% of each run, Pallas kernels for 0% -> 0%
where the time goes in v2:
time: 319 us; the launch traced here: 313 us
  waiting for transfers between devices  182 us (57%)
  blocking collectives  39.7 us (12%)
  local copies, waits for them, and re-layouts  34.8 us (11%)
  matrix products  31.1 us (10%)
  between operations  14.6 us (5%)
  other arithmetic  10.2 us (3%)
    all_gather x1, waiting for transfers between devices, per_device(): lax.all_gather(own_block, 'ctx', axis=0, tiled=True)  72.4 us
    all_gather x1, waiting for transfers between devices, per_device(): query_weights = lax.all_gather(query_weight, 'dp', axis=0, tiled=True)  66.9 us
    all_gather x1, waiting for transfers between devices, per_device(): lax.all_gather(jnp.concatenate([key_matrix, value_matrix], axis=1), 'dp',...  42.2 us
    psum x1, blocking collectives, per_device(): sums, tally = lax.psum((sums, tally), 'ctx')  39.7 us
    dot_general x1, local copies, waits for them, and re-layouts, per_device(): query = jnp.dot(inputs, query_weights, preferred_element_type=jnp.float32)  17.6 us
    dot_general x1, matrix products, per_device(): jnp.einsum('qhgd,khd->hgqk', per_head_queries, key_portion, preferred_ele...  10.9 us
    dot_general x1, matrix products, per_device(): jnp.einsum('hgqk,khd->qhgd', weights.astype(jnp.bfloat16), value_portion,...  9.25 us
    dot_general x1, matrix products, per_device(): query = jnp.dot(inputs, query_weights, preferred_element_type=jnp.float32)  6.63 us
  transfers between devices with their start and end apart: 3, of which 3 were waited for; matrix products, arithmetic and copies ran while one was open for 6% of the time, Pallas kernels for 0%

profile of v2, /device:TPU:2, one launch (start us, length us, event | category | flops | bytes accessed | tf_op | source)
XLA Modules:
  0.0 312.6 jit_solution(13906148567668459398)
XLA Ops:
  7.2 1.8 pad_maximum_fusion
  9.1 0.7 convert_element_type.67
  9.8 0.7 copy.51
  10.8 0.7 bitcast_subtract_fusion
  11.5 0.6 dynamic_slice.6
  12.1 0.6 fusion.36
  12.7 0.2 multiply_cosine_fusion
  12.9 42.2 %all-gather.4.cloned.1.call-done = bf16[2560,1024]{1,0:T(8,128)(2,1)} async-done(((bf16[160,1024]{1,0:T(8,128)(2,1)}), bf16[2560,1024]{1,0:T(8,128)(2,1)}) %all-gather.4.cloned.1.call-update) | async-done | bytes 5242896 | tf_op jit(solution)/shard_map/all_gather | solution.py:61
  55.1 4.0 %convolution_bitcast_fusion = f32[128,1024]{0,1:T(8,128)S(1)} fusion(bf16[2560,1024]{1,0:T(8,128)(2,1)} %all-gather.4.cloned.1.call-done, bf16[1,128,2560]{2,1,0:T(8,128)(2,1)S(1)} %copy-done), kind=kOutput, calls=%fused_computation.16 | convolution fusion | flops 671088640 | bytes 6422528 | tf_op jit(solution)/shard_map/dot_general | solution.py:64
  59.4 0.9 copy.53
  60.4 0.7 all-gather.8.cloned.1.call-update
  61.1 0.6 constant_dynamic-slice_fusion
  62.4 0.6 iota_compare_fusion.3
  63.0 0.6 and_select_fusion
  63.9 72.4 %all-gather.6.cloned.1.call-done = bf16[2176,1024]{1,0:T(8,128)(2,1)} async-done(((bf16[136,1024]{1,0:T(8,128)(2,1)}), bf16[2176,1024]{1,0:T(8,128)(2,1)}) %all-gather.6.cloned.1.call-update) | async-done | bytes 4456464 | tf_op jit(solution)/shard_map/all_gather | solution.py:72
  136.3 4.0 %fusion.38 = (bf16[16,128,512]{2,1,0:T(8,128)(2,1)}, bf16[16,128,512]{2,1,0:T(8,128)(2,1)S(1)}) fusion(bf16[16,136,1024]{2,1,0:T(8,128)(2,1)} %bitcast.71), kind=kLoop, calls=%fused_computation.73 | loop fusion | bytes 8388608 | tf_op jit(solution)/shard_map/slice | solution.py:79
  140.3 3.9 %reshape.380 = bf16[2048,4,128]{2,1,0:T(4,128)(2,1)} reshape(bf16[16,128,512]{2,1,0:T(8,128)(2,1)} %get-tuple-element.28) | data formatting | bytes 4194304 | tf_op jit(solution)/shard_map/reshape | solution.py:79
  144.2 2.1 reshape.381
  146.3 0.8 slice_convert_fusion.1
  147.1 2.7 compare_and_fusion
  149.8 66.9 %all-gather.8.cloned.1.call-done = bf16[2560,2560]{1,0:T(8,128)(2,1)} async-done(((bf16[160,2560]{1,0:T(8,128)(2,1)}), bf16[2560,2560]{1,0:T(8,128)(2,1)}) %all-gather.8.cloned.1.call-update) | async-done | bytes 13107216 | tf_op jit(solution)/shard_map/all_gather | solution.py:87
  216.7 17.6 %copy.56 = bf16[2560,2560]{1,0:T(8,128)(2,1)} copy(bf16[2560,2560]{0,1:T(8,128)(2,1)} %bitcast.68) | data formatting | bytes 26214400 | tf_op jit(solution)/shard_map/dot_general | solution.py:88
  234.3 6.6 %fusion.24 = f32[128,20,128]{0,2,1:T(8,128)S(1)} fusion(bf16[20,128,2560]{2,1,0:T(8,128)(2,1)} %bitcast.67, bf16[1,128,2560]{2,1,0:T(8,128)(2,1)S(1)} %copy-done), kind=kOutput, calls=%fused_computation.22 | convolution fusion | flops 1677721600 | bytes 15073280 | tf_op jit(solution)/shard_map/dot_general | solution.py:88
  240.9 0.2 multiply_subtract_fusion
  241.2 1.5 copy.58
  242.7 1.5 copy.57
  244.2 10.9 %fusion = (f32[4,5,128]{2,1,0:T(8,128)S(1)}, f32[4,2048,128,5]{2,1,3,0:T(8,128)}) fusion(pred[128,2048]{0,1:T(8,128)(4,1)} %compare_and_fusion, f32[128,4,5,64]{3,0,2,1:T(8,128)} %copy.58, f32[128,4,5,64]{3,0,2,1:T(8,128)} %copy.57, f32[128,4,5]{0,2,1:T(8,128)S(1)} %rsqrt.21, bf16[2048,4,128,1]{2,1,0,3:T(4,128)(2,1)S(1)} %bitcast.76), kind=kOutput, calls=%fused_computation.1 | convolution fusion | flops 1358886400 | bytes 24662016 | tf_op jit(solution)/shard_map/qhgd,khd->hgqk/dot_general | solution.py:93
  255.2 9.3 %multiply_convert_fusion = bf16[128,4,5,128]{0,3,2,1:T(8,128)(2,1)S(1)} fusion(f32[4,2048,128,5]{2,1,3,0:T(8,128)} %get-tuple-element.37, pred[128,2048]{0,1:T(8,128)(4,1)S(1)} %copy-done.4, bf16[2048,4,128,1]{2,1,0,3:T(4,128)(2,1)S(1)} %bitcast.75, f32[128]{0:T(128)S(1)} %get-tuple-element.41, f32[128,4,5]{0,2,1:T(8,128)S(1)} %select_bitcast_fusion), kind=kOutput, calls=%fused_computation.15 | convolution fusion | flops 1358888960 | bytes 23996928 | tf_op jit(solution)/shard_map/hgqk,khd->qhgd/dot_general | solution.py:103
  264.5 1.1 copy.61
  265.6 0.2 fusion.32
  265.9 39.7 %all-reduce.1 = (f32[32]{0:T(128)S(1)}, f32[32]{0:T(128)S(1)}) all-reduce(f32[32]{0:T(128)S(1)} %get-tuple-element.25, f32[32]{0:T(128)S(1)} %get-tuple-element.24), channel_id=1, replica_groups=mesh['dp'=16,'ctx'=16] {'ctx'}, use_global_device_ids=true, to_apply=%region_5.6 | all-reduce | flops 64 | bytes 512 | tf_op jit(solution)/shard_map/psum | solution.py:119
  305.6 0.5 divide_bitcast_fusion
  (43 shorter events, 1.2 us)
Async XLA Ops:
  7.2 48.0 %copy-start = (bf16[1,128,2560]{2,1,0:T(8,128)(2,1)S(1)}, bf16[1,128,2560]{2,1,0:T(8,128)(2,1)}, u32[]{:S(2)}) copy-start(bf16[1,128,2560]{2,1,0:T(8,128)(2,1)} %param.11) | copy-start | bytes 1966084
  7.2 48.0 %all-gather.4.cloned.1.call-start = ((), (), s32[]{:S(2)}) async-start(), calls=%async_computation | async-start | bytes 5570560 | tf_op jit(solution)/shard_map/all_gather | solution.py:61
  9.1 127.2 %all-gather.6.cloned.1.call-start = ((), (), s32[]{:S(2)}) async-start(), calls=%async_computation.1 | async-start | bytes 4734976 | tf_op jit(solution)/shard_map/all_gather | solution.py:72
  59.2 1.9 copy-start.6
  59.2 3.1 copy-start.5
  60.4 156.3 %all-gather.8.cloned.1.call-start = ((), (), s32[]{:S(2)}) async-start(), calls=%async_computation.2 | async-start | bytes 13926400 | tf_op jit(solution)/shard_map/all_gather | solution.py:87
  144.2 2.8 copy-start.7
  241.2 3.0 copy-start.3
  244.2 11.0 %copy-start.2 = (bf16[2048,4,128]{2,1,0:T(4,128)(2,1)S(1)}, bf16[2048,4,128]{2,1,0:T(4,128)(2,1)}, u32[]{:S(2)}) copy-start(bf16[2048,4,128]{2,1,0:T(4,128)(2,1)} %reshape.380) | copy-start | bytes 6291460
  244.2 11.0 %copy-start.4 = (pred[128,2048]{0,1:T(8,128)(4,1)S(1)}, pred[128,2048]{0,1:T(8,128)(4,1)}, u32[]{:S(2)}) copy-start(pred[128,2048]{0,1:T(8,128)(4,1)} %compare_and_fusion) | copy-start | bytes 786436
  255.2 10.6 %copy-start.8 = (s32[1,128]{1,0:T(1,128)S(1)}, s32[1,128]{1,0:T(1,128)}, u32[]{:S(2)}) copy-start(s32[1,128]{1,0:T(1,128)} %param.15) | copy-start | bytes 1540
  255.2 50.9 %copy-start.1 = (bf16[1,128,2560]{2,1,0:T(8,128)(2,1)S(1)}, bf16[1,128,2560]{2,1,0:T(8,128)(2,1)}, u32[]{:S(2)}) copy-start(bf16[1,128,2560]{2,1,0:T(8,128)(2,1)} %param.11) | copy-start | bytes 1966084
Sparse Core Ops, SparseCore 0:
  10.4 44.6 all-gather.3
  60.5 75.7 all-gather.5
  138.1 78.4 all-gather.7

commit v3 on v2

--- a/solution.py
+++ b/solution.py
@@ -69,6 +69,9 @@
         own_block = jnp.concatenate(
             [jnp.concatenate([key_norm, value_rows], axis=1), seg_row], axis=0
         )
+        query_weights = lax.all_gather(query_weight, "dp", axis=0, tiled=True)
+        own_block, query_weights = lax.optimization_barrier((own_block, query_weights))
+        query = jnp.dot(inputs, query_weights, preferred_element_type=jnp.float32)
         gathered = lax.all_gather(own_block, "ctx", axis=0, tiled=True).reshape(
             shards, token_slots + 8, 2 * kv_width
         )
@@ -84,8 +87,6 @@
         klive = (offsets[None, :] < counts[:, None]).reshape(key_count)
         kchunk = (kpos + STRETCH - cstart) // STRETCH
 
-        query_weights = lax.all_gather(query_weight, "dp", axis=0, tiled=True)
-        query = jnp.dot(inputs, query_weights, preferred_element_type=jnp.float32)
         query_norm = rotary_then_norm(query, token_places, QUERY_HEADS)
         head_group = QUERY_HEADS // KEY_VALUE_HEADS
         per_head_queries = query_norm.reshape(token_slots, KEY_VALUE_HEADS, head_group, HEAD_SIZE)

time: 319 us -> 303 us (0.950)
  local copies, waits for them, and re-layouts: 34.8 us -> 17.3 us
    dot_general x1 -> x0, local copies, waits for them, and re-layouts: 17.6 us -> none  [per_device(): query = jnp.dot(inputs, query_weights, preferred_element_type=jnp.float32)]
    all_gather x1, waiting for transfers between devices: 66.9 us -> 74.1 us  [per_device(): query_weights = lax.all_gather(query_weight, 'dp', axis=0, tiled=True)]
    all_gather x1, waiting for transfers between devices: 72.4 us -> 66.1 us  [per_device(): lax.all_gather(own_block, 'ctx', axis=0, tiled=True)]
    concatenate x3 -> x0, local copies, waits for them, and re-layouts: 3.85 us -> none  [the longest x2 2.97 us: rotary_then_norm(): jnp.concatenate([leading_block * cosine - second * sine, second * cosine...]
  transfers between devices with their start and end apart: 3 -> 3, of which waited for: 3 -> 3; matrix products, arithmetic and copies ran while one was open for 6% -> 7% of each run, Pallas kernels for 0% -> 0%
where the time goes in v3:
time: 303 us; the launch traced here: 297 us
  waiting for transfers between devices  182 us (60%)
  blocking collectives  41.6 us (14%)
  matrix products  32 us (11%)
  local copies, waits for them, and re-layouts  17.3 us (6%)
  between operations  14.6 us (5%)
  other arithmetic  9.36 us (3%)
    all_gather x1, waiting for transfers between devices, per_device(): query_weights = lax.all_gather(query_weight, 'dp', axis=0, tiled=True)  74.1 us
    all_gather x1, waiting for transfers between devices, per_device(): lax.all_gather(own_block, 'ctx', axis=0, tiled=True)  66.1 us
    psum x1, blocking collectives, per_device(): sums, tally = lax.psum((sums, tally), 'ctx')  41.6 us
    all_gather x1, waiting for transfers between devices, per_device(): lax.all_gather(jnp.concatenate([key_matrix, value_matrix], axis=1), 'dp',...  41.5 us
    dot_general x1, matrix products, per_device(): jnp.einsum('qhgd,khd->hgqk', per_head_queries, key_portion, preferred_ele...  11.9 us
    dot_general x1, matrix products, per_device(): jnp.einsum('hgqk,khd->qhgd', weights.astype(jnp.bfloat16), value_portion,...  9.2 us
    dot_general x1, matrix products, per_device(): query = jnp.dot(inputs, query_weights, preferred_element_type=jnp.float32)  6.7 us
  transfers between devices with their start and end apart: 3, of which 3 were waited for; matrix products, arithmetic and copies ran while one was open for 7% of the time, Pallas kernels for 0%

profile of v3, /device:TPU:2, one launch (start us, length us, event | category | flops | bytes accessed | tf_op | source)
XLA Modules:
  0.0 297.4 jit_solution(6423307388458347734)
XLA Ops:
  7.2 1.8 pad_maximum_fusion
  9.1 0.7 all-gather.6.cloned.1.call-update
  9.9 0.7 copy.47
  10.7 0.7 convert_element_type.67
  11.4 0.1 copy.67
  11.5 0.7 bitcast_subtract_fusion
  12.2 0.6 dynamic_slice.6
  12.8 0.6 fusion.36
  13.5 0.2 multiply_cosine_fusion
  13.7 41.5 %all-gather.4.cloned.1.call-done = bf16[2560,1024]{1,0:T(8,128)(2,1)} async-done(((bf16[160,1024]{1,0:T(8,128)(2,1)}), bf16[2560,1024]{1,0:T(8,128)(2,1)}) %all-gather.4.cloned.1.call-update) | async-done | bytes 5242896 | tf_op jit(solution)/shard_map/all_gather | solution.py:61
  55.1 4.0 %convolution_bitcast_fusion = f32[128,1024]{0,1:T(8,128)S(1)} fusion(bf16[2560,1024]{1,0:T(8,128)(2,1)} %all-gather.4.cloned.1.call-done, bf16[1,128,2560]{2,1,0:T(8,128)(2,1)S(1)} %copy-done), kind=kOutput, calls=%fused_computation.16 | convolution fusion | flops 671088640 | bytes 6422528 | tf_op jit(solution)/shard_map/dot_general | solution.py:64
  59.4 74.1 %all-gather.6.cloned.1.call-done = bf16[2560,2560]{1,0:T(8,128)(2,1)} async-done(((bf16[160,2560]{1,0:T(8,128)(2,1)}), bf16[2560,2560]{1,0:T(8,128)(2,1)}) %all-gather.6.cloned.1.call-update) | async-done | bytes 13107216 | tf_op jit(solution)/shard_map/all_gather | solution.py:72
  133.6 0.9 copy.49
  134.5 0.7 constant_dynamic-slice_fusion
  135.8 0.6 and_select_fusion
  136.5 0.6 iota_compare_fusion.3
  137.3 6.7 %fusion.24 = f32[2560,128]{1,0:T(8,128)S(1)} fusion(bf16[2560,2560]{1,0:T(8,128)(2,1)} %all-gather.6.cloned.1.call-done, bf16[1,128,2560]{2,1,0:T(8,128)(2,1)S(1)} %copy-done), kind=kOutput, calls=%fused_computation.22 | convolution fusion | flops 1677721600 | bytes 15073280 | tf_op jit(solution)/shard_map/dot_general | solution.py:74
  144.1 0.2 multiply_subtract_fusion
  144.3 1.5 copy.52
  145.8 1.6 copy.53
  147.5 66.1 %all-gather.8.cloned.1.call-done = bf16[2176,1024]{1,0:T(8,128)(2,1)} async-done(((bf16[136,1024]{1,0:T(8,128)(2,1)}), bf16[2176,1024]{1,0:T(8,128)(2,1)}) %all-gather.8.cloned.1.call-update) | async-done | bytes 4456464 | tf_op jit(solution)/shard_map/all_gather | solution.py:75
  213.6 0.8 slice_convert_fusion.1
  214.3 4.0 %fusion.38 = (bf16[16,128,512]{2,1,0:T(8,128)(2,1)S(1)}, bf16[16,128,512]{2,1,0:T(8,128)(2,1)}) fusion(bf16[16,136,1024]{2,1,0:T(8,128)(2,1)} %bitcast.68), kind=kLoop, calls=%fused_computation.73 | loop fusion | bytes 8388608 | tf_op jit(solution)/shard_map/slice | solution.py:82
  218.3 4.0 %reshape.382 = bf16[2048,4,128]{2,1,0:T(4,128)(2,1)} reshape(bf16[16,128,512]{2,1,0:T(8,128)(2,1)} %get-tuple-element.33) | data formatting | bytes 4194304 | tf_op jit(solution)/shard_map/reshape | solution.py:79
  222.3 2.1 reshape.381
  224.4 1.9 compare_and_fusion
  226.3 11.9 %fusion = (f32[4,5,128]{2,1,0:T(8,128)S(1)}, f32[4,2048,128,5]{2,1,3,0:T(8,128)}) fusion(pred[128,2048]{0,1:T(8,128)(4,1)S(1)} %compare_and_fusion, f32[128,4,5,64]{3,0,2,1:T(8,128)} %bitcast.75, f32[128,4,5,64]{3,0,2,1:T(8,128)} %bitcast.74, f32[128,4,5]{0,2,1:T(8,128)S(1)} %rsqrt.21, bf16[2048,4,128,1]{2,1,0,3:T(4,128)(2,1)} %bitcast.72), kind=kOutput, calls=%fused_computation.1 | convolution fusion | flops 1358886400 | bytes 24662016 | tf_op jit(solution)/shard_map/qhgd,khd->hgqk/dot_general | solution.py:94
  238.2 9.2 %multiply_convert_fusion = bf16[128,4,5,128]{0,3,2,1:T(8,128)(2,1)S(1)} fusion(f32[4,2048,128,5]{2,1,3,0:T(8,128)} %get-tuple-element.41, pred[128,2048]{0,1:T(8,128)(4,1)S(1)} %compare_and_fusion, bf16[2048,4,128,1]{2,1,0,3:T(4,128)(2,1)S(1)} %bitcast.71, f32[128]{0:T(128)S(1)} %get-tuple-element.45, f32[128,4,5]{0,2,1:T(8,128)S(1)} %select_bitcast_fusion), kind=kOutput, calls=%fused_computation.15 | convolution fusion | flops 1358888960 | bytes 23996928 | tf_op jit(solution)/shard_map/hgqk,khd->qhgd/dot_general | solution.py:104
  247.4 1.1 copy.56
  248.5 0.2 fusion.32
  248.8 41.6 %all-reduce.1 = (f32[32]{0:T(128)S(1)}, f32[32]{0:T(128)S(1)}) all-reduce(f32[32]{0:T(128)S(1)} %get-tuple-element.29, f32[32]{0:T(128)S(1)} %get-tuple-element.28), channel_id=1, replica_groups=mesh['dp'=16,'ctx'=16] {'ctx'}, use_global_device_ids=true, to_apply=%region_5.6 | all-reduce | flops 64 | bytes 512 | tf_op jit(solution)/shard_map/psum | solution.py:120
  290.4 0.5 divide_bitcast_fusion
  (36 shorter events, 1.0 us)
Async XLA Ops:
  7.2 48.0 %copy-start = (bf16[1,128,2560]{2,1,0:T(8,128)(2,1)S(1)}, bf16[1,128,2560]{2,1,0:T(8,128)(2,1)}, u32[]{:S(2)}) copy-start(bf16[1,128,2560]{2,1,0:T(8,128)(2,1)} %param.11) | copy-start | bytes 1966084
  7.2 48.0 %all-gather.4.cloned.1.call-start = ((), (), s32[]{:S(2)}) async-start(), calls=%async_computation | async-start | bytes 5570560 | tf_op jit(solution)/shard_map/all_gather | solution.py:61
  9.1 124.5 %all-gather.6.cloned.1.call-start = ((), (), s32[]{:S(2)}) async-start(), calls=%async_computation.1 | async-start | bytes 13926400 | tf_op jit(solution)/shard_map/all_gather | solution.py:72
  9.8 203.8 %all-gather.8.cloned.1.call-start = ((), (), s32[]{:S(2)}) async-start(), calls=%async_computation.2 | async-start | bytes 4734976 | tf_op jit(solution)/shard_map/all_gather | solution.py:75
  59.2 75.3 %copy-start.3 = (s32[1,16]{1,0:T(1,128)S(1)}, s32[1,16]{1,0:T(1,128)}, u32[]{:S(2)}) copy-start(s32[1,16]{1,0:T(1,128)} %param.12) | copy-start | bytes 196
  59.2 76.6 %copy-start.2 = (bf16[2560]{0:T(1024)(128)(2,1)S(1)}, bf16[2560]{0:T(1024)(128)(2,1)}, u32[]{:S(2)}) copy-start(bf16[2560]{0:T(1024)(128)(2,1)} %param.19) | copy-start | bytes 15364
  222.3 2.1 copy-start.4
  226.3 11.9 %copy-start.1 = (bf16[2048,4,128]{2,1,0:T(4,128)(2,1)S(1)}, bf16[2048,4,128]{2,1,0:T(4,128)(2,1)}, u32[]{:S(2)}) copy-start(bf16[2048,4,128]{2,1,0:T(4,128)(2,1)} %reshape.381) | copy-start | bytes 6291460
  238.2 10.5 %copy-start.5 = (s32[1,128]{1,0:T(1,128)S(1)}, s32[1,128]{1,0:T(1,128)}, u32[]{:S(2)}) copy-start(s32[1,128]{1,0:T(1,128)} %param.15) | copy-start | bytes 1540
Sparse Core Ops, SparseCore 0:
  10.4 44.6 all-gather.3
  57.0 76.5 all-gather.5
  136.6 76.8 all-gather.7

commit v4 on v3

--- a/solution.py
+++ b/solution.py
@@ -117,8 +117,13 @@
         onehot = span_ids[0][:, None] == jnp.arange(CAND, dtype=jnp.int32)[None, :]
         sums = jnp.sum(jnp.where(onehot, loglik[:, None], 0.0), axis=0)
         tally = jnp.sum(onehot.astype(jnp.float32), axis=0)
-        sums, tally = lax.psum((sums, tally), "ctx")
-        return (attention[None], (sums / tally)[None])
+        total = jnp.concatenate([sums, tally])
+        bit = 1
+        while bit < shards:
+            pairs = [(s, s ^ bit) for s in range(shards)]
+            total = total + lax.ppermute(total, "ctx", pairs)
+            bit *= 2
+        return (attention[None], (total[:CAND] / total[CAND:])[None])
 
     return per_device
 

time: 303 us -> 279 us (0.921); the launches traced: 297 us -> 278 us
  blocking collectives: 41.6 us -> 0 us
  starting transfers between devices: 0.12 us -> 11.7 us
  waiting for transfers between devices: 182 us -> 193 us
    psum x1 -> x0, blocking collectives: 41.6 us -> none  [per_device(): sums, tally = lax.psum((sums, tally), 'ctx')]
    ppermute x0 -> x4, starting transfers between devices: none -> 11.6 us  [per_device(): total = total + lax.ppermute(total, 'ctx', pairs)]
    ppermute x0 -> x4, waiting for transfers between devices: none -> 10.8 us  [per_device(): total = total + lax.ppermute(total, 'ctx', pairs)]
  transfers between devices with their start and end apart: 3 -> 7, of which waited for: 3 -> 7; matrix products, arithmetic and copies ran while one was open for 7% -> 8% of each run, Pallas kernels for 0% -> 0%
where the time goes in v4:
time: 279 us; the launch traced here: 278 us
  waiting for transfers between devices  193 us (69%)
  matrix products  31.9 us (11%)
  local copies, waits for them, and re-layouts  17.2 us (6%)
  between operations  14.6 us (5%)
  starting transfers between devices  11.7 us (4%)
  other arithmetic  9.58 us (3%)
    all_gather x1, waiting for transfers between devices, per_device(): query_weights = lax.all_gather(query_weight, 'dp', axis=0, tiled=True)  74.1 us
    all_gather x1, waiting for transfers between devices, per_device(): lax.all_gather(own_block, 'ctx', axis=0, tiled=True)  66.2 us
    all_gather x1, waiting for transfers between devices, per_device(): lax.all_gather(jnp.concatenate([key_matrix, value_matrix], axis=1), 'dp',...  41.5 us
    dot_general x1, matrix products, per_device(): jnp.einsum('qhgd,khd->hgqk', per_head_queries, key_portion, preferred_ele...  11.8 us
    ppermute x4, starting transfers between devices, per_device(): total = total + lax.ppermute(total, 'ctx', pairs)  11.6 us
    ppermute x4, waiting for transfers between devices, per_device(): total = total + lax.ppermute(total, 'ctx', pairs)  10.8 us
    dot_general x1, matrix products, per_device(): jnp.einsum('hgqk,khd->qhgd', weights.astype(jnp.bfloat16), value_portion,...  9.19 us
    dot_general x1, matrix products, per_device(): query = jnp.dot(inputs, query_weights, preferred_element_type=jnp.float32)  6.7 us
  transfers between devices with their start and end apart: 7, of which 7 were waited for; matrix products, arithmetic and copies ran while one was open for 8% of the time, Pallas kernels for 0%

profile of v4, /device:TPU:2, one launch (start us, length us, event | category | flops | bytes accessed | tf_op | source)
XLA Modules:
  0.0 278.4 jit_solution(260343690723935003)
XLA Ops:
  7.2 1.8 pad_maximum_fusion
  9.1 0.7 all-gather.6.cloned.1.call-update
  9.9 0.7 copy.47
  10.7 0.7 convert_element_type.67
  11.5 0.7 bitcast_subtract_fusion
  12.2 0.6 dynamic_slice.6
  12.8 0.6 fusion.37
  13.7 41.5 %all-gather.4.cloned.1.call-done = bf16[2560,1024]{1,0:T(8,128)(2,1)} async-done(((bf16[160,1024]{1,0:T(8,128)(2,1)}), bf16[2560,1024]{1,0:T(8,128)(2,1)}) %all-gather.4.cloned.1.call-update) | async-done | bytes 5242896 | tf_op jit(solution)/shard_map/all_gather | solution.py:61
  55.1 4.0 %convolution_bitcast_fusion = f32[128,1024]{0,1:T(8,128)S(1)} fusion(bf16[2560,1024]{1,0:T(8,128)(2,1)} %all-gather.4.cloned.1.call-done, bf16[1,128,2560]{2,1,0:T(8,128)(2,1)S(1)} %copy-done), kind=kOutput, calls=%fused_computation.16 | convolution fusion | flops 671088640 | bytes 6422528 | tf_op jit(solution)/shard_map/dot_general | solution.py:64
  59.4 74.1 %all-gather.6.cloned.1.call-done = bf16[2560,2560]{1,0:T(8,128)(2,1)} async-done(((bf16[160,2560]{1,0:T(8,128)(2,1)}), bf16[2560,2560]{1,0:T(8,128)(2,1)}) %all-gather.6.cloned.1.call-update) | async-done | bytes 13107216 | tf_op jit(solution)/shard_map/all_gather | solution.py:72
  133.6 0.9 copy.49
  135.7 0.6 and_select_fusion
  137.2 6.7 %fusion.24 = f32[2560,128]{1,0:T(8,128)S(1)} fusion(bf16[2560,2560]{1,0:T(8,128)(2,1)} %all-gather.6.cloned.1.call-done, bf16[1,128,2560]{2,1,0:T(8,128)(2,1)S(1)} %copy-done), kind=kOutput, calls=%fused_computation.22 | convolution fusion | flops 1677721600 | bytes 15073280 | tf_op jit(solution)/shard_map/dot_general | solution.py:74
  144.2 1.5 copy.52
  145.6 1.6 copy.53
  147.3 66.2 %all-gather.8.cloned.1.call-done = bf16[2176,1024]{1,0:T(8,128)(2,1)} async-done(((bf16[136,1024]{1,0:T(8,128)(2,1)}), bf16[2176,1024]{1,0:T(8,128)(2,1)}) %all-gather.8.cloned.1.call-update) | async-done | bytes 4456464 | tf_op jit(solution)/shard_map/all_gather | solution.py:75
  213.6 0.8 slice_convert_fusion.1
  214.3 4.0 %fusion.39 = (bf16[16,128,512]{2,1,0:T(8,128)(2,1)S(1)}, bf16[16,128,512]{2,1,0:T(8,128)(2,1)}) fusion(bf16[16,136,1024]{2,1,0:T(8,128)(2,1)} %bitcast.68), kind=kLoop, calls=%fused_computation.75 | loop fusion | bytes 8388608 | tf_op jit(solution)/shard_map/slice | solution.py:82
  218.3 4.0 %reshape.382 = bf16[2048,4,128]{2,1,0:T(4,128)(2,1)} reshape(bf16[16,128,512]{2,1,0:T(8,128)(2,1)} %get-tuple-element.31) | data formatting | bytes 4194304 | tf_op jit(solution)/shard_map/reshape | solution.py:79
  222.3 2.1 reshape.381
  224.4 1.9 compare_and_fusion
  226.3 11.8 %fusion = (f32[4,5,128]{2,1,0:T(8,128)S(1)}, f32[4,2048,128,5]{2,1,3,0:T(8,128)}) fusion(pred[128,2048]{0,1:T(8,128)(4,1)S(1)} %compare_and_fusion, f32[128,4,5,64]{3,0,2,1:T(8,128)} %bitcast.75, f32[128,4,5,64]{3,0,2,1:T(8,128)} %bitcast.74, f32[128,4,5]{0,2,1:T(8,128)S(1)} %rsqrt.21, bf16[2048,4,128,1]{2,1,0,3:T(4,128)(2,1)} %bitcast.72), kind=kOutput, calls=%fused_computation.1 | convolution fusion | flops 1358886400 | bytes 24662016 | tf_op jit(solution)/shard_map/qhgd,khd->hgqk/dot_general | solution.py:94
  238.2 9.2 %multiply_convert_fusion = bf16[128,4,5,128]{0,3,2,1:T(8,128)(2,1)S(1)} fusion(f32[4,2048,128,5]{2,1,3,0:T(8,128)} %get-tuple-element.39, pred[128,2048]{0,1:T(8,128)(4,1)S(1)} %compare_and_fusion, bf16[2048,4,128,1]{2,1,0,3:T(4,128)(2,1)S(1)} %bitcast.71, f32[128]{0:T(128)S(1)} %get-tuple-element.43, f32[128,4,5]{0,2,1:T(8,128)S(1)} %select_bitcast_fusion), kind=kOutput, calls=%fused_computation.15 | convolution fusion | flops 1358888960 | bytes 23996928 | tf_op jit(solution)/shard_map/hgqk,khd->qhgd/dot_general | solution.py:104
  247.8 5.8 %collective-permute-start = (f32[64]{0:T(128)S(1)}, f32[64]{0:T(128)S(1)}, u32[]{:S(2)}, u32[]{:S(2)}) collective-permute-start(f32[64]{0:T(128)S(1)} %pad_maximum_fusion.2), channel_id=1, source_target_pairs={{0,1},{1,0},{2,3},{3,2},{4,5},{5,4},{6,7},{7,6},{8,9},{9,8},{10,11... | collective-permute-start | bytes 776 | tf_op jit(solution)/shard_map/ppermute | solution.py:124
  253.5 1.5 collective-permute-done
  255.2 3.2 %collective-permute-start.1 = (f32[64]{0:T(128)S(1)}, f32[64]{0:T(128)S(1)}, u32[]{:S(2)}, u32[]{:S(2)}) collective-permute-start(f32[64]{0:T(128)S(1)} %fusion.44), channel_id=1, source_target_pairs={{0,2},{1,3},{2,0},{3,1},{4,6},{5,7},{6,4},{7,5},{8,10},{9,11},{10,... | collective-permute-start | bytes 776 | tf_op jit(solution)/shard_map/ppermute | solution.py:124
  258.4 4.3 %collective-permute-done.1 = f32[64]{0:T(128)S(1)} collective-permute-done((f32[64]{0:T(128)S(1)}, f32[64]{0:T(128)S(1)}, u32[]{:S(2)}, u32[]{:S(2)}) %collective-permute-start.1) | collective-permute-done | bytes 288 | tf_op jit(solution)/shard_map/ppermute | solution.py:124
  263.2 3.0 %collective-permute-done.2 = f32[64]{0:T(128)S(1)} collective-permute-done((f32[64]{0:T(128)S(1)}, f32[64]{0:T(128)S(1)}, u32[]{:S(2)}, u32[]{:S(2)}) %collective-permute-start.2) | collective-permute-done | bytes 288 | tf_op jit(solution)/shard_map/ppermute | solution.py:124
  266.2 2.1 collective-permute-start.3
  268.3 1.1 copy.56
  269.4 1.9 collective-permute-done.3
  271.3 0.6 fusion.33
  (48 shorter events, 3.6 us)
Async XLA Ops:
  7.2 48.0 %copy-start = (bf16[1,128,2560]{2,1,0:T(8,128)(2,1)S(1)}, bf16[1,128,2560]{2,1,0:T(8,128)(2,1)}, u32[]{:S(2)}) copy-start(bf16[1,128,2560]{2,1,0:T(8,128)(2,1)} %param.11) | copy-start | bytes 1966084
  7.2 48.0 %all-gather.4.cloned.1.call-start = ((), (), s32[]{:S(2)}) async-start(), calls=%async_computation | async-start | bytes 5570560 | tf_op jit(solution)/shard_map/all_gather | solution.py:61
  9.1 124.5 %all-gather.6.cloned.1.call-start = ((), (), s32[]{:S(2)}) async-start(), calls=%async_computation.1 | async-start | bytes 13926400 | tf_op jit(solution)/shard_map/all_gather | solution.py:72
  9.8 203.8 %all-gather.8.cloned.1.call-start = ((), (), s32[]{:S(2)}) async-start(), calls=%async_computation.2 | async-start | bytes 4734976 | tf_op jit(solution)/shard_map/all_gather | solution.py:75
  59.2 75.3 %copy-start.3 = (s32[1,16]{1,0:T(1,128)S(1)}, s32[1,16]{1,0:T(1,128)}, u32[]{:S(2)}) copy-start(s32[1,16]{1,0:T(1,128)} %param.12) | copy-start | bytes 196
  59.2 76.5 %copy-start.2 = (bf16[2560]{0:T(1024)(128)(2,1)S(1)}, bf16[2560]{0:T(1024)(128)(2,1)}, u32[]{:S(2)}) copy-start(bf16[2560]{0:T(1024)(128)(2,1)} %param.19) | copy-start | bytes 15364
  222.3 2.1 copy-start.4
  226.3 11.8 %copy-start.1 = (bf16[2048,4,128]{2,1,0:T(4,128)(2,1)S(1)}, bf16[2048,4,128]{2,1,0:T(4,128)(2,1)}, u32[]{:S(2)}) copy-start(bf16[2048,4,128]{2,1,0:T(4,128)(2,1)} %reshape.381) | copy-start | bytes 6291460
  238.1 9.4 %copy-start.5 = (s32[1,128]{1,0:T(1,128)S(1)}, s32[1,128]{1,0:T(1,128)}, u32[]{:S(2)}) copy-start(s32[1,128]{1,0:T(1,128)} %param.15) | copy-start | bytes 1540
  247.8 7.3 %collective-permute-start = (f32[64]{0:T(128)S(1)}, f32[64]{0:T(128)S(1)}, u32[]{:S(2)}, u32[]{:S(2)}) collective-permute-start(f32[64]{0:T(128)S(1)} %pad_maximum_fusion.2), channel_id=1, source_target_pairs={{0,1},{1,0},{2,3},{3,2},{4,5},{5,4},{6,7},{7,6},{8,9},{9,8},{10,11... | collective-permute-start | bytes 776 | tf_op jit(solution)/shard_map/ppermute | solution.py:124
  255.2 7.5 %collective-permute-start.1 = (f32[64]{0:T(128)S(1)}, f32[64]{0:T(128)S(1)}, u32[]{:S(2)}, u32[]{:S(2)}) collective-permute-start(f32[64]{0:T(128)S(1)} %fusion.44), channel_id=1, source_target_pairs={{0,2},{1,3},{2,0},{3,1},{4,6},{5,7},{6,4},{7,5},{8,10},{9,11},{10,... | collective-permute-start | bytes 776 | tf_op jit(solution)/shard_map/ppermute | solution.py:124
  262.7 3.6 %collective-permute-start.2 = (f32[64]{0:T(128)S(1)}, f32[64]{0:T(128)S(1)}, u32[]{:S(2)}, u32[]{:S(2)}) collective-permute-start(f32[64]{0:T(128)S(1)} %add.146), channel_id=1, source_target_pairs={{0,4},{1,5},{2,6},{3,7},{4,0},{5,1},{6,2},{7,3},{8,12},{9,13},{10,... | collective-permute-start | bytes 776 | tf_op jit(solution)/shard_map/ppermute | solution.py:124
  266.2 5.1 %collective-permute-start.3 = (f32[64]{0:T(128)S(1)}, f32[64]{0:T(128)S(1)}, u32[]{:S(2)}, u32[]{:S(2)}) collective-permute-start(f32[64]{0:T(128)S(1)} %add.147), channel_id=1, source_target_pairs={{0,8},{1,9},{2,10},{3,11},{4,12},{5,13},{6,14},{7,15},{8,0},{9,1},... | collective-permute-start | bytes 776 | tf_op jit(solution)/shard_map/ppermute | solution.py:124
Sparse Core Ops, SparseCore 0:
  10.4 44.6 all-gather.3
  57.0 76.5 all-gather.5
  136.6 76.8 all-gather.7

commit v5 on v3

--- a/solution.py
+++ b/solution.py
@@ -3,7 +3,7 @@
 import jax
 import jax.numpy as jnp
 from jax import lax
-from jax.sharding import PartitionSpec as P
+from jax.sharding import Mesh, PartitionSpec as P
 
 QUERY_HEADS = 20
 KEY_VALUE_HEADS = 4
@@ -33,7 +33,7 @@
     return (turned * scale).astype(jnp.bfloat16).reshape(token_count, heads * HEAD_SIZE)
 
 
-def make_per_device(shards):
+def make_per_device(shards, inner):
     def per_device(
         tokens,
         shard_counts,
@@ -48,7 +48,7 @@
         inputs = tokens[0]
         token_slots = inputs.shape[0]
         kv_width = KEY_VALUE_HEADS * HEAD_SIZE
-        mine = lax.axis_index("ctx")
+        mine = lax.axis_index("cx") * inner + lax.axis_index("cz")
         counts = shard_counts[0]
         starts = jnp.cumsum(counts) - counts
         offsets = jnp.arange(token_slots, dtype=jnp.int32)
@@ -72,7 +72,8 @@
         query_weights = lax.all_gather(query_weight, "dp", axis=0, tiled=True)
         own_block, query_weights = lax.optimization_barrier((own_block, query_weights))
         query = jnp.dot(inputs, query_weights, preferred_element_type=jnp.float32)
-        gathered = lax.all_gather(own_block, "ctx", axis=0, tiled=True).reshape(
+        gathered = lax.all_gather(own_block, "cz", axis=0, tiled=True)
+        gathered = lax.all_gather(gathered, "cx", axis=0, tiled=True).reshape(
             shards, token_slots + 8, 2 * kv_width
         )
         key_count = shards * token_slots
@@ -117,28 +118,40 @@
         onehot = span_ids[0][:, None] == jnp.arange(CAND, dtype=jnp.int32)[None, :]
         sums = jnp.sum(jnp.where(onehot, loglik[:, None], 0.0), axis=0)
         tally = jnp.sum(onehot.astype(jnp.float32), axis=0)
-        sums, tally = lax.psum((sums, tally), "ctx")
-        return (attention[None], (sums / tally)[None])
+        total = jnp.concatenate([sums, tally])
+        for axis, size in (("cz", inner), ("cx", shards // inner)):
+            bit = 1
+            while bit < size:
+                pairs = [(s, s ^ bit) for s in range(size)]
+                total = total + lax.ppermute(total, axis, pairs)
+                bit *= 2
+        return (attention[None], (total[:CAND] / total[CAND:])[None])
 
     return per_device
 
 
 def solution(mesh):
+    shards = mesh.shape["ctx"]
+    inner = 4 if shards % 4 == 0 else 1
+    split = Mesh(
+        mesh.devices.reshape(mesh.shape["dp"], shards // inner, inner), ("dp", "cx", "cz")
+    )
+    ctx = ("cx", "cz")
     placed = (
-        P("dp", "ctx", None),
+        P("dp", ctx, None),
         P("dp", None),
         P("dp"),
-        P("dp", "ctx"),
-        P("dp", "ctx"),
+        P("dp", ctx),
+        P("dp", ctx),
         P("dp", None),
         P("dp", None),
         P("dp", None),
         P(),
     )
     return jax.shard_map(
-        make_per_device(mesh.shape["ctx"]),
-        mesh=mesh,
+        make_per_device(shards, inner),
+        mesh=split,
         in_specs=placed,
-        out_specs=(P("dp", "ctx", None), P("dp", None)),
+        out_specs=(P("dp", ctx, None), P("dp", None)),
         check_vma=False,
     )

time: 303 us -> 288 us (0.950); the launches traced: 297 us -> 287 us
  blocking collectives: 41.6 us -> 0 us
  waiting for transfers between devices: 182 us -> 203 us
  starting transfers between devices: 0.12 us -> 10.6 us
    psum x1 -> x0, blocking collectives: 41.6 us -> none  [per_device(): sums, tally = lax.psum((sums, tally), 'ctx')]
    all_gather x1 -> x2, waiting for transfers between devices: 66.1 us -> 77.5 us  [the longest x1 39 us: per_device(): lax.all_gather(gathered, 'cx', axis=0, tiled=True)]
    ppermute x0 -> x4, starting transfers between devices: none -> 10.4 us  [per_device(): total = total + lax.ppermute(total, axis, pairs)]
    ppermute x0 -> x4, waiting for transfers between devices: none -> 9.13 us  [per_device(): total = total + lax.ppermute(total, axis, pairs)]
  transfers between devices with their start and end apart: 3 -> 8, of which waited for: 3 -> 8; matrix products, arithmetic and copies ran while one was open for 7% -> 7% of each run, Pallas kernels for 0% -> 0%
where the time goes in v5:
time: 288 us; the launch traced here: 287 us
  waiting for transfers between devices  203 us (70%)
  matrix products  32 us (11%)
  local copies, waits for them, and re-layouts  17.2 us (6%)
  between operations  14.7 us (5%)
  starting transfers between devices  10.6 us (4%)
  other arithmetic  9.51 us (3%)
    all_gather x1, waiting for transfers between devices, per_device(): query_weights = lax.all_gather(query_weight, 'dp', axis=0, tiled=True)  74.1 us
    all_gather x1, waiting for transfers between devices, per_device(): lax.all_gather(jnp.concatenate([key_matrix, value_matrix], axis=1), 'dp',...  41.6 us
    all_gather x1, waiting for transfers between devices, per_device(): lax.all_gather(gathered, 'cx', axis=0, tiled=True)  39 us
    all_gather x1, waiting for transfers between devices, per_device(): gathered = lax.all_gather(own_block, 'cz', axis=0, tiled=True)  38.5 us
    dot_general x1, matrix products, per_device(): jnp.einsum('qhgd,khd->hgqk', per_head_queries, key_portion, preferred_ele...  11.8 us
    ppermute x4, starting transfers between devices, per_device(): total = total + lax.ppermute(total, axis, pairs)  10.4 us
    dot_general x1, matrix products, per_device(): jnp.einsum('hgqk,khd->qhgd', weights.astype(jnp.bfloat16), value_portion,...  9.2 us
    ppermute x4, waiting for transfers between devices, per_device(): total = total + lax.ppermute(total, axis, pairs)  9.13 us
  transfers between devices with their start and end apart: 8, of which 8 were waited for; matrix products, arithmetic and copies ran while one was open for 7% of the time, Pallas kernels for 0%

profile of v5, /device:TPU:2, one launch (start us, length us, event | category | flops | bytes accessed | tf_op | source)
XLA Modules:
  0.0 286.9 jit_solution(175157654301643475)
XLA Ops:
  7.2 1.8 pad_maximum_fusion
  9.1 0.7 all-gather.7.cloned.1.call-update
  9.9 0.7 copy.47
  10.8 0.7 convert_element_type.67
  11.5 0.7 bitcast_subtract_fusion
  13.6 41.6 %all-gather.5.cloned.1.call-done = bf16[2560,1024]{1,0:T(8,128)(2,1)} async-done(((bf16[160,1024]{1,0:T(8,128)(2,1)}), bf16[2560,1024]{1,0:T(8,128)(2,1)}) %all-gather.5.cloned.1.call-update) | async-done | bytes 5242896 | tf_op jit(solution)/shard_map/all_gather | solution.py:61
  55.1 4.0 %convolution_bitcast_fusion = f32[128,1024]{0,1:T(8,128)S(1)} fusion(bf16[2560,1024]{1,0:T(8,128)(2,1)} %all-gather.5.cloned.1.call-done, bf16[1,128,2560]{2,1,0:T(8,128)(2,1)S(1)} %copy-done), kind=kOutput, calls=%fused_computation.16 | convolution fusion | flops 671088640 | bytes 6422528 | tf_op jit(solution)/shard_map/dot_general | solution.py:64
  59.4 74.1 %all-gather.7.cloned.1.call-done = bf16[2560,2560]{1,0:T(8,128)(2,1)} async-done(((bf16[160,2560]{1,0:T(8,128)(2,1)}), bf16[2560,2560]{1,0:T(8,128)(2,1)}) %all-gather.7.cloned.1.call-update) | async-done | bytes 13107216 | tf_op jit(solution)/shard_map/all_gather | solution.py:72
  133.6 0.9 copy.49
  134.5 38.5 %all-gather.9.cloned.1.call-done = bf16[544,1024]{1,0:T(8,128)(2,1)} async-done(((bf16[136,1024]{1,0:T(8,128)(2,1)}), bf16[544,1024]{1,0:T(8,128)(2,1)}) %all-gather.9.cloned.1.call-update) | async-done | bytes 1114128 | tf_op jit(solution)/shard_map/all_gather | solution.py:75
  174.9 0.7 iota_compare_fusion.3
  175.8 6.7 %fusion.24 = f32[2560,128]{1,0:T(8,128)S(1)} fusion(bf16[2560,2560]{1,0:T(8,128)(2,1)} %all-gather.7.cloned.1.call-done, bf16[1,128,2560]{2,1,0:T(8,128)(2,1)S(1)} %copy-done), kind=kOutput, calls=%fused_computation.22 | convolution fusion | flops 1677721600 | bytes 15073280 | tf_op jit(solution)/shard_map/dot_general | solution.py:74
  182.8 1.5 copy.52
  184.2 1.6 copy.53
  185.9 39.0 %all-gather.11.cloned.1.call-done = bf16[2176,1024]{1,0:T(8,128)(2,1)} async-done(((bf16[544,1024]{1,0:T(8,128)(2,1)}), bf16[2176,1024]{1,0:T(8,128)(2,1)}) %all-gather.11.cloned.1.call-update) | async-done | bytes 4456464 | tf_op jit(solution)/shard_map/all_gather | solution.py:76
  224.9 4.0 %fusion.39 = (bf16[16,128,512]{2,1,0:T(8,128)(2,1)S(1)}, bf16[16,128,512]{2,1,0:T(8,128)(2,1)}) fusion(bf16[16,136,1024]{2,1,0:T(8,128)(2,1)} %bitcast.67), kind=kLoop, calls=%fused_computation.75 | loop fusion | bytes 8388608 | tf_op jit(solution)/shard_map/slice | solution.py:83
  228.9 0.8 slice_convert_fusion.1
  229.7 4.0 %reshape.382 = bf16[2048,4,128]{2,1,0:T(4,128)(2,1)} reshape(bf16[16,128,512]{2,1,0:T(8,128)(2,1)} %get-tuple-element.31) | data formatting | bytes 4194304 | tf_op jit(solution)/shard_map/reshape | solution.py:80
  233.6 2.1 reshape.381
  235.7 1.9 compare_and_fusion
  237.6 11.8 %fusion = (f32[4,5,128]{2,1,0:T(8,128)S(1)}, f32[4,2048,128,5]{2,1,3,0:T(8,128)}) fusion(pred[128,2048]{0,1:T(8,128)(4,1)S(1)} %compare_and_fusion, f32[128,4,5,64]{3,0,2,1:T(8,128)} %bitcast.75, f32[128,4,5,64]{3,0,2,1:T(8,128)} %bitcast.74, f32[128,4,5]{0,2,1:T(8,128)S(1)} %rsqrt.21, bf16[2048,4,128,1]{2,1,0,3:T(4,128)(2,1)} %bitcast.72), kind=kOutput, calls=%fused_computation.1 | convolution fusion | flops 1358886400 | bytes 24662016 | tf_op jit(solution)/shard_map/qhgd,khd->hgqk/dot_general | solution.py:95
  249.5 9.2 %multiply_convert_fusion = bf16[128,4,5,128]{0,3,2,1:T(8,128)(2,1)S(1)} fusion(f32[4,2048,128,5]{2,1,3,0:T(8,128)} %get-tuple-element.39, pred[128,2048]{0,1:T(8,128)(4,1)S(1)} %compare_and_fusion, bf16[2048,4,128,1]{2,1,0,3:T(4,128)(2,1)S(1)} %bitcast.71, f32[128]{0:T(128)S(1)} %get-tuple-element.43, f32[128,4,5]{0,2,1:T(8,128)S(1)} %select_bitcast_fusion), kind=kOutput, calls=%fused_computation.15 | convolution fusion | flops 1358888960 | bytes 23996928 | tf_op jit(solution)/shard_map/hgqk,khd->qhgd/dot_general | solution.py:105
  259.1 2.6 collective-permute-start
  261.7 1.9 collective-permute-done
  263.7 5.8 %collective-permute-start.1 = (f32[64]{0:T(128)S(1)}, f32[64]{0:T(128)S(1)}, u32[]{:S(2)}, u32[]{:S(2)}) collective-permute-start(f32[64]{0:T(128)S(1)} %fusion.44), channel_id=1, source_target_pairs={{0,2},{1,3},{2,0},{3,1},{4,6},{5,7},{6,4},{7,5},{8,10},{9,11},{10,... | collective-permute-start | bytes 776 | tf_op jit(solution)/shard_map/ppermute | solution.py:126
  269.4 1.7 collective-permute-done.1
  271.2 1.1 collective-permute-start.2
  272.3 2.4 collective-permute-done.2
  274.7 1.0 collective-permute-start.3
  275.7 1.1 copy.56
  276.8 3.0 %collective-permute-done.3 = f32[64]{0:T(128)S(1)} collective-permute-done((f32[64]{0:T(128)S(1)}, f32[64]{0:T(128)S(1)}, u32[]{:S(2)}, u32[]{:S(2)}) %collective-permute-start.3) | collective-permute-done | bytes 288 | tf_op jit(solution)/shard_map/ppermute | solution.py:126
  279.8 0.6 fusion.33
  (51 shorter events, 4.3 us)
Async XLA Ops:
  7.2 48.0 %copy-start = (bf16[1,128,2560]{2,1,0:T(8,128)(2,1)S(1)}, bf16[1,128,2560]{2,1,0:T(8,128)(2,1)}, u32[]{:S(2)}) copy-start(bf16[1,128,2560]{2,1,0:T(8,128)(2,1)} %param.11) | copy-start | bytes 1966084
  7.2 48.0 %all-gather.5.cloned.1.call-start = ((), (), s32[]{:S(2)}) async-start(), calls=%async_computation | async-start | bytes 5570560 | tf_op jit(solution)/shard_map/all_gather | solution.py:61
  9.1 124.5 %all-gather.7.cloned.1.call-start = ((), (), s32[]{:S(2)}) async-start(), calls=%async_computation.1 | async-start | bytes 13926400 | tf_op jit(solution)/shard_map/all_gather | solution.py:72
  9.8 163.2 %all-gather.9.cloned.1.call-start = ((), (), s32[]{:S(2)}) async-start(), calls=%async_computation.2 | async-start | bytes 1392640 | tf_op jit(solution)/shard_map/all_gather | solution.py:75
  59.2 113.8 %copy-start.3 = (s32[1,16]{1,0:T(1,128)S(1)}, s32[1,16]{1,0:T(1,128)}, u32[]{:S(2)}) copy-start(s32[1,16]{1,0:T(1,128)} %param.12) | copy-start | bytes 196
  59.2 115.1 %copy-start.2 = (bf16[2560]{0:T(1024)(128)(2,1)S(1)}, bf16[2560]{0:T(1024)(128)(2,1)}, u32[]{:S(2)}) copy-start(bf16[2560]{0:T(1024)(128)(2,1)} %param.19) | copy-start | bytes 15364
  134.5 90.4 %all-gather.11.cloned.1.call-start = ((), (), s32[]{:S(2)}) async-start(), calls=%async_computation.3 | async-start | bytes 5570560 | tf_op jit(solution)/shard_map/all_gather | solution.py:76
  233.6 2.1 copy-start.4
  237.6 11.9 %copy-start.1 = (bf16[2048,4,128]{2,1,0:T(4,128)(2,1)S(1)}, bf16[2048,4,128]{2,1,0:T(4,128)(2,1)}, u32[]{:S(2)}) copy-start(bf16[2048,4,128]{2,1,0:T(4,128)(2,1)} %reshape.381) | copy-start | bytes 6291460
  249.5 9.4 %copy-start.5 = (s32[1,128]{1,0:T(1,128)S(1)}, s32[1,128]{1,0:T(1,128)}, u32[]{:S(2)}) copy-start(s32[1,128]{1,0:T(1,128)} %param.15) | copy-start | bytes 1540
  259.1 4.5 %collective-permute-start = (f32[64]{0:T(128)S(1)}, f32[64]{0:T(128)S(1)}, u32[]{:S(2)}, u32[]{:S(2)}) collective-permute-start(f32[64]{0:T(128)S(1)} %pad_maximum_fusion.2), channel_id=1, source_target_pairs={{0,1},{1,0},{2,3},{3,2},{4,5},{5,4},{6,7},{7,6},{8,9},{9,8},{10,11... | collective-permute-start | bytes 776 | tf_op jit(solution)/shard_map/ppermute | solution.py:126
  263.7 7.5 %collective-permute-start.1 = (f32[64]{0:T(128)S(1)}, f32[64]{0:T(128)S(1)}, u32[]{:S(2)}, u32[]{:S(2)}) collective-permute-start(f32[64]{0:T(128)S(1)} %fusion.44), channel_id=1, source_target_pairs={{0,2},{1,3},{2,0},{3,1},{4,6},{5,7},{6,4},{7,5},{8,10},{9,11},{10,... | collective-permute-start | bytes 776 | tf_op jit(solution)/shard_map/ppermute | solution.py:126
  271.2 3.6 %collective-permute-start.2 = (f32[64]{0:T(128)S(1)}, f32[64]{0:T(128)S(1)}, u32[]{:S(2)}, u32[]{:S(2)}) collective-permute-start(f32[64]{0:T(128)S(1)} %add.150), channel_id=1, source_target_pairs={{0,4},{4,0},{8,12},{12,8},{1,5},{5,1},{9,13},{13,9},{2,6},{6,2},{1... | collective-permute-start | bytes 776 | tf_op jit(solution)/shard_map/ppermute | solution.py:126
  274.7 5.1 %collective-permute-start.3 = (f32[64]{0:T(128)S(1)}, f32[64]{0:T(128)S(1)}, u32[]{:S(2)}, u32[]{:S(2)}) collective-permute-start(f32[64]{0:T(128)S(1)} %add.151), channel_id=1, source_target_pairs={{0,8},{4,12},{8,0},{12,4},{1,9},{5,13},{9,1},{13,5},{2,10},{6,14},... | collective-permute-start | bytes 776 | tf_op jit(solution)/shard_map/ppermute | solution.py:126
Sparse Core Ops, SparseCore 0:
  10.4 44.6 all-gather.4
  57.0 76.5 all-gather.6
  136.0 37.0 all-gather.8
  174.7 50.1 all-gather.10

commit v6 on v5

--- a/solution.py
+++ b/solution.py
@@ -58,22 +58,40 @@
         qseg = segment_ids[0]
         qchunk = (token_places + STRETCH - cstart) // STRETCH
 
-        kv_weights = lax.all_gather(
-            jnp.concatenate([key_matrix, value_matrix], axis=1), "dp", axis=0, tiled=True
+        q_width = QUERY_HEADS * HEAD_SIZE
+        core = lax.axis_index("dc")
+        swap = [(0, 1), (1, 0)]
+        weights_local = jnp.concatenate([query_weight, key_matrix, value_matrix], axis=1)
+        half = weights_local.shape[1] // 2
+        chunk = weights_local.shape[0]
+        mine_half = lax.dynamic_slice_in_dim(weights_local, core * half, half, axis=1)
+        other_half = lax.dynamic_slice_in_dim(weights_local, (1 - core) * half, half, axis=1)
+        partner_rows = lax.ppermute(other_half, "dc", swap)
+        partner_tokens = lax.ppermute(inputs, "dc", swap)
+        rows_block = jnp.concatenate([mine_half, partner_rows], axis=0)
+        half_weights = lax.all_gather(rows_block, ("dz", "dy"), axis=0, tiled=True)
+        both = jnp.concatenate([inputs, partner_tokens], axis=0)
+        features = both.shape[1]
+        paired = both.reshape(2 * token_slots, features // (2 * chunk), 2, chunk)
+        paired = jnp.where(core == 0, paired, paired[:, :, ::-1, :])
+        both = paired.reshape(2 * token_slots, features)
+        projected = jnp.dot(both, half_weights, preferred_element_type=jnp.float32)
+        returned = lax.ppermute(projected[token_slots:], "dc", swap)
+        own_part = projected[:token_slots]
+        full = jnp.where(
+            core == 0,
+            jnp.concatenate([own_part, returned], axis=1),
+            jnp.concatenate([returned, own_part], axis=1),
         )
-        kv_rows = jnp.dot(inputs, kv_weights, preferred_element_type=jnp.float32)
-        key_norm = rotary_then_norm(kv_rows[:, :kv_width], token_places, KEY_VALUE_HEADS)
-        value_rows = kv_rows[:, kv_width:].astype(jnp.bfloat16)
+        query = full[:, :q_width]
+        key_norm = rotary_then_norm(full[:, q_width : q_width + kv_width], token_places, KEY_VALUE_HEADS)
+        value_rows = full[:, q_width + kv_width :].astype(jnp.bfloat16)
         seg_row = jnp.zeros((8, 2 * kv_width), jnp.bfloat16)
         seg_row = seg_row.at[0, :token_slots].set(qseg.astype(jnp.bfloat16))
         own_block = jnp.concatenate(
             [jnp.concatenate([key_norm, value_rows], axis=1), seg_row], axis=0
         )
-        query_weights = lax.all_gather(query_weight, "dp", axis=0, tiled=True)
-        own_block, query_weights = lax.optimization_barrier((own_block, query_weights))
-        query = jnp.dot(inputs, query_weights, preferred_element_type=jnp.float32)
-        gathered = lax.all_gather(own_block, "cz", axis=0, tiled=True)
-        gathered = lax.all_gather(gathered, "cx", axis=0, tiled=True).reshape(
+        gathered = lax.all_gather(own_block, ("cx", "cz"), axis=0, tiled=True).reshape(
             shards, token_slots + 8, 2 * kv_width
         )
         key_count = shards * token_slots
@@ -132,26 +150,28 @@
 
 def solution(mesh):
     shards = mesh.shape["ctx"]
-    inner = 4 if shards % 4 == 0 else 1
+    inner = 4
     split = Mesh(
-        mesh.devices.reshape(mesh.shape["dp"], shards // inner, inner), ("dp", "cx", "cz")
+        mesh.devices.reshape(2, mesh.shape["dp"] // 4, 2, shards // inner, inner),
+        ("dz", "dy", "dc", "cx", "cz"),
     )
+    dp = ("dz", "dy", "dc")
     ctx = ("cx", "cz")
     placed = (
-        P("dp", ctx, None),
-        P("dp", None),
-        P("dp"),
-        P("dp", ctx),
-        P("dp", ctx),
-        P("dp", None),
-        P("dp", None),
-        P("dp", None),
+        P(dp, ctx, None),
+        P(dp, None),
+        P(dp),
+        P(dp, ctx),
+        P(dp, ctx),
+        P(dp, None),
+        P(dp, None),
+        P(dp, None),
         P(),
     )
     return jax.shard_map(
         make_per_device(shards, inner),
         mesh=split,
         in_specs=placed,
-        out_specs=(P("dp", ctx, None), P("dp", None)),
+        out_specs=(P(dp, ctx, None), P(dp, None)),
         check_vma=False,
     )

time: 288 us -> 275 us (0.955)
  waiting for transfers between devices: 203 us -> 183 us
  local copies, waits for them, and re-layouts: 17.2 us -> 25.1 us
  matrix products: 32 us -> 27.6 us
    all_gather x4 -> x2, waiting for transfers between devices: 193 us -> 168 us  [the longest x1 102 us: per_device(): half_weights = lax.all_gather(rows_block, ('dz', 'dy'), axis=0, tiled=True)]
    dot_general x2 -> x1, matrix products: 10.7 us -> 6.17 us  [per_device(): projected = jnp.dot(both, half_weights, preferred_element_type=jnp.float32)]
    ppermute x0 -> x3, waiting for transfers between devices: none -> 4.25 us  [the longest x1 1.97 us: per_device(): partner_rows = lax.ppermute(other_half, 'dc', swap)]
    unnamed x15 -> x20, local copies, waits for them, and re-layouts: 1.27 us -> 4.78 us
    concatenate x0 -> x3, local copies, waits for them, and re-layouts: none -> 3.06 us  [the longest x2 3.05 us: rotary_then_norm(): jnp.concatenate([leading_block * cosine - second * sine, second * cosine...]
    slice x2 -> x5, local copies, waits for them, and re-layouts: 0.03 us -> 3.06 us  [the longest x2 2.9 us: per_device(): query = full[:, :q_width]]
  transfers between devices with their start and end apart: 8 -> 9, of which waited for: 8 -> 9; matrix products, arithmetic and copies ran while one was open for 7% -> 4% of each run, Pallas kernels for 0% -> 0%
where the time goes in v6:
time: 275 us; the launch traced here: 274 us
  waiting for transfers between devices  183 us (67%)
  matrix products  27.6 us (10%)
  local copies, waits for them, and re-layouts  25.1 us (9%)
  between operations  15.1 us (5%)
  starting transfers between devices  12.3 us (4%)
  other arithmetic  11.3 us (4%)
    all_gather x1, waiting for transfers between devices, per_device(): half_weights = lax.all_gather(rows_block, ('dz', 'dy'), axis=0, tiled=True)  102 us
    all_gather x1, waiting for transfers between devices, per_device(): lax.all_gather(own_block, ('cx', 'cz'), axis=0, tiled=True)  65.8 us
    dot_general x1, matrix products, per_device(): jnp.einsum('qhgd,khd->hgqk', per_head_queries, key_portion, preferred_ele...  12 us
    ppermute x4, starting transfers between devices, per_device(): total = total + lax.ppermute(total, axis, pairs)  11.6 us
    ppermute x4, waiting for transfers between devices, per_device(): total = total + lax.ppermute(total, axis, pairs)  10.8 us
    dot_general x1, matrix products, per_device(): jnp.einsum('hgqk,khd->qhgd', weights.astype(jnp.bfloat16), value_portion,...  9.2 us
    dot_general x1, matrix products, per_device(): projected = jnp.dot(both, half_weights, preferred_element_type=jnp.float32)  6.17 us
  transfers between devices with their start and end apart: 9, of which 9 were waited for; matrix products, arithmetic and copies ran while one was open for 4% of the time, Pallas kernels for 0%

profile of v6, /device:TPU:2, one launch (start us, length us, event | category | flops | bytes accessed | tf_op | source)
XLA Modules:
  0.0 274.1 jit_solution(2822438134202464601)
XLA Ops:
  7.2 1.2 constant_dynamic-update-slice_fusion.2
  8.5 0.9 constant_dynamic-update-slice_fusion.1
  9.6 2.0 collective-permute-done.1
  11.6 1.1 pad_maximum_fusion.1
  13.3 2.0 collective-permute-done
  15.7 101.9 %all-gather.3.cloned.1.call-done = bf16[2560,1792]{1,0:T(8,128)(2,1)} async-done(((bf16[320,1792]{1,0:T(8,128)(2,1)}), bf16[2560,1792]{1,0:T(8,128)(2,1)}) %all-gather.3.cloned.1.call-update) | async-done | bytes 9175056 | tf_op jit(solution)/shard_map/all_gather | solution.py:72
  117.7 6.2 %fusion.38 = f32[256,1792]{1,0:T(8,128)S(1)} fusion(bf16[256,2560]{0,1:T(8,128)(2,1)S(1)} %bitcast.70, bf16[2560,1792]{1,0:T(8,128)(2,1)} %all-gather.3.cloned.1.call-done), kind=kOutput, calls=%fused_computation.82 | convolution fusion | flops 2348810240 | bytes 12320768 | tf_op jit(solution)/shard_map/dot_general | solution.py:78
  126.7 0.9 copy-done
  127.7 1.6 maximum_select_fusion
  130.6 0.7 fusion.25
  131.3 0.6 constant_dynamic-slice_fusion
  134.2 1.2 slice.82
  135.3 1.7 copy.66
  137.5 1.6 copy.67
  139.0 1.5 copy.68
  140.5 65.8 %all-gather.5.cloned.1.call-done = bf16[2176,1024]{1,0:T(8,128)(2,1)} async-done(((bf16[136,1024]{1,0:T(8,128)(2,1)}), bf16[2176,1024]{1,0:T(8,128)(2,1)}) %all-gather.5.cloned.1.call-update) | async-done | bytes 4456464 | tf_op jit(solution)/shard_map/all_gather | solution.py:94
  206.3 4.7 %fusion.36 = (bf16[16,128,512]{2,1,0:T(8,128)(2,1)}, bf16[16,128,512]{2,1,0:T(8,128)(2,1)}) fusion(bf16[16,136,1024]{2,1,0:T(8,128)(2,1)} %bitcast.74), kind=kLoop, calls=%fused_computation.80 | loop fusion | bytes 8388608 | tf_op jit(solution)/shard_map/slice | solution.py:101
  211.0 0.8 slice_convert_fusion.1
  211.8 2.5 reshape.391
  214.3 2.7 copy.81
  217.0 2.5 reshape.389
  219.6 1.9 compare_and_fusion
  221.5 12.0 %fusion = (f32[4,5,128]{2,1,0:T(8,128)S(1)}, f32[4,2048,128,5]{2,1,3,0:T(8,128)}) fusion(pred[128,2048]{0,1:T(8,128)(4,1)S(1)} %compare_and_fusion, f32[128,4,5,64]{3,0,2,1:T(8,128)} %copy.68, f32[128,4,5,64]{3,0,2,1:T(8,128)} %copy.67, f32[128,4,5]{0,2,1:T(8,128)S(1)} %rsqrt.21, bf16[2048,4,128]{0,2,1:T(8,128)(2,1)} %copy.81), kind=kOutput, calls=%fused_computation.1 | convolution fusion | flops 1358886400 | bytes 24662016 | tf_op jit(solution)/shard_map/qhgd,khd->hgqk/dot_general | solution.py:113
  233.5 9.2 %multiply_convert_fusion = bf16[128,4,5,128]{0,3,2,1:T(8,128)(2,1)S(1)} fusion(f32[4,2048,128,5]{2,1,3,0:T(8,128)} %get-tuple-element.39, pred[128,2048]{0,1:T(8,128)(4,1)S(1)} %compare_and_fusion, bf16[2048,4,128,1]{2,1,0,3:T(4,128)(2,1)S(1)} %bitcast.80, f32[128]{0:T(128)S(1)} %get-tuple-element.43, f32[128,4,5]{0,2,1:T(8,128)S(1)} %select_bitcast_fusion), kind=kOutput, calls=%fused_computation.18 | convolution fusion | flops 1358888960 | bytes 23996928 | tf_op jit(solution)/shard_map/hgqk,khd->qhgd/dot_general | solution.py:123
  243.2 5.8 %collective-permute-start.3 = (f32[64]{0:T(128)S(1)}, f32[64]{0:T(128)S(1)}, u32[]{:S(2)}, u32[]{:S(2)}) collective-permute-start(f32[64]{0:T(128)S(1)} %pad_maximum_fusion.3), channel_id=1, source_target_pairs={{0,1},{1,0},{2,3},{3,2},{4,5},{5,4},{6,7},{7,6},{8,9},{9,8},{10,11... | collective-permute-start | bytes 776 | tf_op jit(solution)/shard_map/ppermute | solution.py:144
  248.9 1.5 collective-permute-done.3
  250.6 3.2 %collective-permute-start.4 = (f32[64]{0:T(128)S(1)}, f32[64]{0:T(128)S(1)}, u32[]{:S(2)}, u32[]{:S(2)}) collective-permute-start(f32[64]{0:T(128)S(1)} %fusion.43), channel_id=1, source_target_pairs={{0,2},{1,3},{2,0},{3,1},{4,6},{5,7},{6,4},{7,5},{8,10},{9,11},{10,... | collective-permute-start | bytes 776 | tf_op jit(solution)/shard_map/ppermute | solution.py:144
  253.8 4.3 %collective-permute-done.4 = f32[64]{0:T(128)S(1)} collective-permute-done((f32[64]{0:T(128)S(1)}, f32[64]{0:T(128)S(1)}, u32[]{:S(2)}, u32[]{:S(2)}) %collective-permute-start.4) | collective-permute-done | bytes 288 | tf_op jit(solution)/shard_map/ppermute | solution.py:144
  258.6 3.0 %collective-permute-done.5 = f32[64]{0:T(128)S(1)} collective-permute-done((f32[64]{0:T(128)S(1)}, f32[64]{0:T(128)S(1)}, u32[]{:S(2)}, u32[]{:S(2)}) %collective-permute-start.5) | collective-permute-done | bytes 288 | tf_op jit(solution)/shard_map/ppermute | solution.py:144
  261.6 2.1 collective-permute-start.6
  263.7 1.1 copy.71
  264.8 1.9 collective-permute-done.6
  (66 shorter events, 8.8 us)
Async XLA Ops:
  7.2 2.2 copy-start.2
  7.2 110.5 %all-gather.3.cloned.1.call-start = ((), (), s32[]{:S(2)}) async-start(), calls=%async_computation | async-start | bytes 10321920 | tf_op jit(solution)/shard_map/all_gather | solution.py:72
  9.5 3.2 %copy-start.1 = (bf16[1,128,2560]{2,1,0:T(8,128)(2,1)S(1)}, bf16[1,128,2560]{2,1,0:T(8,128)(2,1)}, u32[]{:S(2)}) copy-start(bf16[1,128,2560]{2,1,0:T(8,128)(2,1)} %param.11) | copy-start | bytes 1966084
  9.5 2.1 collective-permute-start.1
  12.7 193.6 %all-gather.5.cloned.1.call-start = ((), (), s32[]{:S(2)}) async-start(), calls=%async_computation.1 | async-start | bytes 4734976 | tf_op jit(solution)/shard_map/all_gather | solution.py:94
  13.1 2.2 collective-permute-start
  123.8 0.7 copy-start.4
  123.9 2.5 copy-start.5
  124.0 2.7 collective-permute-start.2
  126.7 0.9 copy-start
  129.5 3.1 %copy-start.3 = (bf16[2560]{0:T(1024)(128)(2,1)S(1)}, bf16[2560]{0:T(1024)(128)(2,1)}, u32[]{:S(2)}) copy-start(bf16[2560]{0:T(1024)(128)(2,1)} %param.19) | copy-start | bytes 15364
  233.5 9.4 %copy-start.6 = (s32[1,128]{1,0:T(1,128)S(1)}, s32[1,128]{1,0:T(1,128)}, u32[]{:S(2)}) copy-start(s32[1,128]{1,0:T(1,128)} %param.15) | copy-start | bytes 1540
  243.2 7.3 %collective-permute-start.3 = (f32[64]{0:T(128)S(1)}, f32[64]{0:T(128)S(1)}, u32[]{:S(2)}, u32[]{:S(2)}) collective-permute-start(f32[64]{0:T(128)S(1)} %pad_maximum_fusion.3), channel_id=1, source_target_pairs={{0,1},{1,0},{2,3},{3,2},{4,5},{5,4},{6,7},{7,6},{8,9},{9,8},{10,11... | collective-permute-start | bytes 776 | tf_op jit(solution)/shard_map/ppermute | solution.py:144
  250.6 7.5 %collective-permute-start.4 = (f32[64]{0:T(128)S(1)}, f32[64]{0:T(128)S(1)}, u32[]{:S(2)}, u32[]{:S(2)}) collective-permute-start(f32[64]{0:T(128)S(1)} %fusion.43), channel_id=1, source_target_pairs={{0,2},{1,3},{2,0},{3,1},{4,6},{5,7},{6,4},{7,5},{8,10},{9,11},{10,... | collective-permute-start | bytes 776 | tf_op jit(solution)/shard_map/ppermute | solution.py:144
  258.1 3.6 %collective-permute-start.5 = (f32[64]{0:T(128)S(1)}, f32[64]{0:T(128)S(1)}, u32[]{:S(2)}, u32[]{:S(2)}) collective-permute-start(f32[64]{0:T(128)S(1)} %add.158), channel_id=1, source_target_pairs={{0,4},{4,0},{8,12},{12,8},{1,5},{5,1},{9,13},{13,9},{2,6},{6,2},{1... | collective-permute-start | bytes 776 | tf_op jit(solution)/shard_map/ppermute | solution.py:144
  261.6 5.1 %collective-permute-start.6 = (f32[64]{0:T(128)S(1)}, f32[64]{0:T(128)S(1)}, u32[]{:S(2)}, u32[]{:S(2)}) collective-permute-start(f32[64]{0:T(128)S(1)} %add.159), channel_id=1, source_target_pairs={{0,8},{4,12},{8,0},{12,4},{1,9},{5,13},{9,1},{13,5},{2,10},{6,14},... | collective-permute-start | bytes 776 | tf_op jit(solution)/shard_map/ppermute | solution.py:144
Sparse Core Ops, SparseCore 0:
  12.8 104.8 all-gather.2
  131.4 74.7 all-gather.4

commit v7 on v6

--- a/solution.py
+++ b/solution.py
@@ -138,11 +138,16 @@
         tally = jnp.sum(onehot.astype(jnp.float32), axis=0)
         total = jnp.concatenate([sums, tally])
         for axis, size in (("cz", inner), ("cx", shards // inner)):
-            bit = 1
-            while bit < size:
-                pairs = [(s, s ^ bit) for s in range(size)]
-                total = total + lax.ppermute(total, axis, pairs)
-                bit *= 2
+            here = lax.axis_index(axis)
+            parts = [total]
+            for shift in range(1, size):
+                pairs = [(s, (s + shift) % size) for s in range(size)]
+                parts.append(lax.ppermute(total, axis, pairs))
+            order = (here - jnp.arange(size, dtype=jnp.int32)) % size
+            by_source = jnp.take(jnp.stack(parts), order, axis=0)
+            total = by_source[0]
+            for s in range(1, size):
+                total = total + by_source[s]
         return (attention[None], (total[:CAND] / total[CAND:])[None])
 
     return per_device

time: 275 us -> 273 us (level)
  waiting for transfers between devices: 183 us -> 177 us
  starting transfers between devices: 12.3 us -> 15.6 us
    ppermute x4 -> x6, waiting for transfers between devices: 10.8 us -> 3.79 us  [per_device(): parts.append(lax.ppermute(total, axis, pairs))]
    ppermute x4 -> x6, starting transfers between devices: 11.6 us -> 14.9 us  [per_device(): parts.append(lax.ppermute(total, axis, pairs))]
  transfers between devices with their start and end apart: 9 -> 11, of which waited for: 9 -> 7; matrix products, arithmetic and copies ran while one was open for 4% -> 4% of each run, Pallas kernels for 0% -> 0%
where the time goes in v7:
time: 273 us; the launch traced here: 271 us
  waiting for transfers between devices  177 us (65%)
  matrix products  27.2 us (10%)
  local copies, waits for them, and re-layouts  25 us (9%)
  starting transfers between devices  15.6 us (6%)
  between operations  15.1 us (6%)
  other arithmetic  11.6 us (4%)
    all_gather x1, waiting for transfers between devices, per_device(): half_weights = lax.all_gather(rows_block, ('dz', 'dy'), axis=0, tiled=True)  102 us
    all_gather x1, waiting for transfers between devices, per_device(): lax.all_gather(own_block, ('cx', 'cz'), axis=0, tiled=True)  66.8 us
    ppermute x6, starting transfers between devices, per_device(): parts.append(lax.ppermute(total, axis, pairs))  14.9 us
    dot_general x1, matrix products, per_device(): jnp.einsum('qhgd,khd->hgqk', per_head_queries, key_portion, preferred_ele...  11.6 us
    dot_general x1, matrix products, per_device(): jnp.einsum('hgqk,khd->qhgd', weights.astype(jnp.bfloat16), value_portion,...  9.2 us
    dot_general x1, matrix products, per_device(): projected = jnp.dot(both, half_weights, preferred_element_type=jnp.float32)  6.17 us
  transfers between devices with their start and end apart: 11, of which 7 were waited for; matrix products, arithmetic and copies ran while one was open for 4% of the time, Pallas kernels for 0%

profile of v7, /device:TPU:2, one launch (start us, length us, event | category | flops | bytes accessed | tf_op | source)
XLA Modules:
  0.0 271.3 jit_solution(13233720374018099216)
XLA Ops:
  7.2 1.2 constant_dynamic-update-slice_fusion.2
  8.5 0.9 constant_dynamic-update-slice_fusion.1
  9.6 2.0 collective-permute-done.1
  11.6 1.1 pad_maximum_fusion.1
  13.3 2.0 collective-permute-done
  15.7 101.9 %all-gather.3.cloned.1.call-done = bf16[2560,1792]{1,0:T(8,128)(2,1)} async-done(((bf16[320,1792]{1,0:T(8,128)(2,1)}), bf16[2560,1792]{1,0:T(8,128)(2,1)}) %all-gather.3.cloned.1.call-update) | async-done | bytes 9175056 | tf_op jit(solution)/shard_map/all_gather | solution.py:72
  117.7 6.2 %fusion.39 = f32[256,1792]{1,0:T(8,128)S(1)} fusion(bf16[256,2560]{0,1:T(8,128)(2,1)S(1)} %bitcast.77, bf16[2560,1792]{1,0:T(8,128)(2,1)} %all-gather.3.cloned.1.call-done), kind=kOutput, calls=%fused_computation.103 | convolution fusion | flops 2348810240 | bytes 12320768 | tf_op jit(solution)/shard_map/dot_general | solution.py:78
  126.7 0.9 copy-done
  127.6 1.7 maximum_select_fusion
  130.6 0.7 fusion.25
  133.3 0.7 iota_compare_fusion.3
  134.3 1.2 slice.120
  135.5 1.7 copy.66
  138.0 1.5 copy.68
  139.5 66.8 %all-gather.5.cloned.1.call-done = bf16[2176,1024]{1,0:T(8,128)(2,1)} async-done(((bf16[136,1024]{1,0:T(8,128)(2,1)}), bf16[2176,1024]{1,0:T(8,128)(2,1)}) %all-gather.5.cloned.1.call-update) | async-done | bytes 4456464 | tf_op jit(solution)/shard_map/all_gather | solution.py:94
  206.3 4.7 %fusion.37 = (bf16[16,128,512]{2,1,0:T(8,128)(2,1)}, bf16[16,128,512]{2,1,0:T(8,128)(2,1)}) fusion(bf16[16,136,1024]{2,1,0:T(8,128)(2,1)} %bitcast.81), kind=kLoop, calls=%fused_computation.101 | loop fusion | bytes 8388608 | tf_op jit(solution)/shard_map/slice | solution.py:101
  211.0 0.8 slice_convert_fusion.1
  211.8 2.5 reshape.428
  214.3 2.7 copy.81
  217.0 2.5 reshape.426
  219.6 1.9 compare_and_fusion
  221.5 11.6 %fusion = (f32[4,5,128]{2,1,0:T(8,128)S(1)}, f32[4,2048,128,5]{2,1,3,0:T(8,128)}) fusion(pred[128,2048]{0,1:T(8,128)(4,1)S(1)} %compare_and_fusion, f32[128,4,5,64]{3,0,2,1:T(8,128)} %copy.68, f32[128,4,5,64]{3,0,2,1:T(8,128)S(1)} %copy.67, f32[128,4,5]{0,2,1:T(8,128)S(1)} %rsqrt.21, bf16[2048,4,128]{0,2,1:T(8,128)(2,1)} %copy.81), kind=kOutput, calls=%fused_computation.3 | convolution fusion | flops 1358886400 | bytes 24662016 | tf_op jit(solution)/shard_map/qhgd,khd->hgqk/dot_general | solution.py:113
  233.1 9.2 %multiply_convert_fusion = bf16[128,4,5,128]{0,3,2,1:T(8,128)(2,1)S(1)} fusion(f32[4,2048,128,5]{2,1,3,0:T(8,128)} %get-tuple-element.40, pred[128,2048]{0,1:T(8,128)(4,1)S(1)} %compare_and_fusion, bf16[2048,4,128,1]{2,1,0,3:T(4,128)(2,1)S(1)} %bitcast.87, f32[128]{0:T(128)S(1)} %get-tuple-element.46, f32[128,4,5]{0,2,1:T(8,128)S(1)} %select_bitcast_fusion), kind=kOutput, calls=%fused_computation.20 | convolution fusion | flops 1358888960 | bytes 23996928 | tf_op jit(solution)/shard_map/hgqk,khd->qhgd/dot_general | solution.py:123
  242.7 5.8 %collective-permute-start.3 = (f32[64]{0:T(128)S(1)}, f32[64]{0:T(128)S(1)}, u32[]{:S(2)}, u32[]{:S(2)}) collective-permute-start(f32[64]{0:T(128)S(1)} %pad_maximum_fusion.5), channel_id=1, source_target_pairs={{0,1},{1,2},{2,3},{3,0},{4,5},{5,6},{6,7},{7,4},{8,9},{9,10},{10,1... | collective-permute-start | bytes 776 | tf_op jit(solution)/shard_map/ppermute | solution.py:145
  248.5 2.4 collective-permute-start.4
  251.0 2.0 collective-permute-start.5
  252.9 1.1 copy.71
  254.0 2.0 collective-permute-done.4
  256.6 1.5 collective-permute-start.6
  258.1 1.2 collective-permute-start.7
  259.3 2.1 collective-permute-start.8
  261.4 1.8 collective-permute-done.7
  (80 shorter events, 10.0 us)
Async XLA Ops:
  7.2 2.2 copy-start.2
  7.2 110.5 %all-gather.3.cloned.1.call-start = ((), (), s32[]{:S(2)}) async-start(), calls=%async_computation | async-start | bytes 10321920 | tf_op jit(solution)/shard_map/all_gather | solution.py:72
  9.5 3.2 %copy-start.1 = (bf16[1,128,2560]{2,1,0:T(8,128)(2,1)S(1)}, bf16[1,128,2560]{2,1,0:T(8,128)(2,1)}, u32[]{:S(2)}) copy-start(bf16[1,128,2560]{2,1,0:T(8,128)(2,1)} %param.13) | copy-start | bytes 1966084
  9.5 2.1 collective-permute-start.1
  12.7 193.6 %all-gather.5.cloned.1.call-start = ((), (), s32[]{:S(2)}) async-start(), calls=%async_computation.1 | async-start | bytes 4734976 | tf_op jit(solution)/shard_map/all_gather | solution.py:94
  13.1 2.2 collective-permute-start
  123.8 0.7 copy-start.4
  123.8 2.6 copy-start.5
  124.0 2.7 %collective-permute-start.2 = (f32[128,1792]{1,0:T(8,128)S(1)}, f32[128,1792]{1,0:T(8,128)S(1)}, u32[]{:S(2)}, u32[]{:S(2)}) collective-permute-start(f32[128,1792]{1,0:T(8,128)S(1)} %get-tuple-element.30), channel_id=1, source_target_pairs={{0,16},{16,0},{1,17},{17,1},{2,18},{18,2},{3,19},{19,3},{4,20},{20... | collective-permute-start | bytes 2752520 | tf_op jit(solution)/shard_map/ppermute | solution.py:79
  126.7 0.9 copy-start
  129.5 3.2 %copy-start.3 = (bf16[2560]{0:T(1024)(128)(2,1)S(1)}, bf16[2560]{0:T(1024)(128)(2,1)}, u32[]{:S(2)}) copy-start(bf16[2560]{0:T(1024)(128)(2,1)} %param.21) | copy-start | bytes 15364
  233.1 9.4 %copy-start.6 = (s32[1,128]{1,0:T(1,128)S(1)}, s32[1,128]{1,0:T(1,128)}, u32[]{:S(2)}) copy-start(s32[1,128]{1,0:T(1,128)} %param.17) | copy-start | bytes 1540
  242.7 11.3 %collective-permute-start.3 = (f32[64]{0:T(128)S(1)}, f32[64]{0:T(128)S(1)}, u32[]{:S(2)}, u32[]{:S(2)}) collective-permute-start(f32[64]{0:T(128)S(1)} %pad_maximum_fusion.5), channel_id=1, source_target_pairs={{0,1},{1,2},{2,3},{3,0},{4,5},{5,6},{6,7},{7,4},{8,9},{9,10},{10,1... | collective-permute-start | bytes 776 | tf_op jit(solution)/shard_map/ppermute | solution.py:145
  248.5 7.5 %collective-permute-start.4 = (f32[64]{0:T(128)S(1)}, f32[64]{0:T(128)S(1)}, u32[]{:S(2)}, u32[]{:S(2)}) collective-permute-start(f32[64]{0:T(128)S(1)} %pad_maximum_fusion.5), channel_id=1, source_target_pairs={{0,2},{1,3},{2,0},{3,1},{4,6},{5,7},{6,4},{7,5},{8,10},{9,11},{10,... | collective-permute-start | bytes 776 | tf_op jit(solution)/shard_map/ppermute | solution.py:145
  251.0 5.0 %collective-permute-start.5 = (f32[64]{0:T(128)S(1)}, f32[64]{0:T(128)S(1)}, u32[]{:S(2)}, u32[]{:S(2)}) collective-permute-start(f32[64]{0:T(128)S(1)} %pad_maximum_fusion.5), channel_id=1, source_target_pairs={{0,3},{1,0},{2,1},{3,2},{4,7},{5,4},{6,5},{7,6},{8,11},{9,8},{10,9... | collective-permute-start | bytes 776 | tf_op jit(solution)/shard_map/ppermute | solution.py:145
  256.6 4.7 %collective-permute-start.6 = (f32[64]{0:T(128)S(1)}, f32[64]{0:T(128)S(1)}, u32[]{:S(2)}, u32[]{:S(2)}) collective-permute-start(f32[64]{0:T(128)S(1)} %fusion.44), channel_id=1, source_target_pairs={{0,4},{4,8},{8,12},{12,0},{1,5},{5,9},{9,13},{13,1},{2,6},{6,10},{... | collective-permute-start | bytes 776 | tf_op jit(solution)/shard_map/ppermute | solution.py:145
  258.1 5.1 %collective-permute-start.7 = (f32[64]{0:T(128)S(1)}, f32[64]{0:T(128)S(1)}, u32[]{:S(2)}, u32[]{:S(2)}) collective-permute-start(f32[64]{0:T(128)S(1)} %fusion.44), channel_id=1, source_target_pairs={{0,8},{4,12},{8,0},{12,4},{1,9},{5,13},{9,1},{13,5},{2,10},{6,14},... | collective-permute-start | bytes 776 | tf_op jit(solution)/shard_map/ppermute | solution.py:145
  259.3 3.9 %collective-permute-start.8 = (f32[64]{0:T(128)S(1)}, f32[64]{0:T(128)S(1)}, u32[]{:S(2)}, u32[]{:S(2)}) collective-permute-start(f32[64]{0:T(128)S(1)} %fusion.44), channel_id=1, source_target_pairs={{0,12},{4,0},{8,4},{12,8},{1,13},{5,1},{9,5},{13,9},{2,14},{6,2},{... | collective-permute-start | bytes 776 | tf_op jit(solution)/shard_map/ppermute | solution.py:145
Sparse Core Ops, SparseCore 0:
  12.8 104.8 all-gather.2
  131.4 74.7 all-gather.4

commit v8 on v7

--- a/solution.py
+++ b/solution.py
@@ -33,7 +33,7 @@
     return (turned * scale).astype(jnp.bfloat16).reshape(token_count, heads * HEAD_SIZE)
 
 
-def make_per_device(shards, inner):
+def make_per_device(shards, inner, dp_size):
     def per_device(
         tokens,
         shard_counts,
@@ -69,11 +69,19 @@
         partner_rows = lax.ppermute(other_half, "dc", swap)
         partner_tokens = lax.ppermute(inputs, "dc", swap)
         rows_block = jnp.concatenate([mine_half, partner_rows], axis=0)
-        half_weights = lax.all_gather(rows_block, ("dz", "dy"), axis=0, tiled=True)
+        chips = dp_size // 2
+        received = [rows_block]
+        for shift in range(1, chips):
+            pairs = [(s, (s + shift) % chips) for s in range(chips)]
+            received.append(lax.ppermute(rows_block, ("dz", "dy"), pairs))
+        half_weights = jnp.concatenate(received, axis=0)
+        chip = lax.axis_index(("dz", "dy"))
         both = jnp.concatenate([inputs, partner_tokens], axis=0)
         features = both.shape[1]
-        paired = both.reshape(2 * token_slots, features // (2 * chunk), 2, chunk)
+        paired = both.reshape(2 * token_slots, chips, 2, chunk)
         paired = jnp.where(core == 0, paired, paired[:, :, ::-1, :])
+        sources = (chip - jnp.arange(chips, dtype=jnp.int32)) % chips
+        paired = jnp.take(paired, sources, axis=1)
         both = paired.reshape(2 * token_slots, features)
         projected = jnp.dot(both, half_weights, preferred_element_type=jnp.float32)
         returned = lax.ppermute(projected[token_slots:], "dc", swap)
@@ -174,7 +182,7 @@
         P(),
     )
     return jax.shard_map(
-        make_per_device(shards, inner),
+        make_per_device(shards, inner, mesh.shape["dp"]),
         mesh=split,
         in_specs=placed,
         out_specs=(P(dp, ctx, None), P(dp, None)),

time: 273 us -> 344 us (1.26)
  waiting for transfers between devices: 177 us -> 218 us
  local copies, waits for them, and re-layouts: 25 us -> 42.9 us
  starting transfers between devices: 15.6 us -> 25.3 us
    ppermute x0 -> x7, waiting for transfers between devices: none -> 130 us  [per_device(): received.append(lax.ppermute(rows_block, ('dz', 'dy'), pairs))]
    all_gather x1 -> x0, waiting for transfers between devices: 102 us -> none  [per_device(): half_weights = lax.all_gather(rows_block, ('dz', 'dy'), axis=0, tiled=True)]
    all_gather x1, waiting for transfers between devices: 66.8 us -> 83.7 us  [per_device(): lax.all_gather(own_block, ('cx', 'cz'), axis=0, tiled=True)]
    unnamed x20 -> x28, local copies, waits for them, and re-layouts: 4.76 us -> 19.5 us
    ppermute x0 -> x7, starting transfers between devices: none -> 9.45 us  [per_device(): received.append(lax.ppermute(rows_block, ('dz', 'dy'), pairs))]
  transfers between devices with their start and end apart: 11 -> 17, of which waited for: 7 -> 8; matrix products, arithmetic and copies ran while one was open for 4% -> 9% of each run, Pallas kernels for 0% -> 0%
where the time goes in v8:
time: 344 us; the launch traced here: 342 us
  waiting for transfers between devices  218 us (63%)
  local copies, waits for them, and re-layouts  42.9 us (12%)
  matrix products  27.6 us (8%)
  starting transfers between devices  25.3 us (7%)
  between operations  15.1 us (4%)
  other arithmetic  12.9 us (4%)
    ppermute x7, waiting for transfers between devices, per_device(): received.append(lax.ppermute(rows_block, ('dz', 'dy'), pairs))  130 us
    all_gather x1, waiting for transfers between devices, per_device(): lax.all_gather(own_block, ('cx', 'cz'), axis=0, tiled=True)  83.7 us
    unnamed x28, local copies, waits for them, and re-layouts  19.5 us
    ppermute x6, starting transfers between devices, per_device(): parts.append(lax.ppermute(total, axis, pairs))  14.9 us
    dot_general x1, matrix products, per_device(): jnp.einsum('qhgd,khd->hgqk', per_head_queries, key_portion, preferred_ele...  12.1 us
    ppermute x7, starting transfers between devices, per_device(): received.append(lax.ppermute(rows_block, ('dz', 'dy'), pairs))  9.45 us
    dot_general x1, matrix products, per_device(): jnp.einsum('hgqk,khd->qhgd', weights.astype(jnp.bfloat16), value_portion,...  9.2 us
  transfers between devices with their start and end apart: 17, of which 8 were waited for; matrix products, arithmetic and copies ran while one was open for 9% of the time, Pallas kernels for 0%

profile of v8, /device:TPU:2, one launch (start us, length us, event | category | flops | bytes accessed | tf_op | source)
XLA Modules:
  0.0 342.0 jit_solution(642664967760290451)
XLA Ops:
  13.5 1.6 collective-permute-start.2
  15.1 2.9 collective-permute-start.3
  18.0 2.7 collective-permute-start.4
  21.6 2.0 collective-permute-start.6
  26.1 42.8 %collective-permute-done.2 = bf16[320,1792]{1,0:T(8,128)(2,1)} collective-permute-done((bf16[320,1792]{1,0:T(8,128)(2,1)}, bf16[320,1792]{1,0:T(8,128)(2,1)}, u32[]{:S(2)}, u32[]{:S(2)}) %collective-permute-start.2) | collective-permute-done | bytes 1146912 | tf_op jit(solution)/shard_map/ppermute | solution.py:76
  69.0 2.3 constant_dynamic-update-slice_fusion.9
  71.4 64.4 %collective-permute-done.3 = bf16[320,1792]{1,0:T(8,128)(2,1)} collective-permute-done((bf16[320,1792]{1,0:T(8,128)(2,1)}, bf16[320,1792]{1,0:T(8,128)(2,1)}, u32[]{:S(2)}, u32[]{:S(2)}) %collective-permute-start.3) | collective-permute-done | bytes 1146912 | tf_op jit(solution)/shard_map/ppermute | solution.py:76
  135.8 2.4 constant_dynamic-update-slice_fusion.8
  138.1 2.4 constant_dynamic-update-slice_fusion.7
  140.5 2.4 constant_dynamic-update-slice_fusion.6
  142.9 2.3 constant_dynamic-update-slice_fusion.5
  146.3 22.4 %collective-permute-done.8 = bf16[320,1792]{1,0:T(8,128)(2,1)S(1)} collective-permute-done((bf16[320,1792]{1,0:T(8,128)(2,1)}, bf16[320,1792]{1,0:T(8,128)(2,1)S(1)}, u32[]{:S(2)}, u32[]{:S(2)}) %collective-permute-start.8) | collective-permute-done | bytes 1146912 | tf_op jit(solution)/shard_map/ppermute | solution.py:76
  170.0 6.2 %fusion.42 = f32[256,1792]{1,0:T(8,128)S(1)} fusion(bf16[256,2560]{0,1:T(8,128)(2,1)S(1)} %bitcast_select_fusion.1, bf16[2560,1792]{1,0:T(8,128)(2,1)} %constant_dynamic-update-slice_fusion.3), kind=kOutput, calls=%fused_computation.127 | convolution fusion | flops 2348810240 | bytes 12320768 | tf_op jit(solution)/shard_map/dot_general | solution.py:86
  180.0 1.6 maximum_select_fusion
  187.8 1.7 copy.66
  189.9 1.6 copy.67
  191.4 1.5 copy.68
  192.9 83.7 %all-gather.2.cloned.1.call-done = bf16[2176,1024]{1,0:T(8,128)(2,1)} async-done(((bf16[136,1024]{1,0:T(8,128)(2,1)}), bf16[2176,1024]{1,0:T(8,128)(2,1)}) %all-gather.2.cloned.1.call-update) | async-done | bytes 4456464 | tf_op jit(solution)/shard_map/all_gather | solution.py:102
  276.6 4.7 %fusion.40 = (bf16[16,128,512]{2,1,0:T(8,128)(2,1)}, bf16[16,128,512]{2,1,0:T(8,128)(2,1)}) fusion(bf16[16,136,1024]{2,1,0:T(8,128)(2,1)} %bitcast.85), kind=kLoop, calls=%fused_computation.125 | loop fusion | bytes 8388608 | tf_op jit(solution)/shard_map/slice | solution.py:109
  282.1 2.5 reshape.489
  284.6 2.7 copy.81
  287.3 2.5 reshape.487
  289.9 1.9 compare_and_fusion
  291.8 12.1 %fusion = (f32[4,5,128]{2,1,0:T(8,128)S(1)}, f32[4,2048,128,5]{2,1,3,0:T(8,128)}) fusion(pred[128,2048]{0,1:T(8,128)(4,1)S(1)} %compare_and_fusion, f32[128,4,5,64]{3,0,2,1:T(8,128)} %copy.68, f32[128,4,5,64]{3,0,2,1:T(8,128)} %copy.67, f32[128,4,5]{0,2,1:T(8,128)S(1)} %rsqrt.21, bf16[2048,4,128]{0,2,1:T(8,128)(2,1)} %copy.81), kind=kOutput, calls=%fused_computation.4 | convolution fusion | flops 1358886400 | bytes 24662016 | tf_op jit(solution)/shard_map/qhgd,khd->hgqk/dot_general | solution.py:121
  303.9 9.2 %multiply_convert_fusion = bf16[128,4,5,128]{0,3,2,1:T(8,128)(2,1)S(1)} fusion(f32[4,2048,128,5]{2,1,3,0:T(8,128)} %get-tuple-element.41, pred[128,2048]{0,1:T(8,128)(4,1)S(1)} %compare_and_fusion, bf16[2048,4,128,1]{2,1,0,3:T(4,128)(2,1)S(1)} %bitcast.91, f32[128]{0:T(128)S(1)} %get-tuple-element.47, f32[128,4,5]{0,2,1:T(8,128)S(1)} %select_bitcast_fusion), kind=kOutput, calls=%fused_computation.22 | convolution fusion | flops 1358888960 | bytes 23996928 | tf_op jit(solution)/shard_map/hgqk,khd->qhgd/dot_general | solution.py:131
  313.5 5.8 %collective-permute-start.10 = (f32[64]{0:T(128)S(1)}, f32[64]{0:T(128)S(1)}, u32[]{:S(2)}, u32[]{:S(2)}) collective-permute-start(f32[64]{0:T(128)S(1)} %pad_maximum_fusion.5), channel_id=1, source_target_pairs={{0,1},{1,2},{2,3},{3,0},{4,5},{5,6},{6,7},{7,4},{8,9},{9,10},{10,1... | collective-permute-start | bytes 776 | tf_op jit(solution)/shard_map/ppermute | solution.py:153
  319.2 2.5 collective-permute-start.11
  321.7 2.0 collective-permute-start.12
  324.8 2.0 collective-permute-done.11
  327.4 1.5 collective-permute-start.13
  330.0 2.1 collective-permute-start.15
  332.1 1.8 collective-permute-done.14
  (106 shorter events, 26.9 us)
Async XLA Ops:
  7.2 2.3 copy-start.2
  7.2 269.4 %all-gather.2.cloned.1.call-start = ((), (), s32[]{:S(2)}) async-start(), calls=%async_computation | async-start | bytes 4734976 | tf_op jit(solution)/shard_map/all_gather | solution.py:102
  8.5 2.0 copy-start.1
  10.4 2.0 collective-permute-start.1
  10.8 10.9 %collective-permute-start = (bf16[128,2560]{0,1:T(8,128)(2,1)S(1)}, bf16[128,2560]{0,1:T(8,128)(2,1)S(1)}, u32[]{:S(2)}, u32[]{:S(2)}) collective-permute-start(bf16[128,2560]{0,1:T(8,128)(2,1)S(1)} %bitcast.87), channel_id=1, source_target_pairs={{0,16},{16,0},{1,17},{17,1},{2,18},{18,2},{3,19},{19,3},{4,20},{20... | collective-permute-start | bytes 1966088 | tf_op jit(solution)/shard_map/ppermute | solution.py:70
  13.5 55.4 %collective-permute-start.2 = (bf16[320,1792]{1,0:T(8,128)(2,1)}, bf16[320,1792]{1,0:T(8,128)(2,1)}, u32[]{:S(2)}, u32[]{:S(2)}) collective-permute-start(bf16[320,1792]{1,0:T(8,128)(2,1)} %pad_maximum_fusion.1), channel_id=1, source_target_pairs={{0,32},{32,64},{64,96},{96,128},{128,160},{160,192},{192,224},{224... | collective-permute-start | bytes 3440648 | tf_op jit(solution)/shard_map/ppermute | solution.py:76
  15.1 120.7 %collective-permute-start.3 = (bf16[320,1792]{1,0:T(8,128)(2,1)}, bf16[320,1792]{1,0:T(8,128)(2,1)}, u32[]{:S(2)}, u32[]{:S(2)}) collective-permute-start(bf16[320,1792]{1,0:T(8,128)(2,1)} %pad_maximum_fusion.1), channel_id=1, source_target_pairs={{0,64},{32,96},{64,128},{96,160},{128,192},{160,224},{192,0},{224,... | collective-permute-start | bytes 3440648 | tf_op jit(solution)/shard_map/ppermute | solution.py:76
  18.0 120.2 %collective-permute-start.4 = (bf16[320,1792]{1,0:T(8,128)(2,1)}, bf16[320,1792]{1,0:T(8,128)(2,1)}, u32[]{:S(2)}, u32[]{:S(2)}) collective-permute-start(bf16[320,1792]{1,0:T(8,128)(2,1)} %pad_maximum_fusion.1), channel_id=1, source_target_pairs={{0,96},{32,128},{64,160},{96,192},{128,224},{160,0},{192,32},{224,... | collective-permute-start | bytes 3440648 | tf_op jit(solution)/shard_map/ppermute | solution.py:76
  20.7 119.8 %collective-permute-start.5 = (bf16[320,1792]{1,0:T(8,128)(2,1)}, bf16[320,1792]{1,0:T(8,128)(2,1)}, u32[]{:S(2)}, u32[]{:S(2)}) collective-permute-start(bf16[320,1792]{1,0:T(8,128)(2,1)} %pad_maximum_fusion.1), channel_id=1, source_target_pairs={{0,128},{32,160},{64,192},{96,224},{128,0},{160,32},{192,64},{224,... | collective-permute-start | bytes 3440648 | tf_op jit(solution)/shard_map/ppermute | solution.py:76
  21.6 121.3 %collective-permute-start.6 = (bf16[320,1792]{1,0:T(8,128)(2,1)}, bf16[320,1792]{1,0:T(8,128)(2,1)}, u32[]{:S(2)}, u32[]{:S(2)}) collective-permute-start(bf16[320,1792]{1,0:T(8,128)(2,1)} %pad_maximum_fusion.1), channel_id=1, source_target_pairs={{0,160},{32,192},{64,224},{96,0},{128,32},{160,64},{192,96},{224,1... | collective-permute-start | bytes 3440648 | tf_op jit(solution)/shard_map/ppermute | solution.py:76
  68.9 76.3 %collective-permute-start.7 = (bf16[320,1792]{1,0:T(8,128)(2,1)}, bf16[320,1792]{1,0:T(8,128)(2,1)S(1)}, u32[]{:S(2)}, u32[]{:S(2)}) collective-permute-start(bf16[320,1792]{1,0:T(8,128)(2,1)} %pad_maximum_fusion.1), channel_id=1, source_target_pairs={{0,192},{32,224},{64,0},{96,32},{128,64},{160,96},{192,128},{224,1... | collective-permute-start | bytes 3440648 | tf_op jit(solution)/shard_map/ppermute | solution.py:76
  135.8 33.0 %collective-permute-start.8 = (bf16[320,1792]{1,0:T(8,128)(2,1)}, bf16[320,1792]{1,0:T(8,128)(2,1)S(1)}, u32[]{:S(2)}, u32[]{:S(2)}) collective-permute-start(bf16[320,1792]{1,0:T(8,128)(2,1)} %pad_maximum_fusion.1), channel_id=1, source_target_pairs={{0,224},{32,0},{64,32},{96,64},{128,96},{160,128},{192,160},{224,1... | collective-permute-start | bytes 3440648 | tf_op jit(solution)/shard_map/ppermute | solution.py:76
  176.1 0.7 copy-start.4
  176.2 2.6 copy-start.5
  176.3 2.7 collective-permute-start.9
  179.0 0.9 copy-start
  181.8 3.2 copy-start.3
  303.8 9.4 %copy-start.6 = (s32[1,128]{1,0:T(1,128)S(1)}, s32[1,128]{1,0:T(1,128)}, u32[]{:S(2)}) copy-start(s32[1,128]{1,0:T(1,128)} %param.17) | copy-start | bytes 1540
  313.5 11.3 %collective-permute-start.10 = (f32[64]{0:T(128)S(1)}, f32[64]{0:T(128)S(1)}, u32[]{:S(2)}, u32[]{:S(2)}) collective-permute-start(f32[64]{0:T(128)S(1)} %pad_maximum_fusion.5), channel_id=1, source_target_pairs={{0,1},{1,2},{2,3},{3,0},{4,5},{5,6},{6,7},{7,4},{8,9},{9,10},{10,1... | collective-permute-start | bytes 776 | tf_op jit(solution)/shard_map/ppermute | solution.py:153
  319.2 7.5 %collective-permute-start.11 = (f32[64]{0:T(128)S(1)}, f32[64]{0:T(128)S(1)}, u32[]{:S(2)}, u32[]{:S(2)}) collective-permute-start(f32[64]{0:T(128)S(1)} %pad_maximum_fusion.5), channel_id=1, source_target_pairs={{0,2},{1,3},{2,0},{3,1},{4,6},{5,7},{6,4},{7,5},{8,10},{9,11},{10,... | collective-permute-start | bytes 776 | tf_op jit(solution)/shard_map/ppermute | solution.py:153
  321.7 5.0 %collective-permute-start.12 = (f32[64]{0:T(128)S(1)}, f32[64]{0:T(128)S(1)}, u32[]{:S(2)}, u32[]{:S(2)}) collective-permute-start(f32[64]{0:T(128)S(1)} %pad_maximum_fusion.5), channel_id=1, source_target_pairs={{0,3},{1,0},{2,1},{3,2},{4,7},{5,4},{6,5},{7,6},{8,11},{9,8},{10,9... | collective-permute-start | bytes 776 | tf_op jit(solution)/shard_map/ppermute | solution.py:153
  327.4 4.7 %collective-permute-start.13 = (f32[64]{0:T(128)S(1)}, f32[64]{0:T(128)S(1)}, u32[]{:S(2)}, u32[]{:S(2)}) collective-permute-start(f32[64]{0:T(128)S(1)} %fusion.47), channel_id=1, source_target_pairs={{0,4},{4,8},{8,12},{12,0},{1,5},{5,9},{9,13},{13,1},{2,6},{6,10},{... | collective-permute-start | bytes 776 | tf_op jit(solution)/shard_map/ppermute | solution.py:153
  328.9 5.1 %collective-permute-start.14 = (f32[64]{0:T(128)S(1)}, f32[64]{0:T(128)S(1)}, u32[]{:S(2)}, u32[]{:S(2)}) collective-permute-start(f32[64]{0:T(128)S(1)} %fusion.47), channel_id=1, source_target_pairs={{0,8},{4,12},{8,0},{12,4},{1,9},{5,13},{9,1},{13,5},{2,10},{6,14},... | collective-permute-start | bytes 776 | tf_op jit(solution)/shard_map/ppermute | solution.py:153
  330.0 3.9 %collective-permute-start.15 = (f32[64]{0:T(128)S(1)}, f32[64]{0:T(128)S(1)}, u32[]{:S(2)}, u32[]{:S(2)}) collective-permute-start(f32[64]{0:T(128)S(1)} %fusion.47), channel_id=1, source_target_pairs={{0,12},{4,0},{8,4},{12,8},{1,13},{5,1},{9,5},{13,9},{2,14},{6,2},{... | collective-permute-start | bytes 776 | tf_op jit(solution)/shard_map/ppermute | solution.py:153
Sparse Core Ops, SparseCore 0:
  183.7 92.8 all-gather.1

commit v9 on v6

--- a/solution.py
+++ b/solution.py
@@ -33,6 +33,21 @@
     return (turned * scale).astype(jnp.bfloat16).reshape(token_count, heads * HEAD_SIZE)
 
 
+def ctx_sum(total, shards, inner):
+    for axis, size in (("cz", inner), ("cx", shards // inner)):
+        here = lax.axis_index(axis)
+        parts = [total]
+        for shift in range(1, size):
+            pairs = [(s, (s + shift) % size) for s in range(size)]
+            parts.append(lax.ppermute(total, axis, pairs))
+        order = (here - jnp.arange(size, dtype=jnp.int32)) % size
+        by_source = jnp.take(jnp.stack(parts), order, axis=0)
+        total = by_source[0]
+        for s in range(1, size):
+            total = total + by_source[s]
+    return total
+
+
 def make_per_device(shards, inner):
     def per_device(
         tokens,
@@ -57,6 +72,8 @@
         cstart = stretch_start[0]
         qseg = segment_ids[0]
         qchunk = (token_places + STRETCH - cstart) // STRETCH
+        first_count = jnp.sum((live & (qseg == 0)).astype(jnp.int32)).reshape(1)
+        doc_edge = ctx_sum(first_count, shards, inner)[0]
 
         q_width = QUERY_HEADS * HEAD_SIZE
         core = lax.axis_index("dc")
@@ -86,13 +103,9 @@
         query = full[:, :q_width]
         key_norm = rotary_then_norm(full[:, q_width : q_width + kv_width], token_places, KEY_VALUE_HEADS)
         value_rows = full[:, q_width + kv_width :].astype(jnp.bfloat16)
-        seg_row = jnp.zeros((8, 2 * kv_width), jnp.bfloat16)
-        seg_row = seg_row.at[0, :token_slots].set(qseg.astype(jnp.bfloat16))
-        own_block = jnp.concatenate(
-            [jnp.concatenate([key_norm, value_rows], axis=1), seg_row], axis=0
-        )
+        own_block = jnp.concatenate([key_norm, value_rows], axis=1)
         gathered = lax.all_gather(own_block, ("cx", "cz"), axis=0, tiled=True).reshape(
-            shards, token_slots + 8, 2 * kv_width
+            shards, token_slots, 2 * kv_width
         )
         key_count = shards * token_slots
         key_portion = gathered[:, :token_slots, :kv_width].reshape(
@@ -101,8 +114,8 @@
         value_portion = gathered[:, :token_slots, kv_width:].reshape(
             key_count, KEY_VALUE_HEADS, HEAD_SIZE
         )
-        kseg = gathered[:, token_slots, :token_slots].reshape(key_count).astype(jnp.int32)
         kpos = (starts[:, None] + offsets[None, :]).reshape(key_count)
+        kseg = (kpos >= doc_edge).astype(jnp.int32)
         klive = (offsets[None, :] < counts[:, None]).reshape(key_count)
         kchunk = (kpos + STRETCH - cstart) // STRETCH
 
@@ -137,12 +150,7 @@
         sums = jnp.sum(jnp.where(onehot, loglik[:, None], 0.0), axis=0)
         tally = jnp.sum(onehot.astype(jnp.float32), axis=0)
         total = jnp.concatenate([sums, tally])
-        for axis, size in (("cz", inner), ("cx", shards // inner)):
-            bit = 1
-            while bit < size:
-                pairs = [(s, s ^ bit) for s in range(size)]
-                total = total + lax.ppermute(total, axis, pairs)
-                bit *= 2
+        total = ctx_sum(total, shards, inner)
         return (attention[None], (total[:CAND] / total[CAND:])[None])
 
     return per_device

time: 275 us -> 268 us (0.975)
  waiting for transfers between devices: 183 us -> 141 us
  starting transfers between devices: 12.3 us -> 32.2 us
  other arithmetic: 11.3 us -> 16.7 us
  between operations: 15.1 us -> 20.2 us
  local copies, waits for them, and re-layouts: 25.1 us -> 28.8 us
    all_gather x1, waiting for transfers between devices: 65.8 us -> 30.5 us  [per_device(): lax.all_gather(own_block, ('cx', 'cz'), axis=0, tiled=True)]
    ppermute x4 -> x12, starting transfers between devices: 11.6 us -> 31.8 us  [ctx_sum(): parts.append(lax.ppermute(total, axis, pairs))]
    ppermute x4 -> x12, waiting for transfers between devices: 10.8 us -> 4.53 us  [ctx_sum(): parts.append(lax.ppermute(total, axis, pairs))]
    another operation x2 -> x6, other arithmetic: 0.16 us -> 4.77 us  [the longest x4 4.62 us: ctx_sum(): by_source = jnp.take(jnp.stack(parts), order, axis=0)]
  transfers between devices with their start and end apart: 9 -> 17, of which waited for: 9 -> 10; matrix products, arithmetic and copies ran while one was open for 4% -> 9% of each run, Pallas kernels for 0% -> 0%
where the time goes in v9:
time: 268 us; the launch traced here: 267 us
  waiting for transfers between devices  141 us (53%)
  starting transfers between devices  32.2 us (12%)
  local copies, waits for them, and re-layouts  28.8 us (11%)
  matrix products  27.6 us (10%)
  between operations  20.2 us (8%)
  other arithmetic  16.7 us (6%)
    all_gather x1, waiting for transfers between devices, per_device(): half_weights = lax.all_gather(rows_block, ('dz', 'dy'), axis=0, tiled=True)  102 us
    ppermute x12, starting transfers between devices, ctx_sum(): parts.append(lax.ppermute(total, axis, pairs))  31.8 us
    all_gather x1, waiting for transfers between devices, per_device(): lax.all_gather(own_block, ('cx', 'cz'), axis=0, tiled=True)  30.5 us
    dot_general x1, matrix products, per_device(): jnp.einsum('qhgd,khd->hgqk', per_head_queries, key_portion, preferred_ele...  12 us
    dot_general x1, matrix products, per_device(): jnp.einsum('hgqk,khd->qhgd', weights.astype(jnp.bfloat16), value_portion,...  9.2 us
    dot_general x1, matrix products, per_device(): projected = jnp.dot(both, half_weights, preferred_element_type=jnp.float32)  6.17 us
  transfers between devices with their start and end apart: 17, of which 10 were waited for; matrix products, arithmetic and copies ran while one was open for 9% of the time, Pallas kernels for 0%

profile of v9, /device:TPU:2, one launch (start us, length us, event | category | flops | bytes accessed | tf_op | source)
XLA Modules:
  0.0 266.5 jit_solution(11815030397909226946)
XLA Ops:
  9.6 2.0 collective-permute-done.1
  13.3 2.0 collective-permute-done
  15.7 101.9 %all-gather.3.cloned.1.call-done = bf16[2560,1792]{1,0:T(8,128)(2,1)} async-done(((bf16[320,1792]{1,0:T(8,128)(2,1)}), bf16[2560,1792]{1,0:T(8,128)(2,1)}) %all-gather.3.cloned.1.call-update) | async-done | bytes 9175056 | tf_op jit(solution)/shard_map/all_gather | solution.py:89
  117.7 6.2 %fusion.40 = f32[256,1792]{1,0:T(8,128)S(1)} fusion(bf16[256,2560]{0,1:T(8,128)(2,1)S(1)} %bitcast.97, bf16[2560,1792]{1,0:T(8,128)(2,1)} %all-gather.3.cloned.1.call-done), kind=kOutput, calls=%fused_computation.111 | convolution fusion | flops 2348810240 | bytes 12320768 | tf_op jit(solution)/shard_map/dot_general | solution.py:95
  127.5 1.6 maximum_select_fusion
  132.4 2.0 and_select_fusion
  134.4 2.5 collective-permute-start.3
  136.9 3.0 %collective-permute-start.4 = (s32[1]{0:T(128)}, s32[1]{0:T(128)}, u32[]{:S(2)}, u32[]{:S(2)}) collective-permute-start(s32[1]{0:T(128)} %bitcast.13), channel_id=1, source_target_pairs={{0,2},{1,3},{2,0},{3,1},{4,6},{5,7},{6,4},{7,5},{8,10},{9,11},{10,... | collective-permute-start | bytes 20 | tf_op jit(solution)/shard_map/ppermute | solution.py:42
  140.0 3.4 %collective-permute-start.5 = (s32[1]{0:T(128)}, s32[1]{0:T(128)}, u32[]{:S(2)}, u32[]{:S(2)}) collective-permute-start(s32[1]{0:T(128)} %bitcast.13), channel_id=1, source_target_pairs={{0,3},{1,0},{2,1},{3,2},{4,7},{5,4},{6,5},{7,6},{8,11},{9,8},{10,9... | collective-permute-start | bytes 20 | tf_op jit(solution)/shard_map/ppermute | solution.py:42
  144.7 2.6 add_bitcast_fusion.1
  151.2 2.8 %collective-permute-start.6 = (s32[1]{0:T(128)}, s32[1]{0:T(128)}, u32[]{:S(2)}, u32[]{:S(2)}) collective-permute-start(s32[1]{0:T(128)} %bitcast.19), channel_id=1, source_target_pairs={{0,4},{4,8},{8,12},{12,0},{1,5},{5,9},{9,13},{13,1},{2,6},{6,10},{... | collective-permute-start | bytes 20 | tf_op jit(solution)/shard_map/ppermute | solution.py:42
  154.0 2.5 collective-permute-start.7
  156.4 3.4 %collective-permute-start.8 = (s32[1]{0:T(128)}, s32[1]{0:T(128)}, u32[]{:S(2)}, u32[]{:S(2)}) collective-permute-start(s32[1]{0:T(128)} %bitcast.19), channel_id=1, source_target_pairs={{0,12},{4,0},{8,4},{12,8},{1,13},{5,1},{9,5},{13,9},{2,14},{6,2},{... | collective-permute-start | bytes 20 | tf_op jit(solution)/shard_map/ppermute | solution.py:42
  160.1 2.0 add_bitcast_fusion.2
  166.0 1.9 compare_and_fusion
  169.1 1.7 copy.66
  171.2 1.6 copy.67
  172.7 1.5 copy.68
  174.2 30.5 %all-gather.5.cloned.1.call-done = bf16[2048,1024]{1,0:T(8,128)(2,1)} async-done(((bf16[128,1024]{1,0:T(8,128)(2,1)}), bf16[2048,1024]{1,0:T(8,128)(2,1)}) %all-gather.5.cloned.1.call-update) | async-done | bytes 4194320 | tf_op jit(solution)/shard_map/all_gather | solution.py:107
  204.7 4.6 %fusion.36 = (bf16[16,128,512]{2,1,0:T(8,128)(2,1)}, bf16[16,128,512]{2,1,0:T(8,128)(2,1)}) fusion(bf16[16,128,1024]{2,1,0:T(8,128)(2,1)} %bitcast.101), kind=kLoop, calls=%fused_computation.107 | loop fusion | bytes 8388608 | tf_op jit(solution)/shard_map/slice | solution.py:114
  209.3 2.5 reshape.452
  211.9 2.7 %copy.81 = bf16[2048,4,128]{0,2,1:T(8,128)(2,1)} copy(bf16[2048,4,128]{2,1,0:T(4,128)(2,1)S(1)} %reshape.452) | data formatting | bytes 4194304 | tf_op jit(solution)/shard_map/reshape | solution.py:111
  214.5 2.5 reshape.450
  217.1 12.0 %fusion = (f32[4,5,128]{2,1,0:T(8,128)S(1)}, f32[4,2048,128,5]{2,1,3,0:T(8,128)}) fusion(pred[128,2048]{0,1:T(8,128)(4,1)S(1)} %compare_and_fusion, f32[128,4,5,64]{3,0,2,1:T(8,128)} %copy.68, f32[128,4,5,64]{3,0,2,1:T(8,128)} %copy.67, f32[128,4,5]{0,2,1:T(8,128)S(1)} %rsqrt.21, bf16[2048,4,128]{0,2,1:T(8,128)(2,1)} %copy.81), kind=kOutput, calls=%fused_computation.5 | convolution fusion | flops 1358886400 | bytes 24662016 | tf_op jit(solution)/shard_map/qhgd,khd->hgqk/dot_general | solution.py:126
  229.1 9.2 %multiply_convert_fusion = bf16[128,4,5,128]{0,3,2,1:T(8,128)(2,1)S(1)} fusion(f32[4,2048,128,5]{2,1,3,0:T(8,128)} %get-tuple-element.37, pred[128,2048]{0,1:T(8,128)(4,1)S(1)} %compare_and_fusion, bf16[2048,4,128,1]{2,1,0,3:T(4,128)(2,1)S(1)} %bitcast.106, f32[128]{0:T(128)S(1)} %get-tuple-element.43, f32[128,4,5]{0,2,1:T(8,128)S(1)} %select_bitcast_fusion), kind=kOutput, calls=%fused_computation.22 | convolution fusion | flops 1358888960 | bytes 23996928 | tf_op jit(solution)/shard_map/hgqk,khd->qhgd/dot_general | solution.py:136
  238.7 5.0 %collective-permute-start.9 = (f32[64]{0:T(128)S(1)}, f32[64]{0:T(128)S(1)}, u32[]{:S(2)}, u32[]{:S(2)}) collective-permute-start(f32[64]{0:T(128)S(1)} %pad_maximum_fusion.6), channel_id=1, source_target_pairs={{0,1},{1,2},{2,3},{3,0},{4,5},{5,6},{6,7},{7,4},{8,9},{9,10},{10,1... | collective-permute-start | bytes 776 | tf_op jit(solution)/shard_map/ppermute | solution.py:42
  243.7 2.4 collective-permute-start.10
  246.2 1.9 collective-permute-start.11
  249.2 2.0 collective-permute-done.10
  251.8 1.5 collective-permute-start.12
  254.5 2.1 collective-permute-start.14
  256.6 1.9 collective-permute-done.13
  (99 shorter events, 20.9 us)
Async XLA Ops:
  7.2 2.2 copy-start.2
  7.2 110.5 %all-gather.3.cloned.1.call-start = ((), (), s32[]{:S(2)}) async-start(), calls=%async_computation | async-start | bytes 10321920 | tf_op jit(solution)/shard_map/all_gather | solution.py:89
  9.5 3.2 %copy-start.1 = (bf16[1,128,2560]{2,1,0:T(8,128)(2,1)S(1)}, bf16[1,128,2560]{2,1,0:T(8,128)(2,1)}, u32[]{:S(2)}) copy-start(bf16[1,128,2560]{2,1,0:T(8,128)(2,1)} %param.13) | copy-start | bytes 1966084
  9.5 2.1 collective-permute-start.1
  12.7 192.0 %all-gather.5.cloned.1.call-start = ((), (), s32[]{:S(2)}) async-start(), calls=%async_computation.1 | async-start | bytes 4456448 | tf_op jit(solution)/shard_map/all_gather | solution.py:107
  13.1 2.2 collective-permute-start
  123.8 0.7 copy-start.5
  124.0 2.6 collective-permute-start.2
  126.5 0.9 copy-start
  129.3 3.1 %copy-start.4 = (s32[1,128]{1,0:T(1,128)S(1)}, s32[1,128]{1,0:T(1,128)}, u32[]{:S(2)}) copy-start(s32[1,128]{1,0:T(1,128)} %param.16) | copy-start | bytes 1540
  129.3 14.1 %copy-start.3 = (bf16[2560]{0:T(1024)(128)(2,1)S(1)}, bf16[2560]{0:T(1024)(128)(2,1)}, u32[]{:S(2)}) copy-start(bf16[2560]{0:T(1024)(128)(2,1)} %param.21) | copy-start | bytes 15364
  134.4 9.9 %collective-permute-start.3 = (s32[1]{0:T(128)}, s32[1]{0:T(128)}, u32[]{:S(2)}, u32[]{:S(2)}) collective-permute-start(s32[1]{0:T(128)} %bitcast.13), channel_id=1, source_target_pairs={{0,1},{1,2},{2,3},{3,0},{4,5},{5,6},{6,7},{7,4},{8,9},{9,10},{10,1... | collective-permute-start | bytes 20 | tf_op jit(solution)/shard_map/ppermute | solution.py:42
  136.9 7.5 %collective-permute-start.4 = (s32[1]{0:T(128)}, s32[1]{0:T(128)}, u32[]{:S(2)}, u32[]{:S(2)}) collective-permute-start(s32[1]{0:T(128)} %bitcast.13), channel_id=1, source_target_pairs={{0,2},{1,3},{2,0},{3,1},{4,6},{5,7},{6,4},{7,5},{8,10},{9,11},{10,... | collective-permute-start | bytes 20 | tf_op jit(solution)/shard_map/ppermute | solution.py:42
  140.0 4.7 %collective-permute-start.5 = (s32[1]{0:T(128)}, s32[1]{0:T(128)}, u32[]{:S(2)}, u32[]{:S(2)}) collective-permute-start(s32[1]{0:T(128)} %bitcast.13), channel_id=1, source_target_pairs={{0,3},{1,0},{2,1},{3,2},{4,7},{5,4},{6,5},{7,6},{8,11},{9,8},{10,9... | collective-permute-start | bytes 20 | tf_op jit(solution)/shard_map/ppermute | solution.py:42
  151.2 8.7 %collective-permute-start.6 = (s32[1]{0:T(128)}, s32[1]{0:T(128)}, u32[]{:S(2)}, u32[]{:S(2)}) collective-permute-start(s32[1]{0:T(128)} %bitcast.19), channel_id=1, source_target_pairs={{0,4},{4,8},{8,12},{12,0},{1,5},{5,9},{9,13},{13,1},{2,6},{6,10},{... | collective-permute-start | bytes 20 | tf_op jit(solution)/shard_map/ppermute | solution.py:42
  154.0 5.8 %collective-permute-start.7 = (s32[1]{0:T(128)}, s32[1]{0:T(128)}, u32[]{:S(2)}, u32[]{:S(2)}) collective-permute-start(s32[1]{0:T(128)} %bitcast.19), channel_id=1, source_target_pairs={{0,8},{4,12},{8,0},{12,4},{1,9},{5,13},{9,1},{13,5},{2,10},{6,14},... | collective-permute-start | bytes 20 | tf_op jit(solution)/shard_map/ppermute | solution.py:42
  156.4 3.7 %collective-permute-start.8 = (s32[1]{0:T(128)}, s32[1]{0:T(128)}, u32[]{:S(2)}, u32[]{:S(2)}) collective-permute-start(s32[1]{0:T(128)} %bitcast.19), channel_id=1, source_target_pairs={{0,12},{4,0},{8,4},{12,8},{1,13},{5,1},{9,5},{13,9},{2,14},{6,2},{... | collective-permute-start | bytes 20 | tf_op jit(solution)/shard_map/ppermute | solution.py:42
  229.1 9.4 %copy-start.6 = (s32[1,128]{1,0:T(1,128)S(1)}, s32[1,128]{1,0:T(1,128)}, u32[]{:S(2)}) copy-start(s32[1,128]{1,0:T(1,128)} %param.17) | copy-start | bytes 1540
  238.7 10.5 %collective-permute-start.9 = (f32[64]{0:T(128)S(1)}, f32[64]{0:T(128)S(1)}, u32[]{:S(2)}, u32[]{:S(2)}) collective-permute-start(f32[64]{0:T(128)S(1)} %pad_maximum_fusion.6), channel_id=1, source_target_pairs={{0,1},{1,2},{2,3},{3,0},{4,5},{5,6},{6,7},{7,4},{8,9},{9,10},{10,1... | collective-permute-start | bytes 776 | tf_op jit(solution)/shard_map/ppermute | solution.py:42
  243.7 7.5 %collective-permute-start.10 = (f32[64]{0:T(128)S(1)}, f32[64]{0:T(128)S(1)}, u32[]{:S(2)}, u32[]{:S(2)}) collective-permute-start(f32[64]{0:T(128)S(1)} %pad_maximum_fusion.6), channel_id=1, source_target_pairs={{0,2},{1,3},{2,0},{3,1},{4,6},{5,7},{6,4},{7,5},{8,10},{9,11},{10,... | collective-permute-start | bytes 776 | tf_op jit(solution)/shard_map/ppermute | solution.py:42
  246.2 5.0 %collective-permute-start.11 = (f32[64]{0:T(128)S(1)}, f32[64]{0:T(128)S(1)}, u32[]{:S(2)}, u32[]{:S(2)}) collective-permute-start(f32[64]{0:T(128)S(1)} %pad_maximum_fusion.6), channel_id=1, source_target_pairs={{0,3},{1,0},{2,1},{3,2},{4,7},{5,4},{6,5},{7,6},{8,11},{9,8},{10,9... | collective-permute-start | bytes 776 | tf_op jit(solution)/shard_map/ppermute | solution.py:42
  251.8 4.7 %collective-permute-start.12 = (f32[64]{0:T(128)S(1)}, f32[64]{0:T(128)S(1)}, u32[]{:S(2)}, u32[]{:S(2)}) collective-permute-start(f32[64]{0:T(128)S(1)} %fusion.45), channel_id=1, source_target_pairs={{0,4},{4,8},{8,12},{12,0},{1,5},{5,9},{9,13},{13,1},{2,6},{6,10},{... | collective-permute-start | bytes 776 | tf_op jit(solution)/shard_map/ppermute | solution.py:42
  253.4 5.1 %collective-permute-start.13 = (f32[64]{0:T(128)S(1)}, f32[64]{0:T(128)S(1)}, u32[]{:S(2)}, u32[]{:S(2)}) collective-permute-start(f32[64]{0:T(128)S(1)} %fusion.45), channel_id=1, source_target_pairs={{0,8},{4,12},{8,0},{12,4},{1,9},{5,13},{9,1},{13,5},{2,10},{6,14},... | collective-permute-start | bytes 776 | tf_op jit(solution)/shard_map/ppermute | solution.py:42
  254.5 4.0 %collective-permute-start.14 = (f32[64]{0:T(128)S(1)}, f32[64]{0:T(128)S(1)}, u32[]{:S(2)}, u32[]{:S(2)}) collective-permute-start(f32[64]{0:T(128)S(1)} %fusion.45), channel_id=1, source_target_pairs={{0,12},{4,0},{8,4},{12,8},{1,13},{5,1},{9,5},{13,9},{2,14},{6,2},{... | collective-permute-start | bytes 776 | tf_op jit(solution)/shard_map/ppermute | solution.py:42
Sparse Core Ops, SparseCore 0:
  12.8 104.8 all-gather.2
  131.2 73.3 all-gather.4

commit v10 on v9

--- a/solution.py
+++ b/solution.py
@@ -103,17 +103,13 @@
         query = full[:, :q_width]
         key_norm = rotary_then_norm(full[:, q_width : q_width + kv_width], token_places, KEY_VALUE_HEADS)
         value_rows = full[:, q_width + kv_width :].astype(jnp.bfloat16)
-        own_block = jnp.concatenate([key_norm, value_rows], axis=1)
-        gathered = lax.all_gather(own_block, ("cx", "cz"), axis=0, tiled=True).reshape(
-            shards, token_slots, 2 * kv_width
-        )
+        key_t = key_norm.reshape(token_slots, KEY_VALUE_HEADS, HEAD_SIZE).transpose(1, 2, 0)
+        value_t = value_rows.reshape(token_slots, KEY_VALUE_HEADS, HEAD_SIZE).transpose(1, 2, 0)
+        own_block = jnp.concatenate([key_t, value_t], axis=0)
+        gathered = lax.all_gather(own_block, ("cx", "cz"), axis=2, tiled=True)
         key_count = shards * token_slots
-        key_portion = gathered[:, :token_slots, :kv_width].reshape(
-            key_count, KEY_VALUE_HEADS, HEAD_SIZE
-        )
-        value_portion = gathered[:, :token_slots, kv_width:].reshape(
-            key_count, KEY_VALUE_HEADS, HEAD_SIZE
-        )
+        key_portion = gathered[:KEY_VALUE_HEADS]
+        value_portion = gathered[KEY_VALUE_HEADS:]
         kpos = (starts[:, None] + offsets[None, :]).reshape(key_count)
         kseg = (kpos >= doc_edge).astype(jnp.int32)
         klive = (offsets[None, :] < counts[:, None]).reshape(key_count)
@@ -124,7 +120,7 @@
         per_head_queries = query_norm.reshape(token_slots, KEY_VALUE_HEADS, head_group, HEAD_SIZE)
 
         scores = jnp.einsum(
-            "qhgd,khd->hgqk",
+            "qhgd,hdk->hgqk",
             per_head_queries,
             key_portion,
             preferred_element_type=jnp.float32,
@@ -134,7 +130,7 @@
         weights = jnp.where(allowed[None, None], jnp.exp(scores), 0.0)
         denom = jnp.sum(weights, axis=-1)
         numer = jnp.einsum(
-            "hgqk,khd->qhgd",
+            "hgqk,hdk->qhgd",
             weights.astype(jnp.bfloat16),
             value_portion,
             preferred_element_type=jnp.float32,

time: 268 us -> 254 us (0.948)
  local copies, waits for them, and re-layouts: 28.8 us -> 15.6 us
    reshape x3 -> x0, local copies, waits for them, and re-layouts: 7.76 us -> none  [the longest x2 5.22 us: per_device(): gathered[:, :token_slots, :kv_width]]
    slice x2 -> x1, local copies, waits for them, and re-layouts: 4.67 us -> 0.2 us  [rotary_then_norm(): leading_block = shaped[..., :half]]
  transfers between devices with their start and end apart: 17 -> 17, of which waited for: 10 -> 8; matrix products, arithmetic and copies ran while one was open for 9% -> 9% of each run, Pallas kernels for 0% -> 0%
where the time goes in v10:
time: 254 us; the launch traced here: 253 us
  waiting for transfers between devices  142 us (56%)
  starting transfers between devices  32 us (13%)
  matrix products  26.7 us (11%)
  between operations  20.3 us (8%)
  other arithmetic  16.3 us (6%)
  local copies, waits for them, and re-layouts  15.6 us (6%)
    all_gather x1, waiting for transfers between devices, per_device(): half_weights = lax.all_gather(rows_block, ('dz', 'dy'), axis=0, tiled=True)  102 us
    all_gather x1, waiting for transfers between devices, per_device(): gathered = lax.all_gather(own_block, ('cx', 'cz'), axis=2, tiled=True)  32.1 us
    ppermute x12, starting transfers between devices, ctx_sum(): parts.append(lax.ppermute(total, axis, pairs))  31.5 us
    dot_general x1, matrix products, per_device(): jnp.einsum('qhgd,hdk->hgqk', per_head_queries, key_portion, preferred_ele...  11.3 us
    dot_general x1, matrix products, per_device(): jnp.einsum('hgqk,hdk->qhgd', weights.astype(jnp.bfloat16), value_portion,...  9.08 us
    dot_general x1, matrix products, per_device(): projected = jnp.dot(both, half_weights, preferred_element_type=jnp.float32)  6.17 us
  transfers between devices with their start and end apart: 17, of which 8 were waited for; matrix products, arithmetic and copies ran while one was open for 9% of the time, Pallas kernels for 0%

profile of v10, /device:TPU:2, one launch (start us, length us, event | category | flops | bytes accessed | tf_op | source)
XLA Modules:
  0.0 252.9 jit_solution(14716008330005083120)
XLA Ops:
  7.2 1.2 constant_dynamic-update-slice_fusion.2
  9.6 2.0 collective-permute-done.1
  11.6 1.1 pad_maximum_fusion.1
  13.3 2.0 collective-permute-done
  15.7 101.9 %all-gather.3.cloned.1.call-done = bf16[2560,1792]{1,0:T(8,128)(2,1)} async-done(((bf16[320,1792]{1,0:T(8,128)(2,1)}), bf16[2560,1792]{1,0:T(8,128)(2,1)}) %all-gather.3.cloned.1.call-update) | async-done | bytes 9175056 | tf_op jit(solution)/shard_map/all_gather | solution.py:89
  117.7 6.2 %fusion.36 = f32[256,1792]{1,0:T(8,128)S(1)} fusion(bf16[256,2560]{0,1:T(8,128)(2,1)S(1)} %bitcast.109, bf16[2560,1792]{1,0:T(8,128)(2,1)} %all-gather.3.cloned.1.call-done), kind=kOutput, calls=%fused_computation.113 | convolution fusion | flops 2348810240 | bytes 12320768 | tf_op jit(solution)/shard_map/dot_general | solution.py:95
  127.5 1.7 maximum_select_fusion
  131.5 1.3 fusion.23
  132.8 2.5 %collective-permute-start.3 = (s32[1]{0:T(128)}, s32[1]{0:T(128)}, u32[]{:S(2)}, u32[]{:S(2)}) collective-permute-start(s32[1]{0:T(128)} %bitcast.14), channel_id=1, source_target_pairs={{0,1},{1,2},{2,3},{3,0},{4,5},{5,6},{6,7},{7,4},{8,9},{9,10},{10,1... | collective-permute-start | bytes 20 | tf_op jit(solution)/shard_map/ppermute | solution.py:42
  135.4 3.0 %collective-permute-start.4 = (s32[1]{0:T(128)}, s32[1]{0:T(128)}, u32[]{:S(2)}, u32[]{:S(2)}) collective-permute-start(s32[1]{0:T(128)} %bitcast.14), channel_id=1, source_target_pairs={{0,2},{1,3},{2,0},{3,1},{4,6},{5,7},{6,4},{7,5},{8,10},{9,11},{10,... | collective-permute-start | bytes 20 | tf_op jit(solution)/shard_map/ppermute | solution.py:42
  138.4 3.4 %collective-permute-start.5 = (s32[1]{0:T(128)}, s32[1]{0:T(128)}, u32[]{:S(2)}, u32[]{:S(2)}) collective-permute-start(s32[1]{0:T(128)} %bitcast.14), channel_id=1, source_target_pairs={{0,3},{1,0},{2,1},{3,2},{4,7},{5,4},{6,5},{7,6},{8,11},{9,8},{10,9... | collective-permute-start | bytes 20 | tf_op jit(solution)/shard_map/ppermute | solution.py:42
  144.1 2.6 %add_bitcast_fusion.1 = s32[4]{0:T(128)S(1)} fusion(s32[1,1]{0,1:T(1,128)} %bitcast.17, s32[1,1]{0,1:T(1,128)} %bitcast.16, s32[1,1]{0,1:T(1,128)} %bitcast.15, s32[1,1]{0,1:T(1,128)} %bitcast.13), kind=kLoop, calls=%fused_computation.92 | loop fusion | flops 12 | bytes 32 | tf_op jit(solution)/shard_map/jit(_take)/Arg_0.15 | solution.py:44
  150.6 2.8 %collective-permute-start.6 = (s32[1]{0:T(128)}, s32[1]{0:T(128)}, u32[]{:S(2)}, u32[]{:S(2)}) collective-permute-start(s32[1]{0:T(128)} %bitcast.20), channel_id=1, source_target_pairs={{0,4},{4,8},{8,12},{12,0},{1,5},{5,9},{9,13},{13,1},{2,6},{6,10},{... | collective-permute-start | bytes 20 | tf_op jit(solution)/shard_map/ppermute | solution.py:42
  153.5 2.5 collective-permute-start.7
  155.9 3.4 %collective-permute-start.8 = (s32[1]{0:T(128)}, s32[1]{0:T(128)}, u32[]{:S(2)}, u32[]{:S(2)}) collective-permute-start(s32[1]{0:T(128)} %bitcast.20), channel_id=1, source_target_pairs={{0,12},{4,0},{8,4},{12,8},{1,13},{5,1},{9,5},{13,9},{2,14},{6,2},{... | collective-permute-start | bytes 20 | tf_op jit(solution)/shard_map/ppermute | solution.py:42
  159.5 2.0 add_bitcast_fusion.2
  165.4 1.9 compare_and_fusion
  167.3 1.2 slice.135
  168.5 1.7 copy.56
  171.0 1.6 copy.58
  172.6 32.1 %all-gather.5.cloned.1.call-done = bf16[8,128,2048]{1,2,0:T(8,128)(2,1)} async-done(((bf16[8,128,128]{1,2,0:T(8,128)(2,1)}), bf16[8,128,2048]{1,2,0:T(8,128)(2,1)}) %all-gather.5.cloned.1.call-update) | async-done | bytes 4194320 | tf_op jit(solution)/shard_map/all_gather | solution.py:109
  204.7 11.3 %fusion = (f32[4,5,128]{2,1,0:T(8,128)S(1)}, f32[4,2048,128,5]{2,1,3,0:T(8,128)}) fusion(pred[128,2048]{0,1:T(8,128)(4,1)S(1)} %compare_and_fusion, f32[128,4,5,64]{3,0,2,1:T(8,128)} %copy.58, f32[128,4,5,64]{3,0,2,1:T(8,128)S(1)} %copy.57, f32[128,4,5]{0,2,1:T(8,128)S(1)} %rsqrt.21, bf16[8,128,2048]{1,2,0:T(8,128)(2,1)} %all-gather.5.cloned.1.call-done), kind=kOutput, calls=%fused_computation.5 | convolution fusion | flops 1358886400 | bytes 25317376 | tf_op jit(solution)/shard_map/qhgd,hdk->hgqk/dot_general | solution.py:122
  216.0 9.1 %multiply_convert_fusion = bf16[128,4,5,128]{0,3,2,1:T(8,128)(2,1)S(1)} fusion(f32[4,2048,128,5]{2,1,3,0:T(8,128)} %get-tuple-element.35, pred[128,2048]{0,1:T(8,128)(4,1)S(1)} %compare_and_fusion, bf16[8,128,2048]{1,2,0:T(8,128)(2,1)S(1)} %copy-done.7, f32[128]{0:T(128)S(1)} %get-tuple-element.39, f32[128,4,5]{0,2,1:T(8,128)S(1)} %select_bitcast_fusion), kind=kOutput, calls=%fused_computation.22 | convolution fusion | flops 1358888960 | bytes 24003072 | tf_op jit(solution)/shard_map/hgqk,hdk->qhgd/dot_general | solution.py:132
  225.5 4.7 %collective-permute-start.9 = (f32[64]{0:T(128)S(1)}, f32[64]{0:T(128)S(1)}, u32[]{:S(2)}, u32[]{:S(2)}) collective-permute-start(f32[64]{0:T(128)S(1)} %pad_maximum_fusion.6), channel_id=1, source_target_pairs={{0,1},{1,2},{2,3},{3,0},{4,5},{5,6},{6,7},{7,4},{8,9},{9,10},{10,1... | collective-permute-start | bytes 776 | tf_op jit(solution)/shard_map/ppermute | solution.py:42
  230.1 2.5 collective-permute-start.10
  232.6 1.9 collective-permute-start.11
  234.5 1.1 copy.61
  235.7 2.0 collective-permute-done.10
  238.3 1.5 collective-permute-start.12
  239.8 1.1 collective-permute-start.13
  240.9 2.2 collective-permute-start.14
  243.1 1.8 collective-permute-done.13
  (98 shorter events, 15.5 us)
Async XLA Ops:
  7.2 2.2 copy-start.2
  7.2 110.5 %all-gather.3.cloned.1.call-start = ((), (), s32[]{:S(2)}) async-start(), calls=%async_computation | async-start | bytes 10321920 | tf_op jit(solution)/shard_map/all_gather | solution.py:89
  9.5 3.2 %copy-start.1 = (bf16[1,128,2560]{2,1,0:T(8,128)(2,1)S(1)}, bf16[1,128,2560]{2,1,0:T(8,128)(2,1)}, u32[]{:S(2)}) copy-start(bf16[1,128,2560]{2,1,0:T(8,128)(2,1)} %param.13) | copy-start | bytes 1966084
  9.5 2.1 collective-permute-start.1
  12.7 192.0 %all-gather.5.cloned.1.call-start = ((), (), s32[]{:S(2)}) async-start(), calls=%async_computation.1 | async-start | bytes 4456448 | tf_op jit(solution)/shard_map/all_gather | solution.py:109
  13.1 2.2 collective-permute-start
  123.8 0.7 copy-start.4
  124.0 2.6 %collective-permute-start.2 = (f32[128,1792]{1,0:T(8,128)S(1)}, f32[128,1792]{1,0:T(8,128)S(1)}, u32[]{:S(2)}, u32[]{:S(2)}) collective-permute-start(f32[128,1792]{1,0:T(8,128)S(1)} %get-tuple-element.15), channel_id=1, source_target_pairs={{0,16},{16,0},{1,17},{17,1},{2,18},{18,2},{3,19},{19,3},{4,20},{20... | collective-permute-start | bytes 2752520 | tf_op jit(solution)/shard_map/ppermute | solution.py:96
  126.5 0.9 copy-start
  129.5 1.9 copy-start.5
  129.5 12.9 %copy-start.3 = (bf16[2560]{0:T(1024)(128)(2,1)S(1)}, bf16[2560]{0:T(1024)(128)(2,1)}, u32[]{:S(2)}) copy-start(bf16[2560]{0:T(1024)(128)(2,1)} %param.21) | copy-start | bytes 15364
  132.8 11.2 %collective-permute-start.3 = (s32[1]{0:T(128)}, s32[1]{0:T(128)}, u32[]{:S(2)}, u32[]{:S(2)}) collective-permute-start(s32[1]{0:T(128)} %bitcast.14), channel_id=1, source_target_pairs={{0,1},{1,2},{2,3},{3,0},{4,5},{5,6},{6,7},{7,4},{8,9},{9,10},{10,1... | collective-permute-start | bytes 20 | tf_op jit(solution)/shard_map/ppermute | solution.py:42
  135.4 8.7 %collective-permute-start.4 = (s32[1]{0:T(128)}, s32[1]{0:T(128)}, u32[]{:S(2)}, u32[]{:S(2)}) collective-permute-start(s32[1]{0:T(128)} %bitcast.14), channel_id=1, source_target_pairs={{0,2},{1,3},{2,0},{3,1},{4,6},{5,7},{6,4},{7,5},{8,10},{9,11},{10,... | collective-permute-start | bytes 20 | tf_op jit(solution)/shard_map/ppermute | solution.py:42
  138.4 5.7 %collective-permute-start.5 = (s32[1]{0:T(128)}, s32[1]{0:T(128)}, u32[]{:S(2)}, u32[]{:S(2)}) collective-permute-start(s32[1]{0:T(128)} %bitcast.14), channel_id=1, source_target_pairs={{0,3},{1,0},{2,1},{3,2},{4,7},{5,4},{6,5},{7,6},{8,11},{9,8},{10,9... | collective-permute-start | bytes 20 | tf_op jit(solution)/shard_map/ppermute | solution.py:42
  150.6 8.7 %collective-permute-start.6 = (s32[1]{0:T(128)}, s32[1]{0:T(128)}, u32[]{:S(2)}, u32[]{:S(2)}) collective-permute-start(s32[1]{0:T(128)} %bitcast.20), channel_id=1, source_target_pairs={{0,4},{4,8},{8,12},{12,0},{1,5},{5,9},{9,13},{13,1},{2,6},{6,10},{... | collective-permute-start | bytes 20 | tf_op jit(solution)/shard_map/ppermute | solution.py:42
  153.5 5.8 %collective-permute-start.7 = (s32[1]{0:T(128)}, s32[1]{0:T(128)}, u32[]{:S(2)}, u32[]{:S(2)}) collective-permute-start(s32[1]{0:T(128)} %bitcast.20), channel_id=1, source_target_pairs={{0,8},{4,12},{8,0},{12,4},{1,9},{5,13},{9,1},{13,5},{2,10},{6,14},... | collective-permute-start | bytes 20 | tf_op jit(solution)/shard_map/ppermute | solution.py:42
  155.9 3.5 %collective-permute-start.8 = (s32[1]{0:T(128)}, s32[1]{0:T(128)}, u32[]{:S(2)}, u32[]{:S(2)}) collective-permute-start(s32[1]{0:T(128)} %bitcast.20), channel_id=1, source_target_pairs={{0,12},{4,0},{8,4},{12,8},{1,13},{5,1},{9,5},{13,9},{2,14},{6,2},{... | collective-permute-start | bytes 20 | tf_op jit(solution)/shard_map/ppermute | solution.py:42
  204.7 11.3 %copy-start.7 = (bf16[8,128,2048]{1,2,0:T(8,128)(2,1)S(1)}, bf16[8,128,2048]{1,2,0:T(8,128)(2,1)}, u32[]{:S(2)}) copy-start(bf16[8,128,2048]{1,2,0:T(8,128)(2,1)} %all-gather.5.cloned.1.call-done) | copy-start | bytes 12582916
  215.9 9.3 %copy-start.6 = (s32[1,128]{1,0:T(1,128)S(1)}, s32[1,128]{1,0:T(1,128)}, u32[]{:S(2)}) copy-start(s32[1,128]{1,0:T(1,128)} %param.17) | copy-start | bytes 1540
  225.5 10.2 %collective-permute-start.9 = (f32[64]{0:T(128)S(1)}, f32[64]{0:T(128)S(1)}, u32[]{:S(2)}, u32[]{:S(2)}) collective-permute-start(f32[64]{0:T(128)S(1)} %pad_maximum_fusion.6), channel_id=1, source_target_pairs={{0,1},{1,2},{2,3},{3,0},{4,5},{5,6},{6,7},{7,4},{8,9},{9,10},{10,1... | collective-permute-start | bytes 776 | tf_op jit(solution)/shard_map/ppermute | solution.py:42
  230.1 7.5 %collective-permute-start.10 = (f32[64]{0:T(128)S(1)}, f32[64]{0:T(128)S(1)}, u32[]{:S(2)}, u32[]{:S(2)}) collective-permute-start(f32[64]{0:T(128)S(1)} %pad_maximum_fusion.6), channel_id=1, source_target_pairs={{0,2},{1,3},{2,0},{3,1},{4,6},{5,7},{6,4},{7,5},{8,10},{9,11},{10,... | collective-permute-start | bytes 776 | tf_op jit(solution)/shard_map/ppermute | solution.py:42
  232.6 5.0 %collective-permute-start.11 = (f32[64]{0:T(128)S(1)}, f32[64]{0:T(128)S(1)}, u32[]{:S(2)}, u32[]{:S(2)}) collective-permute-start(f32[64]{0:T(128)S(1)} %pad_maximum_fusion.6), channel_id=1, source_target_pairs={{0,3},{1,0},{2,1},{3,2},{4,7},{5,4},{6,5},{7,6},{8,11},{9,8},{10,9... | collective-permute-start | bytes 776 | tf_op jit(solution)/shard_map/ppermute | solution.py:42
  238.3 4.8 %collective-permute-start.12 = (f32[64]{0:T(128)S(1)}, f32[64]{0:T(128)S(1)}, u32[]{:S(2)}, u32[]{:S(2)}) collective-permute-start(f32[64]{0:T(128)S(1)} %fusion.41), channel_id=1, source_target_pairs={{0,4},{4,8},{8,12},{12,0},{1,5},{5,9},{9,13},{13,1},{2,6},{6,10},{... | collective-permute-start | bytes 776 | tf_op jit(solution)/shard_map/ppermute | solution.py:42
  239.8 5.1 %collective-permute-start.13 = (f32[64]{0:T(128)S(1)}, f32[64]{0:T(128)S(1)}, u32[]{:S(2)}, u32[]{:S(2)}) collective-permute-start(f32[64]{0:T(128)S(1)} %fusion.41), channel_id=1, source_target_pairs={{0,8},{4,12},{8,0},{12,4},{1,9},{5,13},{9,1},{13,5},{2,10},{6,14},... | collective-permute-start | bytes 776 | tf_op jit(solution)/shard_map/ppermute | solution.py:42
  240.9 4.0 %collective-permute-start.14 = (f32[64]{0:T(128)S(1)}, f32[64]{0:T(128)S(1)}, u32[]{:S(2)}, u32[]{:S(2)}) collective-permute-start(f32[64]{0:T(128)S(1)} %fusion.41), channel_id=1, source_target_pairs={{0,12},{4,0},{8,4},{12,8},{1,13},{5,1},{9,5},{13,9},{2,14},{6,2},{... | collective-permute-start | bytes 776 | tf_op jit(solution)/shard_map/ppermute | solution.py:42
Sparse Core Ops, SparseCore 0:
  12.8 104.8 all-gather.2
  131.0 73.6 all-gather.4

commit v11 on v10

--- a/solution.py
+++ b/solution.py
@@ -78,7 +78,7 @@
         q_width = QUERY_HEADS * HEAD_SIZE
         core = lax.axis_index("dc")
         swap = [(0, 1), (1, 0)]
-        weights_local = jnp.concatenate([query_weight, key_matrix, value_matrix], axis=1)
+        weights_local = jnp.concatenate([key_matrix, value_matrix, query_weight], axis=1)
         half = weights_local.shape[1] // 2
         chunk = weights_local.shape[0]
         mine_half = lax.dynamic_slice_in_dim(weights_local, core * half, half, axis=1)
@@ -92,17 +92,22 @@
         paired = both.reshape(2 * token_slots, features // (2 * chunk), 2, chunk)
         paired = jnp.where(core == 0, paired, paired[:, :, ::-1, :])
         both = paired.reshape(2 * token_slots, features)
-        projected = jnp.dot(both, half_weights, preferred_element_type=jnp.float32)
-        returned = lax.ppermute(projected[token_slots:], "dc", swap)
-        own_part = projected[:token_slots]
+        split_at = 2 * kv_width
+        projected_kv = jnp.dot(both, half_weights[:, :split_at], preferred_element_type=jnp.float32)
+        returned_kv = lax.ppermute(projected_kv[token_slots:], "dc", swap)
+        projected_rest = jnp.dot(both, half_weights[:, split_at:], preferred_element_type=jnp.float32)
+        returned_rest = lax.ppermute(projected_rest[token_slots:], "dc", swap)
+        own_kv = projected_kv[:token_slots]
+        own_rest = projected_rest[:token_slots]
+        kv_rows = jnp.where(core == 0, own_kv, returned_kv)
         full = jnp.where(
             core == 0,
-            jnp.concatenate([own_part, returned], axis=1),
-            jnp.concatenate([returned, own_part], axis=1),
+            jnp.concatenate([own_kv, own_rest, returned_kv, returned_rest], axis=1),
+            jnp.concatenate([returned_kv, returned_rest, own_kv, own_rest], axis=1),
         )
-        query = full[:, :q_width]
-        key_norm = rotary_then_norm(full[:, q_width : q_width + kv_width], token_places, KEY_VALUE_HEADS)
-        value_rows = full[:, q_width + kv_width :].astype(jnp.bfloat16)
+        query = full[:, 2 * kv_width :]
+        key_norm = rotary_then_norm(kv_rows[:, :kv_width], token_places, KEY_VALUE_HEADS)
+        value_rows = kv_rows[:, kv_width:].astype(jnp.bfloat16)
         key_t = key_norm.reshape(token_slots, KEY_VALUE_HEADS, HEAD_SIZE).transpose(1, 2, 0)
         value_t = value_rows.reshape(token_slots, KEY_VALUE_HEADS, HEAD_SIZE).transpose(1, 2, 0)
         own_block = jnp.concatenate([key_t, value_t], axis=0)

time: 254 us -> 250 us (0.984)
  local copies, waits for them, and re-layouts: 15.6 us -> 12.6 us
    dot_general x1 -> x2, matrix products: 6.17 us -> 7.77 us  [the longest x1 4.04 us: per_device(): jnp.dot(both, half_weights[:, :split_at], preferred_element_type=jnp.floa...]
  transfers between devices with their start and end apart: 17 -> 18, of which waited for: 8 -> 8; matrix products, arithmetic and copies ran while one was open for 9% -> 9% of each run, Pallas kernels for 0% -> 0%
where the time goes in v11:
time: 250 us; the launch traced here: 249 us
  waiting for transfers between devices  141 us (56%)
  starting transfers between devices  32.1 us (13%)
  matrix products  28.4 us (11%)
  between operations  20.2 us (8%)
  other arithmetic  14.6 us (6%)
  local copies, waits for them, and re-layouts  12.6 us (5%)
    all_gather x1, waiting for transfers between devices, per_device(): half_weights = lax.all_gather(rows_block, ('dz', 'dy'), axis=0, tiled=True)  102 us
    ppermute x12, starting transfers between devices, ctx_sum(): parts.append(lax.ppermute(total, axis, pairs))  31.4 us
    all_gather x1, waiting for transfers between devices, per_device(): gathered = lax.all_gather(own_block, ('cx', 'cz'), axis=2, tiled=True)  30.7 us
    dot_general x1, matrix products, per_device(): jnp.einsum('qhgd,hdk->hgqk', per_head_queries, key_portion, preferred_ele...  11.3 us
    dot_general x1, matrix products, per_device(): jnp.einsum('hgqk,hdk->qhgd', weights.astype(jnp.bfloat16), value_portion,...  9.08 us
  transfers between devices with their start and end apart: 18, of which 8 were waited for; matrix products, arithmetic and copies ran while one was open for 9% of the time, Pallas kernels for 0%

profile of v11, /device:TPU:2, one launch (start us, length us, event | category | flops | bytes accessed | tf_op | source)
XLA Modules:
  0.0 248.5 jit_solution(8341229733553863861)
XLA Ops:
  7.2 0.9 constant_dynamic-update-slice_fusion.2
  8.1 0.9 constant_dynamic-update-slice_fusion.1
  9.1 1.2 constant_dynamic-update-slice_fusion
  10.5 2.0 collective-permute-done.1
  12.4 1.1 pad_maximum_fusion.7
  14.6 1.7 collective-permute-done
  16.8 101.8 %all-gather.3.cloned.1.call-done = bf16[2560,1792]{1,0:T(8,128)(2,1)} async-done(((bf16[320,1792]{1,0:T(8,128)(2,1)}), bf16[2560,1792]{1,0:T(8,128)(2,1)}) %all-gather.3.cloned.1.call-update) | async-done | bytes 9175056 | tf_op jit(solution)/shard_map/all_gather | solution.py:89
  118.6 4.0 %fusion.7 = f32[256,1024]{1,0:T(8,128)S(1)} fusion(bf16[256,2560]{0,1:T(8,128)(2,1)S(1)} %bitcast.116, bf16[2560,1792]{1,0:T(8,128)(2,1)} %all-gather.3.cloned.1.call-done), kind=kOutput, calls=%fused_computation.11 | convolution fusion | flops 1342177280 | bytes 7602176 | tf_op jit(solution)/shard_map/dot_general | solution.py:96
  127.1 1.3 fusion.28
  128.3 2.5 %collective-permute-start.3 = (s32[1]{0:T(128)}, s32[1]{0:T(128)}, u32[]{:S(2)}, u32[]{:S(2)}) collective-permute-start(s32[1]{0:T(128)} %bitcast.14), channel_id=1, source_target_pairs={{0,1},{1,2},{2,3},{3,0},{4,5},{5,6},{6,7},{7,4},{8,9},{9,10},{10,1... | collective-permute-start | bytes 20 | tf_op jit(solution)/shard_map/ppermute | solution.py:42
  130.9 3.0 %collective-permute-start.4 = (s32[1]{0:T(128)}, s32[1]{0:T(128)}, u32[]{:S(2)}, u32[]{:S(2)}) collective-permute-start(s32[1]{0:T(128)} %bitcast.14), channel_id=1, source_target_pairs={{0,2},{1,3},{2,0},{3,1},{4,6},{5,7},{6,4},{7,5},{8,10},{9,11},{10,... | collective-permute-start | bytes 20 | tf_op jit(solution)/shard_map/ppermute | solution.py:42
  133.9 3.4 %collective-permute-start.5 = (s32[1]{0:T(128)}, s32[1]{0:T(128)}, u32[]{:S(2)}, u32[]{:S(2)}) collective-permute-start(s32[1]{0:T(128)} %bitcast.14), channel_id=1, source_target_pairs={{0,3},{1,0},{2,1},{3,2},{4,7},{5,4},{6,5},{7,6},{8,11},{9,8},{10,9... | collective-permute-start | bytes 20 | tf_op jit(solution)/shard_map/ppermute | solution.py:42
  139.5 2.6 %add_bitcast_fusion.1 = s32[4]{0:T(128)S(1)} fusion(s32[1,1]{0,1:T(1,128)} %bitcast.17, s32[1,1]{0,1:T(1,128)} %bitcast.16, s32[1,1]{0,1:T(1,128)} %bitcast.15, s32[1,1]{0,1:T(1,128)} %bitcast.13), kind=kLoop, calls=%fused_computation.103 | loop fusion | flops 12 | bytes 32 | tf_op jit(solution)/shard_map/jit(_take)/Arg_0.15 | solution.py:44
  145.9 2.8 %collective-permute-start.6 = (s32[1]{0:T(128)}, s32[1]{0:T(128)}, u32[]{:S(2)}, u32[]{:S(2)}) collective-permute-start(s32[1]{0:T(128)} %bitcast.20), channel_id=1, source_target_pairs={{0,4},{4,8},{8,12},{12,0},{1,5},{5,9},{9,13},{13,1},{2,6},{6,10},{... | collective-permute-start | bytes 20 | tf_op jit(solution)/shard_map/ppermute | solution.py:42
  148.8 2.5 collective-permute-start.7
  151.2 3.4 %collective-permute-start.8 = (s32[1]{0:T(128)}, s32[1]{0:T(128)}, u32[]{:S(2)}, u32[]{:S(2)}) collective-permute-start(s32[1]{0:T(128)} %bitcast.20), channel_id=1, source_target_pairs={{0,12},{4,0},{8,4},{12,8},{1,13},{5,1},{9,5},{13,9},{2,14},{6,2},{... | collective-permute-start | bytes 20 | tf_op jit(solution)/shard_map/ppermute | solution.py:42
  154.9 1.9 add_bitcast_fusion.2
  160.7 3.7 %fusion.9 = f32[256,768]{1,0:T(8,128)S(1)} fusion(bf16[256,2560]{0,1:T(8,128)(2,1)} %bitcast.117, bf16[2560,1792]{1,0:T(8,128)(2,1)} %all-gather.3.cloned.1.call-done), kind=kOutput, calls=%fused_computation.13 | convolution fusion | flops 1006632960 | bytes 6029312 | tf_op jit(solution)/shard_map/dot_general | solution.py:98
  164.8 1.9 compare_and_fusion
  168.1 1.6 copy.58
  169.6 30.7 %all-gather.5.cloned.1.call-done = bf16[8,128,2048]{1,2,0:T(8,128)(2,1)} async-done(((bf16[8,128,128]{1,2,0:T(8,128)(2,1)}), bf16[8,128,2048]{1,2,0:T(8,128)(2,1)}) %all-gather.5.cloned.1.call-update) | async-done | bytes 4194320 | tf_op jit(solution)/shard_map/all_gather | solution.py:114
  200.3 11.3 %fusion = (f32[4,5,128]{2,1,0:T(8,128)S(1)}, f32[4,2048,128,5]{2,1,3,0:T(8,128)}) fusion(pred[128,2048]{0,1:T(8,128)(4,1)S(1)} %compare_and_fusion, f32[128,4,5,64]{3,0,2,1:T(8,128)} %copy.58, f32[128,4,5,64]{3,0,2,1:T(8,128)S(1)} %copy.57, f32[128,4,5]{0,2,1:T(8,128)S(1)} %rsqrt.21, bf16[8,128,2048]{1,2,0:T(8,128)(2,1)} %all-gather.5.cloned.1.call-done), kind=kOutput, calls=%fused_computation.5 | convolution fusion | flops 1358886400 | bytes 25317376 | tf_op jit(solution)/shard_map/qhgd,hdk->hgqk/dot_general | solution.py:127
  211.6 9.1 %multiply_convert_fusion = bf16[128,4,5,128]{0,3,2,1:T(8,128)(2,1)S(1)} fusion(f32[4,2048,128,5]{2,1,3,0:T(8,128)} %get-tuple-element.37, pred[128,2048]{0,1:T(8,128)(4,1)S(1)} %compare_and_fusion, bf16[8,128,2048]{1,2,0:T(8,128)(2,1)S(1)} %copy-done.6, f32[128]{0:T(128)S(1)} %get-tuple-element.41, f32[128,4,5]{0,2,1:T(8,128)S(1)} %select_bitcast_fusion), kind=kOutput, calls=%fused_computation.32 | convolution fusion | flops 1358888960 | bytes 24003072 | tf_op jit(solution)/shard_map/hgqk,hdk->qhgd/dot_general | solution.py:137
  221.2 4.6 %collective-permute-start.10 = (f32[64]{0:T(128)S(1)}, f32[64]{0:T(128)S(1)}, u32[]{:S(2)}, u32[]{:S(2)}) collective-permute-start(f32[64]{0:T(128)S(1)} %pad_maximum_fusion.12), channel_id=1, source_target_pairs={{0,1},{1,2},{2,3},{3,0},{4,5},{5,6},{6,7},{7,4},{8,9},{9,10},{10,1... | collective-permute-start | bytes 776 | tf_op jit(solution)/shard_map/ppermute | solution.py:42
  225.7 2.5 collective-permute-start.11
  228.2 2.0 collective-permute-start.12
  230.2 1.1 copy.61
  231.3 2.0 collective-permute-done.11
  233.9 1.5 collective-permute-start.13
  235.4 1.2 collective-permute-start.14
  236.5 2.1 collective-permute-start.15
  238.6 1.8 collective-permute-done.14
  (100 shorter events, 14.4 us)
Async XLA Ops:
  7.2 111.4 %all-gather.3.cloned.1.call-start = ((), (), s32[]{:S(2)}) async-start(), calls=%async_computation | async-start | bytes 10321920 | tf_op jit(solution)/shard_map/all_gather | solution.py:89
  10.4 2.1 collective-permute-start.1
  12.4 1.3 copy-start.1
  13.5 0.8 copy-start.3
  13.6 186.7 %all-gather.5.cloned.1.call-start = ((), (), s32[]{:S(2)}) async-start(), calls=%async_computation.1 | async-start | bytes 4456448 | tf_op jit(solution)/shard_map/all_gather | solution.py:114
  14.1 2.2 collective-permute-start
  16.8 105.8 %copy-start = (bf16[256,8,2,160]{0,3,2,1:T(8,128)(2,1)}, bf16[256,8,2,160]{0,3,2,1:T(8,128)(2,1)S(1)}, u32[]{:S(2)}) copy-start(bf16[256,8,2,160]{0,3,2,1:T(8,128)(2,1)S(1)} %reverse_select_fusion) | copy-start | bytes 3932164
  122.7 2.0 collective-permute-start.2
  125.1 1.9 copy-start.4
  125.1 12.8 %copy-start.2 = (bf16[2560]{0:T(1024)(128)(2,1)S(1)}, bf16[2560]{0:T(1024)(128)(2,1)}, u32[]{:S(2)}) copy-start(bf16[2560]{0:T(1024)(128)(2,1)} %param.21) | copy-start | bytes 15364
  128.3 11.2 %collective-permute-start.3 = (s32[1]{0:T(128)}, s32[1]{0:T(128)}, u32[]{:S(2)}, u32[]{:S(2)}) collective-permute-start(s32[1]{0:T(128)} %bitcast.14), channel_id=1, source_target_pairs={{0,1},{1,2},{2,3},{3,0},{4,5},{5,6},{6,7},{7,4},{8,9},{9,10},{10,1... | collective-permute-start | bytes 20 | tf_op jit(solution)/shard_map/ppermute | solution.py:42
  130.9 8.6 %collective-permute-start.4 = (s32[1]{0:T(128)}, s32[1]{0:T(128)}, u32[]{:S(2)}, u32[]{:S(2)}) collective-permute-start(s32[1]{0:T(128)} %bitcast.14), channel_id=1, source_target_pairs={{0,2},{1,3},{2,0},{3,1},{4,6},{5,7},{6,4},{7,5},{8,10},{9,11},{10,... | collective-permute-start | bytes 20 | tf_op jit(solution)/shard_map/ppermute | solution.py:42
  133.9 5.6 %collective-permute-start.5 = (s32[1]{0:T(128)}, s32[1]{0:T(128)}, u32[]{:S(2)}, u32[]{:S(2)}) collective-permute-start(s32[1]{0:T(128)} %bitcast.14), channel_id=1, source_target_pairs={{0,3},{1,0},{2,1},{3,2},{4,7},{5,4},{6,5},{7,6},{8,11},{9,8},{10,9... | collective-permute-start | bytes 20 | tf_op jit(solution)/shard_map/ppermute | solution.py:42
  145.9 8.7 %collective-permute-start.6 = (s32[1]{0:T(128)}, s32[1]{0:T(128)}, u32[]{:S(2)}, u32[]{:S(2)}) collective-permute-start(s32[1]{0:T(128)} %bitcast.20), channel_id=1, source_target_pairs={{0,4},{4,8},{8,12},{12,0},{1,5},{5,9},{9,13},{13,1},{2,6},{6,10},{... | collective-permute-start | bytes 20 | tf_op jit(solution)/shard_map/ppermute | solution.py:42
  148.8 5.8 %collective-permute-start.7 = (s32[1]{0:T(128)}, s32[1]{0:T(128)}, u32[]{:S(2)}, u32[]{:S(2)}) collective-permute-start(s32[1]{0:T(128)} %bitcast.20), channel_id=1, source_target_pairs={{0,8},{4,12},{8,0},{12,4},{1,9},{5,13},{9,1},{13,5},{2,10},{6,14},... | collective-permute-start | bytes 20 | tf_op jit(solution)/shard_map/ppermute | solution.py:42
  151.2 3.7 %collective-permute-start.8 = (s32[1]{0:T(128)}, s32[1]{0:T(128)}, u32[]{:S(2)}, u32[]{:S(2)}) collective-permute-start(s32[1]{0:T(128)} %bitcast.20), channel_id=1, source_target_pairs={{0,12},{4,0},{8,4},{12,8},{1,13},{5,1},{9,5},{13,9},{2,14},{6,2},{... | collective-permute-start | bytes 20 | tf_op jit(solution)/shard_map/ppermute | solution.py:42
  164.5 2.2 collective-permute-start.9
  200.3 11.3 %copy-start.6 = (bf16[8,128,2048]{1,2,0:T(8,128)(2,1)S(1)}, bf16[8,128,2048]{1,2,0:T(8,128)(2,1)}, u32[]{:S(2)}) copy-start(bf16[8,128,2048]{1,2,0:T(8,128)(2,1)} %all-gather.5.cloned.1.call-done) | copy-start | bytes 12582916
  211.6 9.3 %copy-start.5 = (s32[1,128]{1,0:T(1,128)S(1)}, s32[1,128]{1,0:T(1,128)}, u32[]{:S(2)}) copy-start(s32[1,128]{1,0:T(1,128)} %param.17) | copy-start | bytes 1540
  221.2 10.1 %collective-permute-start.10 = (f32[64]{0:T(128)S(1)}, f32[64]{0:T(128)S(1)}, u32[]{:S(2)}, u32[]{:S(2)}) collective-permute-start(f32[64]{0:T(128)S(1)} %pad_maximum_fusion.12), channel_id=1, source_target_pairs={{0,1},{1,2},{2,3},{3,0},{4,5},{5,6},{6,7},{7,4},{8,9},{9,10},{10,1... | collective-permute-start | bytes 776 | tf_op jit(solution)/shard_map/ppermute | solution.py:42
  225.7 7.5 %collective-permute-start.11 = (f32[64]{0:T(128)S(1)}, f32[64]{0:T(128)S(1)}, u32[]{:S(2)}, u32[]{:S(2)}) collective-permute-start(f32[64]{0:T(128)S(1)} %pad_maximum_fusion.12), channel_id=1, source_target_pairs={{0,2},{1,3},{2,0},{3,1},{4,6},{5,7},{6,4},{7,5},{8,10},{9,11},{10,... | collective-permute-start | bytes 776 | tf_op jit(solution)/shard_map/ppermute | solution.py:42
  228.2 5.0 %collective-permute-start.12 = (f32[64]{0:T(128)S(1)}, f32[64]{0:T(128)S(1)}, u32[]{:S(2)}, u32[]{:S(2)}) collective-permute-start(f32[64]{0:T(128)S(1)} %pad_maximum_fusion.12), channel_id=1, source_target_pairs={{0,3},{1,0},{2,1},{3,2},{4,7},{5,4},{6,5},{7,6},{8,11},{9,8},{10,9... | collective-permute-start | bytes 776 | tf_op jit(solution)/shard_map/ppermute | solution.py:42
  233.9 4.7 %collective-permute-start.13 = (f32[64]{0:T(128)S(1)}, f32[64]{0:T(128)S(1)}, u32[]{:S(2)}, u32[]{:S(2)}) collective-permute-start(f32[64]{0:T(128)S(1)} %fusion.46), channel_id=1, source_target_pairs={{0,4},{4,8},{8,12},{12,0},{1,5},{5,9},{9,13},{13,1},{2,6},{6,10},{... | collective-permute-start | bytes 776 | tf_op jit(solution)/shard_map/ppermute | solution.py:42
  235.4 5.1 %collective-permute-start.14 = (f32[64]{0:T(128)S(1)}, f32[64]{0:T(128)S(1)}, u32[]{:S(2)}, u32[]{:S(2)}) collective-permute-start(f32[64]{0:T(128)S(1)} %fusion.46), channel_id=1, source_target_pairs={{0,8},{4,12},{8,0},{12,4},{1,9},{5,13},{9,1},{13,5},{2,10},{6,14},... | collective-permute-start | bytes 776 | tf_op jit(solution)/shard_map/ppermute | solution.py:42
  236.5 3.9 %collective-permute-start.15 = (f32[64]{0:T(128)S(1)}, f32[64]{0:T(128)S(1)}, u32[]{:S(2)}, u32[]{:S(2)}) collective-permute-start(f32[64]{0:T(128)S(1)} %fusion.46), channel_id=1, source_target_pairs={{0,12},{4,0},{8,4},{12,8},{1,13},{5,1},{9,5},{13,9},{2,14},{6,2},{... | collective-permute-start | bytes 776 | tf_op jit(solution)/shard_map/ppermute | solution.py:42
Sparse Core Ops, SparseCore 0:
  13.7 104.8 all-gather.2
  126.6 73.7 all-gather.4
